TPU v7x, 256 devices: a whole 4x4x8 slice. The times are simulated.
256 devices in a mesh: ver: 16 (over y, x), row: 16 (over z, core).
Axes of the slice: x: 4, y: 4, z: 8, core: 2. Of those that a mesh axis runs over, the one named last changes fastest.
Arguments:
- embedding: bfloat16 [16, 32768, 512], P('ver', 'row'), may hold values from -48 to 48
- anchor_rows: int32 [16384], P('row'), may hold values from 0 to 32767, as said below
Outputs:
- aligned: bfloat16 [16, 32768, 512], P('ver', 'row')
Inputs may be any that keep to these rules, and one draw needn't show every extreme that they name: `anchor_rows`: the k-th block of 1024 entries names rows k * 2048 to (k + 1) * 2048 - 1; rows may repeat.
All inputs are finite; a program needn't handle non-finite values.
Results may differ from a plain program's by a relative error of at most 0.0019.
The roundings to bfloat16 on the way count: a program that leaves them out, or rounds other values in their place, can miss the bound.
Values may be sent and summed in bfloat16 or wider, within the bound.
No kernel may reach another device: no remote copies, remote signals or barrier semaphores. Data moves between devices by JAX's collectives and lax.ppermute only.
A program may use at most 64 MiB of HBM per device.

v0:
```python
import jax
import jax.numpy as jnp
from jax import lax
from jax.sharding import PartitionSpec as P

ITERS = 12
HIGHEST = lax.Precision.HIGHEST


def shifted(value, axis, steps):
    count = lax.axis_size(axis)
    return lax.ppermute(value, axis, [(source, source + steps) for source in range(count - steps)])


def swapped(value, axis, mask):
    count = lax.axis_size(axis)
    return lax.ppermute(value, axis, [(source, source ^ mask) for source in range(count)])


def summed_over(partial, axis):
    count = lax.axis_size(axis)
    pieces = partial.reshape(count, partial.shape[0] // count, partial.shape[1])
    reduced = lax.all_to_all(pieces, axis, 0, 0, tiled=False).sum(0)
    copies = jnp.broadcast_to(reduced[None], (count,) + reduced.shape)
    return lax.all_to_all(copies, axis, 0, 0, tiled=False).reshape(partial.shape)


def newton_update(sweep_index, iterate):
    square = jnp.dot(iterate.T, iterate, precision=HIGHEST)
    return 1.5 * iterate - 0.5 * jnp.dot(iterate, square, precision=HIGHEST)


def running_product(rotation, axis, core):
    count, mine = (lax.axis_size(axis), lax.axis_index(axis))
    half = rotation.shape[0] // 2
    product = rotation
    steps = 1
    while steps < count:
        sent = jnp.where(core == 0, product[:half], product[half:])
        received = shifted(sent, axis, steps)
        partner = swapped(received, "row", 1)
        earlier = jnp.where(
            core == 0,
            jnp.concatenate([received, partner]),
            jnp.concatenate([partner, received]),
        )
        longer = jnp.dot(product, earlier, precision=HIGHEST)
        product = jnp.where(mine >= steps, longer, product)
        steps *= 2
    return product


def per_device(embedding, anchor_rows):
    own_rows = embedding[0]
    width = own_rows.shape[1]
    positions = anchor_rows - lax.axis_index("row") * own_rows.shape[0]
    own_slab = jnp.take(own_rows, positions, axis=0)
    previous_slab = shifted(own_slab, "ver", 1)
    partial_gram = lax.dot_general(
        own_slab, previous_slab, (((0,), (0,)), ((), ())), preferred_element_type=jnp.float32
    )
    cross_gram = summed_over(partial_gram, "row")
    frobenius = jnp.sqrt(jnp.sum(cross_gram * cross_gram) + 1e-06)
    iterate = cross_gram / frobenius
    rotation = lax.fori_loop(0, ITERS, newton_update, iterate)
    identity_matrix = jnp.eye(width, dtype=jnp.float32)
    rotation = jnp.where(lax.axis_index("ver") == 0, identity_matrix, rotation)
    prefix = running_product(rotation, "ver", lax.axis_index("row") % 2)
    prefix_low = prefix.astype(jnp.bfloat16)
    aligned = jnp.dot(own_rows, prefix_low, preferred_element_type=jnp.float32).astype(jnp.bfloat16)
    return aligned[None]


def solution(mesh):
    return jax.shard_map(
        per_device,
        mesh=mesh,
        in_specs=(P("ver", "row", None), P("row")),
        out_specs=P("ver", "row", None),
        check_vma=False,
    )
```

profile of v0, /device:TPU:1, one launch (start us, length us, event | category | flops | bytes accessed | tf_op | source)
XLA Modules:
  0.0 257.8 jit_solution(1628214108658413994)
XLA Ops:
  1.6 4.0 %gather_fusion = bf16[1024,512]{1,0:T(8,128)(2,1)S(1)} fusion(bf16[2048,512]{1,0:T(8,128)(2,1)S(1)} %bitcast.34, s32[1024]{0:T(1024)S(1)} %fusion.28), kind=kCustom, calls=%fused_computation | custom fusion | bytes 2101248 | tf_op jit(solution)/shard_map/jit(_take)/gather | solution.py:57
  5.8 4.0 %collective-permute-start = (bf16[1024,512]{1,0:T(8,128)(2,1)S(1)}, bf16[1024,512]{1,0:T(8,128)(2,1)S(1)}, u32[]{:S(2)}, u32[]{:S(2)}) collective-permute-start(bf16[1024,512]{1,0:T(8,128)(2,1)S(1)} %broadcast_select_fusion), channel_id=1, source_target_pairs={{0,16},{16,32},{32,48},{48,64},{64,80},{80,96},{96,112},{112,128},... | collective-permute-start | bytes 3145736 | tf_op jit(solution)/shard_map/ppermute | solution.py:12
  9.8 21.8 %collective-permute-done = bf16[1024,512]{1,0:T(8,128)(2,1)S(1)} collective-permute-done((bf16[1024,512]{1,0:T(8,128)(2,1)S(1)}, bf16[1024,512]{1,0:T(8,128)(2,1)S(1)}, u32[]{:S(2)}, u32[]{:S(2)}) %collective-permute-start) | collective-permute-done | bytes 1048608 | tf_op jit(solution)/shard_map/ppermute | solution.py:12
  32.3 38.2 %all_to_all.10 = f32[16,32,512]{2,1,0:T(8,128)S(1)} all-to-all(f32[16,32,512]{2,1,0:T(8,128)S(1)} %bitcast.36), channel_id=1, replica_groups=mesh['ver'=16,'row'=16] {'row'}, dimensions={0} | all-to-all | bytes 2097152 | tf_op jit(solution)/shard_map/all_to_all | solution.py:23
  71.7 3.6 %all-to-all-start.1 = ((f32[16,32,512]{2,1,0:T(8,128)}), f32[16,32,512]{2,1,0:T(8,128)S(1)}, u32[]{:S(2)}, u32[]{:S(2)}) async-start(f32[16,32,512]{2,1,0:T(8,128)} %broadcast_in_dim.24), calls=%async_computation.1 | async-start | bytes 2097152 | tf_op jit(solution)/shard_map/all_to_all | solution.py:25
  75.3 27.3 %all-to-all-done.1 = f32[16,32,512]{2,1,0:T(8,128)S(1)} async-done(((f32[16,32,512]{2,1,0:T(8,128)}), f32[16,32,512]{2,1,0:T(8,128)S(1)}, u32[]{:S(2)}, u32[]{:S(2)}) %all-to-all-start.1) | async-done | bytes 1048608 | tf_op jit(solution)/shard_map/all_to_all | solution.py:25
  106.9 45.8 %while.10 = (s32[]{:T(128)}, f32[512,512]{0,1:T(8,128)S(1)}, s32[]{:T(128)}) while((s32[]{:T(128)}, f32[512,512]{0,1:T(8,128)S(1)}, s32[]{:T(128)}) %tuple.19), condition=%wide.region_3.4_spmd, body=%wide.region_2.3_spmd.sunk | while | flops 3222011904 | bytes 7340077 | solution.py:65
  110.8 1.9 fusion.57
  154.2 6.1 %collective-permute-start.1 = (f32[256,512]{1,0:T(8,128)S(1)}, f32[256,512]{1,0:T(8,128)}, u32[]{:S(2)}, u32[]{:S(2)}) collective-permute-start(f32[256,512]{1,0:T(8,128)S(1)} %slice_select_fusion.3), channel_id=1, source_target_pairs={{0,16},{16,32},{32,48},{48,64},{64,80},{80,96},{96,112},{112,128},... | collective-permute-start | bytes 1572872 | tf_op jit(solution)/shard_map/ppermute | solution.py:12
  160.4 10.1 %collective-permute-done.1 = f32[256,512]{1,0:T(8,128)} collective-permute-done((f32[256,512]{1,0:T(8,128)S(1)}, f32[256,512]{1,0:T(8,128)}, u32[]{:S(2)}, u32[]{:S(2)}) %collective-permute-start.1) | collective-permute-done | bytes 524320 | tf_op jit(solution)/shard_map/ppermute | solution.py:12
  170.4 2.2 collective-permute-done.2
  172.7 3.4 %convolution_select_fusion.3 = f32[512,512]{1,0:T(8,128)S(1)} fusion(f32[512,512]{1,0:T(8,128)S(1)} %convert_select_fusion, f32[256,512]{1,0:T(8,128)} %collective-permute-done.2, f32[256,512]{1,0:T(8,128)} %collective-permute-done.1, pred[]{:T(512)S(6)} %eq.10, pred[]{:T(512)S(6)} %ge.22), kind=kOutput, calls=%fused_computation.9 | convolution fusion | flops 1611661312 | bytes 3145730 | tf_op jit(solution)/shard_map/dot_general | solution.py:47
  177.2 5.5 %collective-permute-start.3 = (f32[256,512]{1,0:T(8,128)S(1)}, f32[256,512]{1,0:T(8,128)S(1)}, u32[]{:S(2)}, u32[]{:S(2)}) collective-permute-start(f32[256,512]{1,0:T(8,128)S(1)} %slice_select_fusion.2), channel_id=1, source_target_pairs={{0,32},{16,48},{32,64},{48,80},{64,96},{80,112},{96,128},{112,144}... | collective-permute-start | bytes 1572872 | tf_op jit(solution)/shard_map/ppermute | solution.py:12
  182.7 11.1 %collective-permute-done.3 = f32[256,512]{1,0:T(8,128)S(1)} collective-permute-done((f32[256,512]{1,0:T(8,128)S(1)}, f32[256,512]{1,0:T(8,128)S(1)}, u32[]{:S(2)}, u32[]{:S(2)}) %collective-permute-start.3) | collective-permute-done | bytes 524320 | tf_op jit(solution)/shard_map/ppermute | solution.py:12
  196.3 3.5 %convolution_select_fusion.2 = f32[512,512]{1,0:T(8,128)S(1)} fusion(f32[512,512]{1,0:T(8,128)} %copy-done.1, f32[256,512]{1,0:T(8,128)S(1)} %collective-permute-done.4, f32[256,512]{1,0:T(8,128)S(1)} %collective-permute-done.3, pred[]{:T(512)S(6)} %eq.10, pred[]{:T(512)S(6)} %ge.21), kind=kOutput, calls=%fused_computation.8 | convolution fusion | flops 1611661312 | bytes 3145730 | tf_op jit(solution)/shard_map/dot_general | solution.py:47
  200.8 9.3 %collective-permute-start.5 = (f32[256,512]{1,0:T(8,128)S(1)}, f32[256,512]{1,0:T(8,128)S(1)}, u32[]{:S(2)}, u32[]{:S(2)}) collective-permute-start(f32[256,512]{1,0:T(8,128)S(1)} %slice_select_fusion.1), channel_id=1, source_target_pairs={{0,64},{16,80},{32,96},{48,112},{64,128},{80,144},{96,160},{112,17... | collective-permute-start | bytes 1572872 | tf_op jit(solution)/shard_map/ppermute | solution.py:12
  210.2 10.9 %collective-permute-done.5 = f32[256,512]{1,0:T(8,128)S(1)} collective-permute-done((f32[256,512]{1,0:T(8,128)S(1)}, f32[256,512]{1,0:T(8,128)S(1)}, u32[]{:S(2)}, u32[]{:S(2)}) %collective-permute-start.5) | collective-permute-done | bytes 524320 | tf_op jit(solution)/shard_map/ppermute | solution.py:12
  223.9 4.1 %convolution_select_fusion.1 = f32[512,512]{1,0:T(8,128)S(1)} fusion(f32[512,512]{1,0:T(8,128)} %copy-done.2, f32[256,512]{1,0:T(8,128)} %collective-permute-done.6, f32[256,512]{1,0:T(8,128)} %copy-done.3, pred[]{:T(512)S(6)} %eq.10, pred[]{:T(512)S(6)} %ge.20), kind=kOutput, calls=%fused_computation.7 | convolution fusion | flops 1611661312 | bytes 3145730 | tf_op jit(solution)/shard_map/dot_general | solution.py:47
  228.1 6.5 %collective-permute-start.7 = (f32[256,512]{1,0:T(8,128)S(1)}, f32[256,512]{1,0:T(8,128)}, u32[]{:S(2)}, u32[]{:S(2)}) collective-permute-start(f32[256,512]{1,0:T(8,128)S(1)} %slice_select_fusion), channel_id=1, source_target_pairs={{0,128},{16,144},{32,160},{48,176},{64,192},{80,208},{96,224},{112... | collective-permute-start | bytes 1572872 | tf_op jit(solution)/shard_map/ppermute | solution.py:12
  234.6 10.1 %collective-permute-done.7 = f32[256,512]{1,0:T(8,128)} collective-permute-done((f32[256,512]{1,0:T(8,128)S(1)}, f32[256,512]{1,0:T(8,128)}, u32[]{:S(2)}, u32[]{:S(2)}) %collective-permute-start.7) | collective-permute-done | bytes 524320 | tf_op jit(solution)/shard_map/ppermute | solution.py:12
  245.9 1.9 collective-permute-done.8
  247.8 3.4 %fusion.3 = bf16[512,512]{1,0:T(8,128)(2,1)S(1)} fusion(f32[512,512]{1,0:T(8,128)S(1)} %convolution_select_fusion.1, f32[256,512]{1,0:T(8,128)} %collective-permute-done.8, f32[256,512]{1,0:T(8,128)} %collective-permute-done.7, pred[]{:T(512)S(6)} %eq.10, pred[]{:T(512)S(6)} %ge.19), kind=kOutput, calls=%fused_computation.10 | convolution fusion | flops 1611923456 | bytes 2621442 | tf_op jit(solution)/shard_map/dot_general | solution.py:47
  251.2 2.7 %fusion.2 = bf16[1,2048,512]{1,2,0:T(8,128)(2,1)} fusion(bf16[512,512]{1,0:T(8,128)(2,1)S(1)} %fusion.3, bf16[1,2048,512]{2,1,0:T(8,128)(2,1)S(1)} %copy-done), kind=kOutput, calls=%fused_computation.5 | convolution fusion | flops 1074790400 | bytes 4718592 | tf_op jit(solution)/shard_map/dot_general | solution.py:70
  253.9 3.9 %copy.7 = bf16[1,2048,512]{2,1,0:T(8,128)(2,1)} copy(bf16[1,2048,512]{1,2,0:T(8,128)(2,1)} %fusion.2) | data formatting | bytes 4194304 | tf_op jit(solution)/shard_map/broadcast_in_dim | solution.py:71
  (64 shorter events, 61.1 us)
Async XLA Ops:
  0.0 1.6 copy-start
  5.8 25.8 %collective-permute-start = (bf16[1024,512]{1,0:T(8,128)(2,1)S(1)}, bf16[1024,512]{1,0:T(8,128)(2,1)S(1)}, u32[]{:S(2)}, u32[]{:S(2)}) collective-permute-start(bf16[1024,512]{1,0:T(8,128)(2,1)S(1)} %broadcast_select_fusion), channel_id=1, source_target_pairs={{0,16},{16,32},{32,48},{48,64},{64,80},{80,96},{96,112},{112,128},... | collective-permute-start | bytes 3145736 | tf_op jit(solution)/shard_map/ppermute | solution.py:12
  71.7 30.9 %all-to-all-start.1 = ((f32[16,32,512]{2,1,0:T(8,128)}), f32[16,32,512]{2,1,0:T(8,128)S(1)}, u32[]{:S(2)}, u32[]{:S(2)}) async-start(f32[16,32,512]{2,1,0:T(8,128)} %broadcast_in_dim.24), calls=%async_computation.1 | async-start | bytes 2097152 | tf_op jit(solution)/shard_map/all_to_all | solution.py:25
  154.2 16.2 %collective-permute-start.1 = (f32[256,512]{1,0:T(8,128)S(1)}, f32[256,512]{1,0:T(8,128)}, u32[]{:S(2)}, u32[]{:S(2)}) collective-permute-start(f32[256,512]{1,0:T(8,128)S(1)} %slice_select_fusion.3), channel_id=1, source_target_pairs={{0,16},{16,32},{32,48},{48,64},{64,80},{80,96},{96,112},{112,128},... | collective-permute-start | bytes 1572872 | tf_op jit(solution)/shard_map/ppermute | solution.py:12
  170.4 2.3 collective-permute-start.2
  176.1 1.0 copy-start.1
  177.2 16.6 %collective-permute-start.3 = (f32[256,512]{1,0:T(8,128)S(1)}, f32[256,512]{1,0:T(8,128)S(1)}, u32[]{:S(2)}, u32[]{:S(2)}) collective-permute-start(f32[256,512]{1,0:T(8,128)S(1)} %slice_select_fusion.2), channel_id=1, source_target_pairs={{0,32},{16,48},{32,64},{48,80},{64,96},{80,112},{96,128},{112,144}... | collective-permute-start | bytes 1572872 | tf_op jit(solution)/shard_map/ppermute | solution.py:12
  193.8 2.5 collective-permute-start.4
  199.8 1.0 copy-start.2
  200.8 20.2 %collective-permute-start.5 = (f32[256,512]{1,0:T(8,128)S(1)}, f32[256,512]{1,0:T(8,128)S(1)}, u32[]{:S(2)}, u32[]{:S(2)}) collective-permute-start(f32[256,512]{1,0:T(8,128)S(1)} %slice_select_fusion.1), channel_id=1, source_target_pairs={{0,64},{16,80},{32,96},{48,112},{64,128},{80,144},{96,160},{112,17... | collective-permute-start | bytes 1572872 | tf_op jit(solution)/shard_map/ppermute | solution.py:12
  221.0 1.2 copy-start.3
  221.0 2.9 %collective-permute-start.6 = (f32[256,512]{1,0:T(8,128)S(1)}, f32[256,512]{1,0:T(8,128)}, u32[]{:S(2)}, u32[]{:S(2)}) collective-permute-start(f32[256,512]{1,0:T(8,128)S(1)} %collective-permute-done.5), channel_id=1, source_target_pairs={{0,1},{1,0},{2,3},{3,2},{4,5},{5,4},{6,7},{7,6},{8,9},{9,8},{10,11... | collective-permute-start | bytes 1572872 | tf_op jit(solution)/shard_map/ppermute | solution.py:17
  228.1 16.6 %collective-permute-start.7 = (f32[256,512]{1,0:T(8,128)S(1)}, f32[256,512]{1,0:T(8,128)}, u32[]{:S(2)}, u32[]{:S(2)}) collective-permute-start(f32[256,512]{1,0:T(8,128)S(1)} %slice_select_fusion), channel_id=1, source_target_pairs={{0,128},{16,144},{32,160},{48,176},{64,192},{80,208},{96,224},{112... | collective-permute-start | bytes 1572872 | tf_op jit(solution)/shard_map/ppermute | solution.py:12
  244.7 3.1 %collective-permute-start.8 = (f32[256,512]{1,0:T(8,128)}, f32[256,512]{1,0:T(8,128)}, u32[]{:S(2)}, u32[]{:S(2)}) collective-permute-start(f32[256,512]{1,0:T(8,128)} %collective-permute-done.7), channel_id=1, source_target_pairs={{0,1},{1,0},{2,3},{3,2},{4,5},{5,4},{6,7},{7,6},{8,9},{9,8},{10,11... | collective-permute-start | bytes 1572872 | tf_op jit(solution)/shard_map/ppermute | solution.py:17
where the time goes:
time: 258 us
  waiting for transfers between devices  98.5 us (38%)
  matrix products  62.3 us (24%)
  starting transfers between devices  38.5 us (15%)
  blocking collectives  38.2 us (15%)
  local copies, waits for them, and re-layouts  14.7 us (6%)
  other arithmetic  4.25 us (2%)
    ppermute x5, waiting for transfers between devices, shifted(): lax.ppermute(value, axis, [(source, source + steps) for source in range(c...  63.9 us
    all_to_all x1, blocking collectives, summed_over(): reduced = lax.all_to_all(pieces, axis, 0, 0, tiled=False).sum(0)  38.2 us
    ppermute x5, starting transfers between devices, shifted(): lax.ppermute(value, axis, [(source, source + steps) for source in range(c...  31.5 us
    all_to_all x1, waiting for transfers between devices, summed_over(): lax.all_to_all(copies, axis, 0, 0, tiled=False).reshape(partial.shape)  27.3 us
    dot_general x12, matrix products, newton_update(): square = jnp.dot(iterate.T, iterate, precision=HIGHEST)  22.3 us
    dot_general x12, matrix products, newton_update(): return 1.5 * iterate - 0.5 * jnp.dot(iterate, square, precision=HIGHEST)  22.2 us
    dot_general x4, matrix products, running_product(): longer = jnp.dot(product, earlier, precision=HIGHEST)  14.4 us
    ppermute x4, waiting for transfers between devices, swapped(): lax.ppermute(value, axis, [(source, source ^ mask) for source in range(co...  7.33 us
  transfers between devices with their start and end apart: 10, of which 10 were waited for; matrix products, arithmetic and copies ran while one was open for 0% of the time, Pallas kernels for 0%

commit v1 on v0

v1 whole, which is shorter than its diff:
```python
import jax
import jax.numpy as jnp
from jax import lax
from jax.sharding import Mesh, PartitionSpec as P

ITERS = 12
HIGHEST = lax.Precision.HIGHEST


def shifted(value, axis, steps):
    count = lax.axis_size(axis)
    return lax.ppermute(value, axis, [(source, source + steps) for source in range(count - steps)])


def swapped(value, axis, mask):
    count = lax.axis_size(axis)
    return lax.ppermute(value, axis, [(source, source ^ mask) for source in range(count)])


def halves(matrix, core):
    half = matrix.shape[0] // 2
    return jnp.where(core == 0, matrix[:half], matrix[half:]), jnp.where(core == 0, matrix[half:], matrix[:half])


def joined(mine, other, core):
    return jnp.where(core == 0, jnp.concatenate([mine, other]), jnp.concatenate([other, mine]))


def summed_over(partial, axis, core):
    mine, other = halves(partial, core)
    mine = mine + swapped(other, "core", 1)
    count = lax.axis_size(axis)
    pieces = mine.reshape(count, mine.shape[0] // count, mine.shape[1])
    reduced = lax.all_to_all(pieces, axis, 0, 0, tiled=False).sum(0)
    copies = jnp.broadcast_to(reduced[None], (count,) + reduced.shape)
    mine = lax.all_to_all(copies, axis, 0, 0, tiled=False).reshape(mine.shape)
    return joined(mine, swapped(mine, "core", 1), core)


def newton_update(sweep_index, iterate):
    square = jnp.dot(iterate.T, iterate, precision=HIGHEST)
    return 1.5 * iterate - 0.5 * jnp.dot(iterate, square, precision=HIGHEST)


def running_product(rotation, axis, core):
    count, mine = (lax.axis_size(axis), lax.axis_index(axis))
    product = rotation
    steps = 1
    while steps < count:
        received = shifted(halves(product, core)[0], axis, steps)
        earlier = joined(received, swapped(received, "core", 1), core)
        longer = jnp.dot(product, earlier, precision=HIGHEST)
        product = jnp.where(mine >= steps, longer, product)
        steps *= 2
    return product


def per_device(embedding, anchor_rows):
    own_rows = embedding[0]
    width = own_rows.shape[1]
    core = lax.axis_index("core")
    row_index = lax.axis_index("z") * lax.axis_size("core") + core
    positions = anchor_rows - row_index * own_rows.shape[0]
    own_slab = jnp.take(own_rows, positions, axis=0)
    previous_slab = shifted(own_slab, "ver", 1)
    partial_gram = lax.dot_general(
        own_slab, previous_slab, (((0,), (0,)), ((), ())), preferred_element_type=jnp.float32
    )
    cross_gram = summed_over(partial_gram, "z", core)
    frobenius = jnp.sqrt(jnp.sum(cross_gram * cross_gram) + 1e-06)
    iterate = cross_gram / frobenius
    rotation = lax.fori_loop(0, ITERS, newton_update, iterate)
    identity_matrix = jnp.eye(width, dtype=jnp.float32)
    rotation = jnp.where(lax.axis_index("ver") == 0, identity_matrix, rotation)
    prefix = running_product(rotation, "ver", core)
    prefix_low = prefix.astype(jnp.bfloat16)
    aligned = jnp.dot(own_rows, prefix_low, preferred_element_type=jnp.float32).astype(jnp.bfloat16)
    return aligned[None]


def solution(mesh):
    versions, rows = mesh.devices.shape
    cores = 2
    split_mesh = Mesh(mesh.devices.reshape(versions, rows // cores, cores), ("ver", "z", "core"))
    row = ("z", "core")
    return jax.shard_map(
        per_device,
        mesh=split_mesh,
        in_specs=(P("ver", row, None), P(row)),
        out_specs=P("ver", row, None),
        check_vma=False,
    )
```

time: 258 us -> 242 us (0.938)
  waiting for transfers between devices: 98.5 us -> 74 us
  blocking collectives: 38.2 us -> 42.2 us
  starting transfers between devices: 38.5 us -> 41.5 us
    all_to_all x1 -> x0, waiting for transfers between devices: 27.3 us -> none  [summed_over(): lax.all_to_all(copies, axis, 0, 0, tiled=False).reshape(partial.shape)]
    all_to_all x0 -> x1, blocking collectives: none -> 17.5 us  [summed_over(): mine = lax.all_to_all(copies, axis, 0, 0, tiled=False).reshape(mine.shape)]
    all_to_all x1, blocking collectives: 38.2 us -> 24.7 us  [summed_over(): reduced = lax.all_to_all(pieces, axis, 0, 0, tiled=False).sum(0)]
    ppermute x4 -> x6, starting transfers between devices: 3.46 us -> 9.86 us  [swapped(): lax.ppermute(value, axis, [(source, source ^ mask) for source in range(co...]
    all_to_all x1 -> x0, starting transfers between devices: 3.55 us -> none  [summed_over(): lax.all_to_all(copies, axis, 0, 0, tiled=False).reshape(partial.shape)]
    ppermute x4 -> x6, waiting for transfers between devices: 7.33 us -> 10 us  [swapped(): lax.ppermute(value, axis, [(source, source ^ mask) for source in range(co...]
  transfers between devices with their start and end apart: 10 -> 11, of which waited for: 10 -> 11; matrix products, arithmetic and copies ran while one was open for 0% -> 0% of each run, Pallas kernels for 0% -> 0%
where the time goes in v1:
time: 242 us
  waiting for transfers between devices  74 us (31%)
  matrix products  63.5 us (26%)
  blocking collectives  42.2 us (17%)
  starting transfers between devices  41.5 us (17%)
  local copies, waits for them, and re-layouts  13.6 us (6%)
  other arithmetic  5.45 us (2%)
    ppermute x5, waiting for transfers between devices, shifted(): lax.ppermute(value, axis, [(source, source + steps) for source in range(c...  64 us
    ppermute x5, starting transfers between devices, shifted(): lax.ppermute(value, axis, [(source, source + steps) for source in range(c...  31.6 us
    all_to_all x1, blocking collectives, summed_over(): reduced = lax.all_to_all(pieces, axis, 0, 0, tiled=False).sum(0)  24.7 us
    dot_general x12, matrix products, newton_update(): square = jnp.dot(iterate.T, iterate, precision=HIGHEST)  22.3 us
    dot_general x12, matrix products, newton_update(): return 1.5 * iterate - 0.5 * jnp.dot(iterate, square, precision=HIGHEST)  22.2 us
    all_to_all x1, blocking collectives, summed_over(): mine = lax.all_to_all(copies, axis, 0, 0, tiled=False).reshape(mine.shape)  17.5 us
    dot_general x4, matrix products, running_product(): longer = jnp.dot(product, earlier, precision=HIGHEST)  14.4 us
    ppermute x6, waiting for transfers between devices, swapped(): lax.ppermute(value, axis, [(source, source ^ mask) for source in range(co...  10 us
  transfers between devices with their start and end apart: 11, of which 11 were waited for; matrix products, arithmetic and copies ran while one was open for 0% of the time, Pallas kernels for 0%

profile of v1, /device:TPU:1, one launch (start us, length us, event | category | flops | bytes accessed | tf_op | source)
XLA Modules:
  0.0 241.6 jit_solution(3104929957596011432)
XLA Ops:
  1.6 4.0 %gather_fusion = bf16[1024,512]{1,0:T(8,128)(2,1)S(1)} fusion(bf16[2048,512]{1,0:T(8,128)(2,1)S(1)} %bitcast.34, s32[1024]{0:T(1024)S(1)} %fusion.29), kind=kCustom, calls=%fused_computation | custom fusion | bytes 2101248 | tf_op jit(solution)/shard_map/jit(_take)/gather | solution.py:64
  6.8 4.0 %collective-permute-start = (bf16[1024,512]{1,0:T(8,128)(2,1)}, bf16[1024,512]{1,0:T(8,128)(2,1)S(1)}, u32[]{:S(2)}, u32[]{:S(2)}) collective-permute-start(bf16[1024,512]{1,0:T(8,128)(2,1)} %broadcast_select_fusion), channel_id=1, source_target_pairs={{0,16},{16,32},{32,48},{48,64},{64,80},{80,96},{96,112},{112,128},... | collective-permute-start | bytes 3145736 | tf_op jit(solution)/shard_map/ppermute | solution.py:12
  10.8 22.1 %collective-permute-done = bf16[1024,512]{1,0:T(8,128)(2,1)S(1)} collective-permute-done((bf16[1024,512]{1,0:T(8,128)(2,1)}, bf16[1024,512]{1,0:T(8,128)(2,1)S(1)}, u32[]{:S(2)}, u32[]{:S(2)}) %collective-permute-start) | collective-permute-done | bytes 1048608 | tf_op jit(solution)/shard_map/ppermute | solution.py:12
  32.8 2.0 fusion.36
  38.2 24.7 %all_to_all.10 = f32[8,32,512]{2,1,0:T(8,128)S(1)} all-to-all(f32[8,32,512]{2,1,0:T(8,128)S(1)} %bitcast.38), channel_id=1, replica_groups=mesh['ver'=16,'z'=8,'core'=2] {'z'}, dimensions={0} | all-to-all | bytes 1048576 | tf_op jit(solution)/shard_map/all_to_all | solution.py:34
  63.0 17.5 %all_to_all.11 = f32[8,32,512]{2,1,0:T(8,128)S(1)} all-to-all(f32[8,32,512]{2,1,0:T(8,128)S(1)} %broadcast_in_dim.24), channel_id=1, replica_groups=mesh['ver'=16,'z'=8,'core'=2] {'z'}, dimensions={0} | all-to-all | bytes 1048576 | tf_op jit(solution)/shard_map/all_to_all | solution.py:36
  80.5 3.3 %collective-permute-start.2 = (f32[256,512]{1,0:T(8,128)S(1)}, f32[256,512]{1,0:T(8,128)S(1)}, u32[]{:S(2)}, u32[]{:S(2)}) collective-permute-start(f32[256,512]{1,0:T(8,128)S(1)} %bitcast.35), channel_id=1, source_target_pairs={{0,1},{1,0},{2,3},{3,2},{4,5},{5,4},{6,7},{7,6},{8,9},{9,8},{10,11... | collective-permute-start | bytes 1572872 | tf_op jit(solution)/shard_map/ppermute | solution.py:17
  89.7 45.8 %while.10 = (s32[]{:T(128)}, f32[512,512]{0,1:T(8,128)S(1)}, s32[]{:T(128)}) while((s32[]{:T(128)}, f32[512,512]{0,1:T(8,128)S(1)}, s32[]{:T(128)}) %tuple.19), condition=%wide.region_3.4_spmd, body=%wide.region_2.3_spmd.sunk | while | flops 3222011904 | bytes 7340077 | solution.py:72
  137.0 6.0 %collective-permute-start.3 = (f32[256,512]{1,0:T(8,128)S(1)}, f32[256,512]{1,0:T(8,128)}, u32[]{:S(2)}, u32[]{:S(2)}) collective-permute-start(f32[256,512]{1,0:T(8,128)S(1)} %slice_select_fusion.3), channel_id=1, source_target_pairs={{0,16},{16,32},{32,48},{48,64},{64,80},{80,96},{96,112},{112,128},... | collective-permute-start | bytes 1572872 | tf_op jit(solution)/shard_map/ppermute | solution.py:12
  143.0 10.1 %collective-permute-done.3 = f32[256,512]{1,0:T(8,128)} collective-permute-done((f32[256,512]{1,0:T(8,128)S(1)}, f32[256,512]{1,0:T(8,128)}, u32[]{:S(2)}, u32[]{:S(2)}) %collective-permute-start.3) | collective-permute-done | bytes 524320 | tf_op jit(solution)/shard_map/ppermute | solution.py:12
  154.4 1.9 collective-permute-done.4
  156.3 3.4 %convolution_select_fusion.3 = f32[512,512]{1,0:T(8,128)S(1)} fusion(f32[512,512]{1,0:T(8,128)S(1)} %convert_select_fusion, f32[256,512]{1,0:T(8,128)} %collective-permute-done.4, f32[256,512]{1,0:T(8,128)} %collective-permute-done.3, pred[]{:T(512)S(6)} %eq.8, pred[]{:T(512)S(6)} %ge.22), kind=kOutput, calls=%fused_computation.9 | convolution fusion | flops 1611661312 | bytes 3145730 | tf_op jit(solution)/shard_map/dot_general | solution.py:52
  160.7 5.8 %collective-permute-start.5 = (f32[256,512]{1,0:T(8,128)S(1)}, f32[256,512]{1,0:T(8,128)S(1)}, u32[]{:S(2)}, u32[]{:S(2)}) collective-permute-start(f32[256,512]{1,0:T(8,128)S(1)} %slice_select_fusion.2), channel_id=1, source_target_pairs={{0,32},{16,48},{32,64},{48,80},{64,96},{80,112},{96,128},{112,144}... | collective-permute-start | bytes 1572872 | tf_op jit(solution)/shard_map/ppermute | solution.py:12
  166.5 10.9 %collective-permute-done.5 = f32[256,512]{1,0:T(8,128)S(1)} collective-permute-done((f32[256,512]{1,0:T(8,128)S(1)}, f32[256,512]{1,0:T(8,128)S(1)}, u32[]{:S(2)}, u32[]{:S(2)}) %collective-permute-start.5) | collective-permute-done | bytes 524320 | tf_op jit(solution)/shard_map/ppermute | solution.py:12
  180.1 3.5 %convolution_select_fusion.2 = f32[512,512]{1,0:T(8,128)S(1)} fusion(f32[512,512]{1,0:T(8,128)} %copy-done.1, f32[256,512]{1,0:T(8,128)S(1)} %collective-permute-done.6, f32[256,512]{1,0:T(8,128)S(1)} %collective-permute-done.5, pred[]{:T(512)S(6)} %eq.8, pred[]{:T(512)S(6)} %ge.21), kind=kOutput, calls=%fused_computation.8 | convolution fusion | flops 1611661312 | bytes 3145730 | tf_op jit(solution)/shard_map/dot_general | solution.py:52
  184.7 9.3 %collective-permute-start.7 = (f32[256,512]{1,0:T(8,128)S(1)}, f32[256,512]{1,0:T(8,128)S(1)}, u32[]{:S(2)}, u32[]{:S(2)}) collective-permute-start(f32[256,512]{1,0:T(8,128)S(1)} %slice_select_fusion.1), channel_id=1, source_target_pairs={{0,64},{16,80},{32,96},{48,112},{64,128},{80,144},{96,160},{112,17... | collective-permute-start | bytes 1572872 | tf_op jit(solution)/shard_map/ppermute | solution.py:12
  194.0 10.9 %collective-permute-done.7 = f32[256,512]{1,0:T(8,128)S(1)} collective-permute-done((f32[256,512]{1,0:T(8,128)S(1)}, f32[256,512]{1,0:T(8,128)S(1)}, u32[]{:S(2)}, u32[]{:S(2)}) %collective-permute-start.7) | collective-permute-done | bytes 524320 | tf_op jit(solution)/shard_map/ppermute | solution.py:12
  207.8 4.1 %convolution_select_fusion.1 = f32[512,512]{1,0:T(8,128)S(1)} fusion(f32[512,512]{1,0:T(8,128)} %copy-done.2, f32[256,512]{1,0:T(8,128)} %collective-permute-done.8, f32[256,512]{1,0:T(8,128)} %copy-done.3, pred[]{:T(512)S(6)} %eq.8, pred[]{:T(512)S(6)} %ge.20), kind=kOutput, calls=%fused_computation.7 | convolution fusion | flops 1611661312 | bytes 3145730 | tf_op jit(solution)/shard_map/dot_general | solution.py:52
  211.9 6.5 %collective-permute-start.9 = (f32[256,512]{1,0:T(8,128)S(1)}, f32[256,512]{1,0:T(8,128)}, u32[]{:S(2)}, u32[]{:S(2)}) collective-permute-start(f32[256,512]{1,0:T(8,128)S(1)} %slice_select_fusion), channel_id=1, source_target_pairs={{0,128},{16,144},{32,160},{48,176},{64,192},{80,208},{96,224},{112... | collective-permute-start | bytes 1572872 | tf_op jit(solution)/shard_map/ppermute | solution.py:12
  218.5 10.1 %collective-permute-done.9 = f32[256,512]{1,0:T(8,128)} collective-permute-done((f32[256,512]{1,0:T(8,128)S(1)}, f32[256,512]{1,0:T(8,128)}, u32[]{:S(2)}, u32[]{:S(2)}) %collective-permute-start.9) | collective-permute-done | bytes 524320 | tf_op jit(solution)/shard_map/ppermute | solution.py:12
  229.8 1.9 collective-permute-done.10
  231.7 3.4 %fusion.3 = bf16[512,512]{1,0:T(8,128)(2,1)S(1)} fusion(f32[512,512]{1,0:T(8,128)S(1)} %convolution_select_fusion.1, f32[256,512]{1,0:T(8,128)} %collective-permute-done.10, f32[256,512]{1,0:T(8,128)} %collective-permute-done.9, pred[]{:T(512)S(6)} %eq.8, pred[]{:T(512)S(6)} %ge.19), kind=kOutput, calls=%fused_computation.10 | convolution fusion | flops 1611923456 | bytes 2621442 | tf_op jit(solution)/shard_map/dot_general | solution.py:52
  235.1 2.7 %fusion.2 = bf16[1,2048,512]{1,2,0:T(8,128)(2,1)} fusion(bf16[512,512]{1,0:T(8,128)(2,1)S(1)} %fusion.3, bf16[1,2048,512]{2,1,0:T(8,128)(2,1)S(1)} %copy-done), kind=kOutput, calls=%fused_computation.5 | convolution fusion | flops 1074790400 | bytes 4718592 | tf_op jit(solution)/shard_map/dot_general | solution.py:77
  237.7 3.9 %copy.5 = bf16[1,2048,512]{2,1,0:T(8,128)(2,1)} copy(bf16[1,2048,512]{1,2,0:T(8,128)(2,1)} %fusion.2) | data formatting | bytes 4194304 | tf_op jit(solution)/shard_map/broadcast_in_dim | solution.py:78
  (69 shorter events, 68.5 us)
Async XLA Ops:
  0.0 1.6 copy-start
  6.8 26.1 %collective-permute-start = (bf16[1024,512]{1,0:T(8,128)(2,1)}, bf16[1024,512]{1,0:T(8,128)(2,1)S(1)}, u32[]{:S(2)}, u32[]{:S(2)}) collective-permute-start(bf16[1024,512]{1,0:T(8,128)(2,1)} %broadcast_select_fusion), channel_id=1, source_target_pairs={{0,16},{16,32},{32,48},{48,64},{64,80},{80,96},{96,112},{112,128},... | collective-permute-start | bytes 3145736 | tf_op jit(solution)/shard_map/ppermute | solution.py:12
  34.9 3.1 %collective-permute-start.1 = (f32[256,512]{1,0:T(8,128)S(1)}, f32[256,512]{1,0:T(8,128)S(1)}, u32[]{:S(2)}, u32[]{:S(2)}) collective-permute-start(f32[256,512]{1,0:T(8,128)S(1)} %slice_select_fusion.4), channel_id=1, source_target_pairs={{0,1},{1,0},{2,3},{3,2},{4,5},{5,4},{6,7},{7,6},{8,9},{9,8},{10,11... | collective-permute-start | bytes 1572872 | tf_op jit(solution)/shard_map/ppermute | solution.py:17
  80.5 4.9 %collective-permute-start.2 = (f32[256,512]{1,0:T(8,128)S(1)}, f32[256,512]{1,0:T(8,128)S(1)}, u32[]{:S(2)}, u32[]{:S(2)}) collective-permute-start(f32[256,512]{1,0:T(8,128)S(1)} %bitcast.35), channel_id=1, source_target_pairs={{0,1},{1,0},{2,3},{3,2},{4,5},{5,4},{6,7},{7,6},{8,9},{9,8},{10,11... | collective-permute-start | bytes 1572872 | tf_op jit(solution)/shard_map/ppermute | solution.py:17
  137.0 16.1 %collective-permute-start.3 = (f32[256,512]{1,0:T(8,128)S(1)}, f32[256,512]{1,0:T(8,128)}, u32[]{:S(2)}, u32[]{:S(2)}) collective-permute-start(f32[256,512]{1,0:T(8,128)S(1)} %slice_select_fusion.3), channel_id=1, source_target_pairs={{0,16},{16,32},{32,48},{48,64},{64,80},{80,96},{96,112},{112,128},... | collective-permute-start | bytes 1572872 | tf_op jit(solution)/shard_map/ppermute | solution.py:12
  153.1 3.1 %collective-permute-start.4 = (f32[256,512]{1,0:T(8,128)}, f32[256,512]{1,0:T(8,128)}, u32[]{:S(2)}, u32[]{:S(2)}) collective-permute-start(f32[256,512]{1,0:T(8,128)} %collective-permute-done.3), channel_id=1, source_target_pairs={{0,1},{1,0},{2,3},{3,2},{4,5},{5,4},{6,7},{7,6},{8,9},{9,8},{10,11... | collective-permute-start | bytes 1572872 | tf_op jit(solution)/shard_map/ppermute | solution.py:17
  159.7 1.0 copy-start.1
  160.7 16.6 %collective-permute-start.5 = (f32[256,512]{1,0:T(8,128)S(1)}, f32[256,512]{1,0:T(8,128)S(1)}, u32[]{:S(2)}, u32[]{:S(2)}) collective-permute-start(f32[256,512]{1,0:T(8,128)S(1)} %slice_select_fusion.2), channel_id=1, source_target_pairs={{0,32},{16,48},{32,64},{48,80},{64,96},{80,112},{96,128},{112,144}... | collective-permute-start | bytes 1572872 | tf_op jit(solution)/shard_map/ppermute | solution.py:12
  177.4 2.8 %collective-permute-start.6 = (f32[256,512]{1,0:T(8,128)S(1)}, f32[256,512]{1,0:T(8,128)S(1)}, u32[]{:S(2)}, u32[]{:S(2)}) collective-permute-start(f32[256,512]{1,0:T(8,128)S(1)} %collective-permute-done.5), channel_id=1, source_target_pairs={{0,1},{1,0},{2,3},{3,2},{4,5},{5,4},{6,7},{7,6},{8,9},{9,8},{10,11... | collective-permute-start | bytes 1572872 | tf_op jit(solution)/shard_map/ppermute | solution.py:17
  183.6 1.0 copy-start.2
  184.7 20.2 %collective-permute-start.7 = (f32[256,512]{1,0:T(8,128)S(1)}, f32[256,512]{1,0:T(8,128)S(1)}, u32[]{:S(2)}, u32[]{:S(2)}) collective-permute-start(f32[256,512]{1,0:T(8,128)S(1)} %slice_select_fusion.1), channel_id=1, source_target_pairs={{0,64},{16,80},{32,96},{48,112},{64,128},{80,144},{96,160},{112,17... | collective-permute-start | bytes 1572872 | tf_op jit(solution)/shard_map/ppermute | solution.py:12
  204.9 1.2 copy-start.3
  204.9 2.9 %collective-permute-start.8 = (f32[256,512]{1,0:T(8,128)S(1)}, f32[256,512]{1,0:T(8,128)}, u32[]{:S(2)}, u32[]{:S(2)}) collective-permute-start(f32[256,512]{1,0:T(8,128)S(1)} %collective-permute-done.7), channel_id=1, source_target_pairs={{0,1},{1,0},{2,3},{3,2},{4,5},{5,4},{6,7},{7,6},{8,9},{9,8},{10,11... | collective-permute-start | bytes 1572872 | tf_op jit(solution)/shard_map/ppermute | solution.py:17
  211.9 16.6 %collective-permute-start.9 = (f32[256,512]{1,0:T(8,128)S(1)}, f32[256,512]{1,0:T(8,128)}, u32[]{:S(2)}, u32[]{:S(2)}) collective-permute-start(f32[256,512]{1,0:T(8,128)S(1)} %slice_select_fusion), channel_id=1, source_target_pairs={{0,128},{16,144},{32,160},{48,176},{64,192},{80,208},{96,224},{112... | collective-permute-start | bytes 1572872 | tf_op jit(solution)/shard_map/ppermute | solution.py:12
  228.6 3.1 %collective-permute-start.10 = (f32[256,512]{1,0:T(8,128)}, f32[256,512]{1,0:T(8,128)}, u32[]{:S(2)}, u32[]{:S(2)}) collective-permute-start(f32[256,512]{1,0:T(8,128)} %collective-permute-done.9), channel_id=1, source_target_pairs={{0,1},{1,0},{2,3},{3,2},{4,5},{5,4},{6,7},{7,6},{8,9},{9,8},{10,11... | collective-permute-start | bytes 1572872 | tf_op jit(solution)/shard_map/ppermute | solution.py:17

commit v2 on v1

--- a/solution.py
+++ b/solution.py
@@ -4,6 +4,7 @@
 from jax.sharding import Mesh, PartitionSpec as P
 
 ITERS = 12
+ROUGH_ITERS = 8
 HIGHEST = lax.Precision.HIGHEST
 
 
@@ -37,9 +38,12 @@
     return joined(mine, swapped(mine, "core", 1), core)
 
 
-def newton_update(sweep_index, iterate):
-    square = jnp.dot(iterate.T, iterate, precision=HIGHEST)
-    return 1.5 * iterate - 0.5 * jnp.dot(iterate, square, precision=HIGHEST)
+def newton_update(precision):
+    def update(sweep_index, iterate):
+        square = jnp.dot(iterate.T, iterate, precision=precision)
+        return 1.5 * iterate - 0.5 * jnp.dot(iterate, square, precision=precision)
+
+    return update
 
 
 def running_product(rotation, axis, core):
@@ -69,7 +73,8 @@
     cross_gram = summed_over(partial_gram, "z", core)
     frobenius = jnp.sqrt(jnp.sum(cross_gram * cross_gram) + 1e-06)
     iterate = cross_gram / frobenius
-    rotation = lax.fori_loop(0, ITERS, newton_update, iterate)
+    iterate = lax.fori_loop(0, ROUGH_ITERS, newton_update(lax.Precision.HIGH), iterate)
+    rotation = lax.fori_loop(ROUGH_ITERS, ITERS, newton_update(HIGHEST), iterate)
     identity_matrix = jnp.eye(width, dtype=jnp.float32)
     rotation = jnp.where(lax.axis_index("ver") == 0, identity_matrix, rotation)
     prefix = running_product(rotation, "ver", core)

time: 242 us -> 229 us (0.946)
  matrix products: 63.5 us -> 50.3 us
    dot_general x24, matrix products: 44.5 us -> 31.3 us  [the longest x12 15.6 us: update(): square = jnp.dot(iterate.T, iterate, precision=precision)]
where the time goes in v2:
time: 229 us; the launch traced here: 228 us
  waiting for transfers between devices  74 us (32%)
  matrix products  50.3 us (22%)
  blocking collectives  42.2 us (18%)
  starting transfers between devices  41.5 us (18%)
  local copies, waits for them, and re-layouts  13.6 us (6%)
  other arithmetic  5.45 us (2%)
    ppermute x5, waiting for transfers between devices, shifted(): lax.ppermute(value, axis, [(source, source + steps) for source in range(c...  64 us
    ppermute x5, starting transfers between devices, shifted(): lax.ppermute(value, axis, [(source, source + steps) for source in range(c...  31.6 us
    all_to_all x1, blocking collectives, summed_over(): reduced = lax.all_to_all(pieces, axis, 0, 0, tiled=False).sum(0)  24.7 us
    all_to_all x1, blocking collectives, summed_over(): mine = lax.all_to_all(copies, axis, 0, 0, tiled=False).reshape(mine.shape)  17.5 us
    dot_general x12, matrix products, update(): square = jnp.dot(iterate.T, iterate, precision=precision)  15.6 us
    dot_general x12, matrix products, update(): return 1.5 * iterate - 0.5 * jnp.dot(iterate, square, precision=precision)  15.6 us
    dot_general x4, matrix products, running_product(): longer = jnp.dot(product, earlier, precision=HIGHEST)  14.4 us
    ppermute x6, waiting for transfers between devices, swapped(): lax.ppermute(value, axis, [(source, source ^ mask) for source in range(co...  10 us
  transfers between devices with their start and end apart: 11, of which 11 were waited for; matrix products, arithmetic and copies ran while one was open for 0% of the time, Pallas kernels for 0%

profile of v2, /device:TPU:1, one launch (start us, length us, event | category | flops | bytes accessed | tf_op | source)
XLA Modules:
  0.0 228.4 jit_solution(7297440688202858643)
XLA Ops:
  1.6 4.0 %gather_fusion = bf16[1024,512]{1,0:T(8,128)(2,1)S(1)} fusion(bf16[2048,512]{1,0:T(8,128)(2,1)S(1)} %bitcast.52, s32[1024]{0:T(1024)S(1)} %fusion.31), kind=kCustom, calls=%fused_computation | custom fusion | bytes 2101248 | tf_op jit(solution)/shard_map/jit(_take)/gather | solution.py:68
  6.8 4.0 %collective-permute-start = (bf16[1024,512]{1,0:T(8,128)(2,1)}, bf16[1024,512]{1,0:T(8,128)(2,1)S(1)}, u32[]{:S(2)}, u32[]{:S(2)}) collective-permute-start(bf16[1024,512]{1,0:T(8,128)(2,1)} %broadcast_select_fusion), channel_id=1, source_target_pairs={{0,16},{16,32},{32,48},{48,64},{64,80},{80,96},{96,112},{112,128},... | collective-permute-start | bytes 3145736 | tf_op jit(solution)/shard_map/ppermute | solution.py:13
  10.8 22.1 %collective-permute-done = bf16[1024,512]{1,0:T(8,128)(2,1)S(1)} collective-permute-done((bf16[1024,512]{1,0:T(8,128)(2,1)}, bf16[1024,512]{1,0:T(8,128)(2,1)S(1)}, u32[]{:S(2)}, u32[]{:S(2)}) %collective-permute-start) | collective-permute-done | bytes 1048608 | tf_op jit(solution)/shard_map/ppermute | solution.py:13
  32.8 2.0 fusion.39
  38.2 24.7 %all_to_all.10 = f32[8,32,512]{2,1,0:T(8,128)S(1)} all-to-all(f32[8,32,512]{2,1,0:T(8,128)S(1)} %bitcast.56), channel_id=1, replica_groups=mesh['ver'=16,'z'=8,'core'=2] {'z'}, dimensions={0} | all-to-all | bytes 1048576 | tf_op jit(solution)/shard_map/all_to_all | solution.py:35
  63.0 17.5 %all_to_all.11 = f32[8,32,512]{2,1,0:T(8,128)S(1)} all-to-all(f32[8,32,512]{2,1,0:T(8,128)S(1)} %broadcast_in_dim.24), channel_id=1, replica_groups=mesh['ver'=16,'z'=8,'core'=2] {'z'}, dimensions={0} | all-to-all | bytes 1048576 | tf_op jit(solution)/shard_map/all_to_all | solution.py:37
  80.5 3.3 %collective-permute-start.2 = (f32[256,512]{1,0:T(8,128)S(1)}, f32[256,512]{1,0:T(8,128)S(1)}, u32[]{:S(2)}, u32[]{:S(2)}) collective-permute-start(f32[256,512]{1,0:T(8,128)S(1)} %bitcast.53), channel_id=1, source_target_pairs={{0,1},{1,0},{2,3},{3,2},{4,5},{5,4},{6,7},{7,6},{8,9},{9,8},{10,11... | collective-permute-start | bytes 1572872 | tf_op jit(solution)/shard_map/ppermute | solution.py:18
  89.7 17.3 %while.20 = (s32[]{:T(128)}, f32[512,512]{0,1:T(8,128)S(1)}, s32[]{:T(128)}) while((s32[]{:T(128)}, f32[512,512]{0,1:T(8,128)S(1)}, s32[]{:T(128)}) %tuple.32), condition=%wide.region_3.4_spmd, body=%wide.region_2.3_spmd.sunk | while | flops 1611399168 | bytes 7340077 | solution.py:76
  107.0 15.3 %while.21 = (s32[]{:T(128)}, f32[512,512]{0,1:T(8,128)S(1)}, s32[]{:T(128)}) while((s32[]{:T(128)}, f32[512,512]{0,1:T(8,128)S(1)}, s32[]{:T(128)}) %tuple.35), condition=%wide.region_5.6_spmd, body=%wide.region_4.5_spmd.sunk | while | flops 3222011904 | bytes 7340077 | solution.py:77
  123.8 6.0 %collective-permute-start.3 = (f32[256,512]{1,0:T(8,128)S(1)}, f32[256,512]{1,0:T(8,128)}, u32[]{:S(2)}, u32[]{:S(2)}) collective-permute-start(f32[256,512]{1,0:T(8,128)S(1)} %slice_select_fusion.3), channel_id=1, source_target_pairs={{0,16},{16,32},{32,48},{48,64},{64,80},{80,96},{96,112},{112,128},... | collective-permute-start | bytes 1572872 | tf_op jit(solution)/shard_map/ppermute | solution.py:13
  129.8 10.1 %collective-permute-done.3 = f32[256,512]{1,0:T(8,128)} collective-permute-done((f32[256,512]{1,0:T(8,128)S(1)}, f32[256,512]{1,0:T(8,128)}, u32[]{:S(2)}, u32[]{:S(2)}) %collective-permute-start.3) | collective-permute-done | bytes 524320 | tf_op jit(solution)/shard_map/ppermute | solution.py:13
  143.0 3.4 %convolution_select_fusion.3 = f32[512,512]{1,0:T(8,128)S(1)} fusion(f32[512,512]{1,0:T(8,128)S(1)} %convert_select_fusion, f32[256,512]{1,0:T(8,128)} %collective-permute-done.4, f32[256,512]{1,0:T(8,128)} %collective-permute-done.3, pred[]{:T(512)S(6)} %eq.8, pred[]{:T(512)S(6)} %ge.22), kind=kOutput, calls=%fused_computation.12 | convolution fusion | flops 1611661312 | bytes 3145730 | tf_op jit(solution)/shard_map/dot_general | solution.py:56
  147.5 5.8 %collective-permute-start.5 = (f32[256,512]{1,0:T(8,128)S(1)}, f32[256,512]{1,0:T(8,128)S(1)}, u32[]{:S(2)}, u32[]{:S(2)}) collective-permute-start(f32[256,512]{1,0:T(8,128)S(1)} %slice_select_fusion.2), channel_id=1, source_target_pairs={{0,32},{16,48},{32,64},{48,80},{64,96},{80,112},{96,128},{112,144}... | collective-permute-start | bytes 1572872 | tf_op jit(solution)/shard_map/ppermute | solution.py:13
  153.3 10.9 %collective-permute-done.5 = f32[256,512]{1,0:T(8,128)S(1)} collective-permute-done((f32[256,512]{1,0:T(8,128)S(1)}, f32[256,512]{1,0:T(8,128)S(1)}, u32[]{:S(2)}, u32[]{:S(2)}) %collective-permute-start.5) | collective-permute-done | bytes 524320 | tf_op jit(solution)/shard_map/ppermute | solution.py:13
  166.9 3.5 %convolution_select_fusion.2 = f32[512,512]{1,0:T(8,128)S(1)} fusion(f32[512,512]{1,0:T(8,128)} %copy-done.1, f32[256,512]{1,0:T(8,128)S(1)} %collective-permute-done.6, f32[256,512]{1,0:T(8,128)S(1)} %collective-permute-done.5, pred[]{:T(512)S(6)} %eq.8, pred[]{:T(512)S(6)} %ge.21), kind=kOutput, calls=%fused_computation.11 | convolution fusion | flops 1611661312 | bytes 3145730 | tf_op jit(solution)/shard_map/dot_general | solution.py:56
  171.5 9.3 %collective-permute-start.7 = (f32[256,512]{1,0:T(8,128)S(1)}, f32[256,512]{1,0:T(8,128)S(1)}, u32[]{:S(2)}, u32[]{:S(2)}) collective-permute-start(f32[256,512]{1,0:T(8,128)S(1)} %slice_select_fusion.1), channel_id=1, source_target_pairs={{0,64},{16,80},{32,96},{48,112},{64,128},{80,144},{96,160},{112,17... | collective-permute-start | bytes 1572872 | tf_op jit(solution)/shard_map/ppermute | solution.py:13
  180.8 10.9 %collective-permute-done.7 = f32[256,512]{1,0:T(8,128)S(1)} collective-permute-done((f32[256,512]{1,0:T(8,128)S(1)}, f32[256,512]{1,0:T(8,128)S(1)}, u32[]{:S(2)}, u32[]{:S(2)}) %collective-permute-start.7) | collective-permute-done | bytes 524320 | tf_op jit(solution)/shard_map/ppermute | solution.py:13
  194.5 4.1 %convolution_select_fusion.1 = f32[512,512]{1,0:T(8,128)S(1)} fusion(f32[512,512]{1,0:T(8,128)} %copy-done.2, f32[256,512]{1,0:T(8,128)} %collective-permute-done.8, f32[256,512]{1,0:T(8,128)} %copy-done.3, pred[]{:T(512)S(6)} %eq.8, pred[]{:T(512)S(6)} %ge.20), kind=kOutput, calls=%fused_computation.10 | convolution fusion | flops 1611661312 | bytes 3145730 | tf_op jit(solution)/shard_map/dot_general | solution.py:56
  198.7 6.5 %collective-permute-start.9 = (f32[256,512]{1,0:T(8,128)S(1)}, f32[256,512]{1,0:T(8,128)}, u32[]{:S(2)}, u32[]{:S(2)}) collective-permute-start(f32[256,512]{1,0:T(8,128)S(1)} %slice_select_fusion), channel_id=1, source_target_pairs={{0,128},{16,144},{32,160},{48,176},{64,192},{80,208},{96,224},{112... | collective-permute-start | bytes 1572872 | tf_op jit(solution)/shard_map/ppermute | solution.py:13
  205.2 10.1 %collective-permute-done.9 = f32[256,512]{1,0:T(8,128)} collective-permute-done((f32[256,512]{1,0:T(8,128)S(1)}, f32[256,512]{1,0:T(8,128)}, u32[]{:S(2)}, u32[]{:S(2)}) %collective-permute-start.9) | collective-permute-done | bytes 524320 | tf_op jit(solution)/shard_map/ppermute | solution.py:13
  216.6 1.9 collective-permute-done.10
  218.4 3.4 %fusion.5 = bf16[512,512]{1,0:T(8,128)(2,1)S(1)} fusion(f32[512,512]{1,0:T(8,128)S(1)} %convolution_select_fusion.1, f32[256,512]{1,0:T(8,128)} %collective-permute-done.10, f32[256,512]{1,0:T(8,128)} %collective-permute-done.9, pred[]{:T(512)S(6)} %eq.8, pred[]{:T(512)S(6)} %ge.19), kind=kOutput, calls=%fused_computation.13 | convolution fusion | flops 1611923456 | bytes 2621442 | tf_op jit(solution)/shard_map/dot_general | solution.py:56
  221.8 2.7 %fusion.4 = bf16[1,2048,512]{1,2,0:T(8,128)(2,1)} fusion(bf16[512,512]{1,0:T(8,128)(2,1)S(1)} %fusion.5, bf16[1,2048,512]{2,1,0:T(8,128)(2,1)S(1)} %copy-done), kind=kOutput, calls=%fused_computation.8 | convolution fusion | flops 1074790400 | bytes 4718592 | tf_op jit(solution)/shard_map/dot_general | solution.py:82
  224.5 3.9 %copy.5 = bf16[1,2048,512]{2,1,0:T(8,128)(2,1)} copy(bf16[1,2048,512]{1,2,0:T(8,128)(2,1)} %fusion.4) | data formatting | bytes 4194304 | tf_op jit(solution)/shard_map/broadcast_in_dim | solution.py:83
  (70 shorter events, 57.2 us)
Async XLA Ops:
  0.0 1.6 copy-start
  6.8 26.1 %collective-permute-start = (bf16[1024,512]{1,0:T(8,128)(2,1)}, bf16[1024,512]{1,0:T(8,128)(2,1)S(1)}, u32[]{:S(2)}, u32[]{:S(2)}) collective-permute-start(bf16[1024,512]{1,0:T(8,128)(2,1)} %broadcast_select_fusion), channel_id=1, source_target_pairs={{0,16},{16,32},{32,48},{48,64},{64,80},{80,96},{96,112},{112,128},... | collective-permute-start | bytes 3145736 | tf_op jit(solution)/shard_map/ppermute | solution.py:13
  34.9 3.1 %collective-permute-start.1 = (f32[256,512]{1,0:T(8,128)S(1)}, f32[256,512]{1,0:T(8,128)S(1)}, u32[]{:S(2)}, u32[]{:S(2)}) collective-permute-start(f32[256,512]{1,0:T(8,128)S(1)} %slice_select_fusion.4), channel_id=1, source_target_pairs={{0,1},{1,0},{2,3},{3,2},{4,5},{5,4},{6,7},{7,6},{8,9},{9,8},{10,11... | collective-permute-start | bytes 1572872 | tf_op jit(solution)/shard_map/ppermute | solution.py:18
  80.5 4.9 %collective-permute-start.2 = (f32[256,512]{1,0:T(8,128)S(1)}, f32[256,512]{1,0:T(8,128)S(1)}, u32[]{:S(2)}, u32[]{:S(2)}) collective-permute-start(f32[256,512]{1,0:T(8,128)S(1)} %bitcast.53), channel_id=1, source_target_pairs={{0,1},{1,0},{2,3},{3,2},{4,5},{5,4},{6,7},{7,6},{8,9},{9,8},{10,11... | collective-permute-start | bytes 1572872 | tf_op jit(solution)/shard_map/ppermute | solution.py:18
  123.8 16.1 %collective-permute-start.3 = (f32[256,512]{1,0:T(8,128)S(1)}, f32[256,512]{1,0:T(8,128)}, u32[]{:S(2)}, u32[]{:S(2)}) collective-permute-start(f32[256,512]{1,0:T(8,128)S(1)} %slice_select_fusion.3), channel_id=1, source_target_pairs={{0,16},{16,32},{32,48},{48,64},{64,80},{80,96},{96,112},{112,128},... | collective-permute-start | bytes 1572872 | tf_op jit(solution)/shard_map/ppermute | solution.py:13
  139.9 3.1 %collective-permute-start.4 = (f32[256,512]{1,0:T(8,128)}, f32[256,512]{1,0:T(8,128)}, u32[]{:S(2)}, u32[]{:S(2)}) collective-permute-start(f32[256,512]{1,0:T(8,128)} %collective-permute-done.3), channel_id=1, source_target_pairs={{0,1},{1,0},{2,3},{3,2},{4,5},{5,4},{6,7},{7,6},{8,9},{9,8},{10,11... | collective-permute-start | bytes 1572872 | tf_op jit(solution)/shard_map/ppermute | solution.py:18
  146.4 1.0 copy-start.1
  147.5 16.7 %collective-permute-start.5 = (f32[256,512]{1,0:T(8,128)S(1)}, f32[256,512]{1,0:T(8,128)S(1)}, u32[]{:S(2)}, u32[]{:S(2)}) collective-permute-start(f32[256,512]{1,0:T(8,128)S(1)} %slice_select_fusion.2), channel_id=1, source_target_pairs={{0,32},{16,48},{32,64},{48,80},{64,96},{80,112},{96,128},{112,144}... | collective-permute-start | bytes 1572872 | tf_op jit(solution)/shard_map/ppermute | solution.py:13
  164.1 2.8 %collective-permute-start.6 = (f32[256,512]{1,0:T(8,128)S(1)}, f32[256,512]{1,0:T(8,128)S(1)}, u32[]{:S(2)}, u32[]{:S(2)}) collective-permute-start(f32[256,512]{1,0:T(8,128)S(1)} %collective-permute-done.5), channel_id=1, source_target_pairs={{0,1},{1,0},{2,3},{3,2},{4,5},{5,4},{6,7},{7,6},{8,9},{9,8},{10,11... | collective-permute-start | bytes 1572872 | tf_op jit(solution)/shard_map/ppermute | solution.py:18
  170.4 1.0 copy-start.2
  171.5 20.2 %collective-permute-start.7 = (f32[256,512]{1,0:T(8,128)S(1)}, f32[256,512]{1,0:T(8,128)S(1)}, u32[]{:S(2)}, u32[]{:S(2)}) collective-permute-start(f32[256,512]{1,0:T(8,128)S(1)} %slice_select_fusion.1), channel_id=1, source_target_pairs={{0,64},{16,80},{32,96},{48,112},{64,128},{80,144},{96,160},{112,17... | collective-permute-start | bytes 1572872 | tf_op jit(solution)/shard_map/ppermute | solution.py:13
  191.6 1.2 copy-start.3
  191.6 2.9 %collective-permute-start.8 = (f32[256,512]{1,0:T(8,128)S(1)}, f32[256,512]{1,0:T(8,128)}, u32[]{:S(2)}, u32[]{:S(2)}) collective-permute-start(f32[256,512]{1,0:T(8,128)S(1)} %collective-permute-done.7), channel_id=1, source_target_pairs={{0,1},{1,0},{2,3},{3,2},{4,5},{5,4},{6,7},{7,6},{8,9},{9,8},{10,11... | collective-permute-start | bytes 1572872 | tf_op jit(solution)/shard_map/ppermute | solution.py:18
  198.7 16.6 %collective-permute-start.9 = (f32[256,512]{1,0:T(8,128)S(1)}, f32[256,512]{1,0:T(8,128)}, u32[]{:S(2)}, u32[]{:S(2)}) collective-permute-start(f32[256,512]{1,0:T(8,128)S(1)} %slice_select_fusion), channel_id=1, source_target_pairs={{0,128},{16,144},{32,160},{48,176},{64,192},{80,208},{96,224},{112... | collective-permute-start | bytes 1572872 | tf_op jit(solution)/shard_map/ppermute | solution.py:13
  215.3 3.1 %collective-permute-start.10 = (f32[256,512]{1,0:T(8,128)}, f32[256,512]{1,0:T(8,128)}, u32[]{:S(2)}, u32[]{:S(2)}) collective-permute-start(f32[256,512]{1,0:T(8,128)} %collective-permute-done.9), channel_id=1, source_target_pairs={{0,1},{1,0},{2,3},{3,2},{4,5},{5,4},{6,7},{7,6},{8,9},{9,8},{10,11... | collective-permute-start | bytes 1572872 | tf_op jit(solution)/shard_map/ppermute | solution.py:18

commit v3 on v2

--- a/solution.py
+++ b/solution.py
@@ -1,6 +1,7 @@
 import jax
 import jax.numpy as jnp
 from jax import lax
+from jax.experimental import pallas as pl
 from jax.sharding import Mesh, PartitionSpec as P
 
 ITERS = 12
@@ -59,6 +60,26 @@
     return product
 
 
+def aligned_block(rows_ref, prefix_ref, out_ref):
+    product = jnp.dot(rows_ref[...], prefix_ref[...], preferred_element_type=jnp.float32)
+    out_ref[...] = product.astype(out_ref.dtype)
+
+
+def aligned_rows(embedding, prefix_low):
+    _, rows, width = embedding.shape
+    block = 512
+    return pl.pallas_call(
+        aligned_block,
+        grid=(rows // block,),
+        in_specs=[
+            pl.BlockSpec((None, block, width), lambda i: (0, i, 0)),
+            pl.BlockSpec((width, width), lambda i: (0, 0)),
+        ],
+        out_specs=pl.BlockSpec((None, block, width), lambda i: (0, i, 0)),
+        out_shape=jax.ShapeDtypeStruct(embedding.shape, embedding.dtype),
+    )(embedding, prefix_low)
+
+
 def per_device(embedding, anchor_rows):
     own_rows = embedding[0]
     width = own_rows.shape[1]
@@ -79,8 +100,7 @@
     rotation = jnp.where(lax.axis_index("ver") == 0, identity_matrix, rotation)
     prefix = running_product(rotation, "ver", core)
     prefix_low = prefix.astype(jnp.bfloat16)
-    aligned = jnp.dot(own_rows, prefix_low, preferred_element_type=jnp.float32).astype(jnp.bfloat16)
-    return aligned[None]
+    return aligned_rows(embedding, prefix_low)
 
 
 def solution(mesh):

time: 229 us -> 213 us (0.930)
  matrix products: 50.3 us -> 40.3 us
  local copies, waits for them, and re-layouts: 13.6 us -> 7.41 us
  Pallas kernels: 0 us -> 4.74 us
  starting transfers between devices: 41.5 us -> 38.7 us
    dot_general x4, matrix products: 14.4 us -> 8.3 us  [running_product(): longer = jnp.dot(product, earlier, precision=HIGHEST)]
    pallas_call x0 -> x1, Pallas kernels: none -> 4.74 us  [aligned_rows(): pl.pallas_call(aligned_block, grid=(rows // block,), in_specs=[pl.BlockSp...]
    broadcast_in_dim x1 -> x0, local copies, waits for them, and re-layouts: 3.92 us -> none  [per_device(): return aligned[None]]
    ppermute x5, starting transfers between devices: 31.6 us -> 28.9 us  [shifted(): lax.ppermute(value, axis, [(source, source + steps) for source in range(c...]
    dot_general x1 -> x0, matrix products: 2.65 us -> none  [per_device(): jnp.dot(own_rows, prefix_low, preferred_element_type=jnp.float32)]
where the time goes in v3:
time: 213 us
  waiting for transfers between devices  74.4 us (35%)
  blocking collectives  42.2 us (20%)
  matrix products  40.3 us (19%)
  starting transfers between devices  38.7 us (18%)
  local copies, waits for them, and re-layouts  7.41 us (3%)
  Pallas kernels  4.74 us (2%)
  other arithmetic  3.42 us (2%)
    ppermute x5, waiting for transfers between devices, shifted(): lax.ppermute(value, axis, [(source, source + steps) for source in range(c...  65.2 us
    ppermute x5, starting transfers between devices, shifted(): lax.ppermute(value, axis, [(source, source + steps) for source in range(c...  28.9 us
    all_to_all x1, blocking collectives, summed_over(): reduced = lax.all_to_all(pieces, axis, 0, 0, tiled=False).sum(0)  24.7 us
    all_to_all x1, blocking collectives, summed_over(): mine = lax.all_to_all(copies, axis, 0, 0, tiled=False).reshape(mine.shape)  17.5 us
    dot_general x12, matrix products, update(): square = jnp.dot(iterate.T, iterate, precision=precision)  15.6 us
    dot_general x12, matrix products, update(): return 1.5 * iterate - 0.5 * jnp.dot(iterate, square, precision=precision)  15.6 us
    ppermute x6, starting transfers between devices, swapped(): lax.ppermute(value, axis, [(source, source ^ mask) for source in range(co...  9.86 us
    ppermute x6, waiting for transfers between devices, swapped(): lax.ppermute(value, axis, [(source, source ^ mask) for source in range(co...  9.22 us
  transfers between devices with their start and end apart: 11, of which 11 were waited for; matrix products, arithmetic and copies ran while one was open for 0% of the time, Pallas kernels for 0%

profile of v3, /device:TPU:1, one launch (start us, length us, event | category | flops | bytes accessed | tf_op | source)
XLA Modules:
  0.0 212.7 jit_solution(13286209519184757584)
XLA Ops:
  1.4 5.8 %gather_fusion = bf16[1024,512]{1,0:T(8,128)(2,1)S(1)} fusion(bf16[2048,512]{1,0:T(8,128)(2,1)} %bitcast.45, s32[1024]{0:T(1024)S(1)} %fusion.30), kind=kCustom, calls=%fused_computation | custom fusion | bytes 2101248 | tf_op jit(solution)/shard_map/jit(_take)/gather | solution.py:89
  7.5 4.0 %collective-permute-start = (bf16[1024,512]{1,0:T(8,128)(2,1)S(1)}, bf16[1024,512]{1,0:T(8,128)(2,1)S(1)}, u32[]{:S(2)}, u32[]{:S(2)}) collective-permute-start(bf16[1024,512]{1,0:T(8,128)(2,1)S(1)} %broadcast_select_fusion), channel_id=1, source_target_pairs={{0,16},{16,32},{32,48},{48,64},{64,80},{80,96},{96,112},{112,128},... | collective-permute-start | bytes 3145736 | tf_op jit(solution)/shard_map/ppermute | solution.py:14
  11.5 21.8 %collective-permute-done = bf16[1024,512]{1,0:T(8,128)(2,1)S(1)} collective-permute-done((bf16[1024,512]{1,0:T(8,128)(2,1)S(1)}, bf16[1024,512]{1,0:T(8,128)(2,1)S(1)}, u32[]{:S(2)}, u32[]{:S(2)}) %collective-permute-start) | collective-permute-done | bytes 1048608 | tf_op jit(solution)/shard_map/ppermute | solution.py:14
  37.3 24.7 %all_to_all.10 = f32[8,32,512]{2,1,0:T(8,128)S(1)} all-to-all(f32[8,32,512]{2,1,0:T(8,128)S(1)} %bitcast.49), channel_id=1, replica_groups=mesh['ver'=16,'z'=8,'core'=2] {'z'}, dimensions={0} | all-to-all | bytes 1048576 | tf_op jit(solution)/shard_map/all_to_all | solution.py:36
  62.2 17.5 %all_to_all.11 = f32[8,32,512]{2,1,0:T(8,128)S(1)} all-to-all(f32[8,32,512]{2,1,0:T(8,128)S(1)} %broadcast_in_dim.21), channel_id=1, replica_groups=mesh['ver'=16,'z'=8,'core'=2] {'z'}, dimensions={0} | all-to-all | bytes 1048576 | tf_op jit(solution)/shard_map/all_to_all | solution.py:38
  79.7 3.3 %collective-permute-start.2 = (f32[256,512]{1,0:T(8,128)S(1)}, f32[256,512]{1,0:T(8,128)S(1)}, u32[]{:S(2)}, u32[]{:S(2)}) collective-permute-start(f32[256,512]{1,0:T(8,128)S(1)} %bitcast.46), channel_id=1, source_target_pairs={{0,1},{1,0},{2,3},{3,2},{4,5},{5,4},{6,7},{7,6},{8,9},{9,8},{10,11... | collective-permute-start | bytes 1572872 | tf_op jit(solution)/shard_map/ppermute | solution.py:19
  86.7 17.3 %while.20 = (s32[]{:T(128)}, f32[512,512]{0,1:T(8,128)S(1)}, s32[]{:T(128)}) while((s32[]{:T(128)}, f32[512,512]{0,1:T(8,128)S(1)}, s32[]{:T(128)}) %tuple.32), condition=%wide.region_3.4_spmd, body=%wide.region_2.3_spmd.sunk | while | flops 1611399168 | bytes 7340077 | solution.py:97
  104.1 15.3 %while.21 = (s32[]{:T(128)}, f32[512,512]{0,1:T(8,128)S(1)}, s32[]{:T(128)}) while((s32[]{:T(128)}, f32[512,512]{0,1:T(8,128)S(1)}, s32[]{:T(128)}) %tuple.35), condition=%wide.region_5.6_spmd, body=%wide.region_4.5_spmd.sunk | while | flops 3222011904 | bytes 7340077 | solution.py:98
  108.0 1.9 fusion.74
  111.8 1.9 fusion.74
  115.6 1.9 fusion.74
  119.9 4.1 %collective-permute-start.3 = (f32[256,512]{1,0:T(8,128)S(1)}, f32[256,512]{1,0:T(8,128)S(1)}, u32[]{:S(2)}, u32[]{:S(2)}) collective-permute-start(f32[256,512]{1,0:T(8,128)S(1)} %slice_select_fusion.3), channel_id=1, source_target_pairs={{0,16},{16,32},{32,48},{48,64},{64,80},{80,96},{96,112},{112,128},... | collective-permute-start | bytes 1572872 | tf_op jit(solution)/shard_map/ppermute | solution.py:14
  124.1 10.9 %collective-permute-done.3 = f32[256,512]{1,0:T(8,128)S(1)} collective-permute-done((f32[256,512]{1,0:T(8,128)S(1)}, f32[256,512]{1,0:T(8,128)S(1)}, u32[]{:S(2)}, u32[]{:S(2)}) %collective-permute-start.3) | collective-permute-done | bytes 524320 | tf_op jit(solution)/shard_map/ppermute | solution.py:14
  137.7 1.9 convolution_select_fusion.3
  139.7 5.7 %collective-permute-start.5 = (f32[256,512]{1,0:T(8,128)S(1)}, f32[256,512]{1,0:T(8,128)S(1)}, u32[]{:S(2)}, u32[]{:S(2)}) collective-permute-start(f32[256,512]{1,0:T(8,128)S(1)} %slice_select_fusion.2), channel_id=1, source_target_pairs={{0,32},{16,48},{32,64},{48,80},{64,96},{80,112},{96,128},{112,144}... | collective-permute-start | bytes 1572872 | tf_op jit(solution)/shard_map/ppermute | solution.py:14
  145.3 10.9 %collective-permute-done.5 = f32[256,512]{1,0:T(8,128)S(1)} collective-permute-done((f32[256,512]{1,0:T(8,128)S(1)}, f32[256,512]{1,0:T(8,128)S(1)}, u32[]{:S(2)}, u32[]{:S(2)}) %collective-permute-start.5) | collective-permute-done | bytes 524320 | tf_op jit(solution)/shard_map/ppermute | solution.py:14
  159.0 1.9 convolution_select_fusion.2
  160.9 9.3 %collective-permute-start.7 = (f32[256,512]{1,0:T(8,128)S(1)}, f32[256,512]{1,0:T(8,128)S(1)}, u32[]{:S(2)}, u32[]{:S(2)}) collective-permute-start(f32[256,512]{1,0:T(8,128)S(1)} %slice_select_fusion.1), channel_id=1, source_target_pairs={{0,64},{16,80},{32,96},{48,112},{64,128},{80,144},{96,160},{112,17... | collective-permute-start | bytes 1572872 | tf_op jit(solution)/shard_map/ppermute | solution.py:14
  170.2 10.9 %collective-permute-done.7 = f32[256,512]{1,0:T(8,128)S(1)} collective-permute-done((f32[256,512]{1,0:T(8,128)S(1)}, f32[256,512]{1,0:T(8,128)S(1)}, u32[]{:S(2)}, u32[]{:S(2)}) %collective-permute-start.7) | collective-permute-done | bytes 524320 | tf_op jit(solution)/shard_map/ppermute | solution.py:14
  183.9 1.9 convolution_select_fusion.1
  185.8 5.8 %collective-permute-start.9 = (f32[256,512]{1,0:T(8,128)S(1)}, f32[256,512]{1,0:T(8,128)S(1)}, u32[]{:S(2)}, u32[]{:S(2)}) collective-permute-start(f32[256,512]{1,0:T(8,128)S(1)} %slice_select_fusion), channel_id=1, source_target_pairs={{0,128},{16,144},{32,160},{48,176},{64,192},{80,208},{96,224},{112... | collective-permute-start | bytes 1572872 | tf_op jit(solution)/shard_map/ppermute | solution.py:14
  191.6 10.9 %collective-permute-done.9 = f32[256,512]{1,0:T(8,128)S(1)} collective-permute-done((f32[256,512]{1,0:T(8,128)S(1)}, f32[256,512]{1,0:T(8,128)S(1)}, u32[]{:S(2)}, u32[]{:S(2)}) %collective-permute-start.9) | collective-permute-done | bytes 524320 | tf_op jit(solution)/shard_map/ppermute | solution.py:14
  205.2 2.7 %fusion.4.prefix_ref = bf16[512,512]{1,0:T(8,128)(2,1)} fusion(f32[512,512]{1,0:T(8,128)S(1)} %convolution_select_fusion.1, f32[256,512]{1,0:T(8,128)S(1)} %collective-permute-done.10, f32[256,512]{1,0:T(8,128)S(1)} %collective-permute-done.9, pred[]{:T(512)S(6)} %eq.8, pred[]{:T(512)S(6)} %ge.19), kind=kOutput, calls=%fused_computation.11 | convolution fusion | flops 1611923456 | bytes 2621442 | tf_op jit(solution)/shard_map/dot_general | solution.py:57
  207.9 4.7 %shard_map.28 = bf16[1,2048,512]{2,1,0:T(8,128)(2,1)} custom-call(bf16[1,2048,512]{2,1,0:T(8,128)(2,1)} %rows_ref.1, bf16[512,512]{1,0:T(8,128)(2,1)} %fusion.4.prefix_ref), custom_call_target="tpu_custom_call" | custom-call | tf_op jit(solution)/shard_map/pallas_call | solution.py:71
  (61 shorter events, 47.2 us)
Async XLA Ops:
  7.5 25.8 %collective-permute-start = (bf16[1024,512]{1,0:T(8,128)(2,1)S(1)}, bf16[1024,512]{1,0:T(8,128)(2,1)S(1)}, u32[]{:S(2)}, u32[]{:S(2)}) collective-permute-start(bf16[1024,512]{1,0:T(8,128)(2,1)S(1)} %broadcast_select_fusion), channel_id=1, source_target_pairs={{0,16},{16,32},{32,48},{48,64},{64,80},{80,96},{96,112},{112,128},... | collective-permute-start | bytes 3145736 | tf_op jit(solution)/shard_map/ppermute | solution.py:14
  34.0 3.2 %collective-permute-start.1 = (f32[256,512]{1,0:T(8,128)S(1)}, f32[256,512]{1,0:T(8,128)S(1)}, u32[]{:S(2)}, u32[]{:S(2)}) collective-permute-start(f32[256,512]{1,0:T(8,128)S(1)} %slice_select_fusion.4), channel_id=1, source_target_pairs={{0,1},{1,0},{2,3},{3,2},{4,5},{5,4},{6,7},{7,6},{8,9},{9,8},{10,11... | collective-permute-start | bytes 1572872 | tf_op jit(solution)/shard_map/ppermute | solution.py:19
  79.7 4.9 %collective-permute-start.2 = (f32[256,512]{1,0:T(8,128)S(1)}, f32[256,512]{1,0:T(8,128)S(1)}, u32[]{:S(2)}, u32[]{:S(2)}) collective-permute-start(f32[256,512]{1,0:T(8,128)S(1)} %bitcast.46), channel_id=1, source_target_pairs={{0,1},{1,0},{2,3},{3,2},{4,5},{5,4},{6,7},{7,6},{8,9},{9,8},{10,11... | collective-permute-start | bytes 1572872 | tf_op jit(solution)/shard_map/ppermute | solution.py:19
  119.9 15.0 %collective-permute-start.3 = (f32[256,512]{1,0:T(8,128)S(1)}, f32[256,512]{1,0:T(8,128)S(1)}, u32[]{:S(2)}, u32[]{:S(2)}) collective-permute-start(f32[256,512]{1,0:T(8,128)S(1)} %slice_select_fusion.3), channel_id=1, source_target_pairs={{0,16},{16,32},{32,48},{48,64},{64,80},{80,96},{96,112},{112,128},... | collective-permute-start | bytes 1572872 | tf_op jit(solution)/shard_map/ppermute | solution.py:14
  134.9 2.8 %collective-permute-start.4 = (f32[256,512]{1,0:T(8,128)S(1)}, f32[256,512]{1,0:T(8,128)S(1)}, u32[]{:S(2)}, u32[]{:S(2)}) collective-permute-start(f32[256,512]{1,0:T(8,128)S(1)} %collective-permute-done.3), channel_id=1, source_target_pairs={{0,1},{1,0},{2,3},{3,2},{4,5},{5,4},{6,7},{7,6},{8,9},{9,8},{10,11... | collective-permute-start | bytes 1572872 | tf_op jit(solution)/shard_map/ppermute | solution.py:19
  139.7 16.5 %collective-permute-start.5 = (f32[256,512]{1,0:T(8,128)S(1)}, f32[256,512]{1,0:T(8,128)S(1)}, u32[]{:S(2)}, u32[]{:S(2)}) collective-permute-start(f32[256,512]{1,0:T(8,128)S(1)} %slice_select_fusion.2), channel_id=1, source_target_pairs={{0,32},{16,48},{32,64},{48,80},{64,96},{80,112},{96,128},{112,144}... | collective-permute-start | bytes 1572872 | tf_op jit(solution)/shard_map/ppermute | solution.py:14
  156.2 2.8 %collective-permute-start.6 = (f32[256,512]{1,0:T(8,128)S(1)}, f32[256,512]{1,0:T(8,128)S(1)}, u32[]{:S(2)}, u32[]{:S(2)}) collective-permute-start(f32[256,512]{1,0:T(8,128)S(1)} %collective-permute-done.5), channel_id=1, source_target_pairs={{0,1},{1,0},{2,3},{3,2},{4,5},{5,4},{6,7},{7,6},{8,9},{9,8},{10,11... | collective-permute-start | bytes 1572872 | tf_op jit(solution)/shard_map/ppermute | solution.py:19
  160.9 20.2 %collective-permute-start.7 = (f32[256,512]{1,0:T(8,128)S(1)}, f32[256,512]{1,0:T(8,128)S(1)}, u32[]{:S(2)}, u32[]{:S(2)}) collective-permute-start(f32[256,512]{1,0:T(8,128)S(1)} %slice_select_fusion.1), channel_id=1, source_target_pairs={{0,64},{16,80},{32,96},{48,112},{64,128},{80,144},{96,160},{112,17... | collective-permute-start | bytes 1572872 | tf_op jit(solution)/shard_map/ppermute | solution.py:14
  181.1 2.8 %collective-permute-start.8 = (f32[256,512]{1,0:T(8,128)S(1)}, f32[256,512]{1,0:T(8,128)S(1)}, u32[]{:S(2)}, u32[]{:S(2)}) collective-permute-start(f32[256,512]{1,0:T(8,128)S(1)} %collective-permute-done.7), channel_id=1, source_target_pairs={{0,1},{1,0},{2,3},{3,2},{4,5},{5,4},{6,7},{7,6},{8,9},{9,8},{10,11... | collective-permute-start | bytes 1572872 | tf_op jit(solution)/shard_map/ppermute | solution.py:19
  185.8 16.6 %collective-permute-start.9 = (f32[256,512]{1,0:T(8,128)S(1)}, f32[256,512]{1,0:T(8,128)S(1)}, u32[]{:S(2)}, u32[]{:S(2)}) collective-permute-start(f32[256,512]{1,0:T(8,128)S(1)} %slice_select_fusion), channel_id=1, source_target_pairs={{0,128},{16,144},{32,160},{48,176},{64,192},{80,208},{96,224},{112... | collective-permute-start | bytes 1572872 | tf_op jit(solution)/shard_map/ppermute | solution.py:14
  202.5 2.8 %collective-permute-start.10 = (f32[256,512]{1,0:T(8,128)S(1)}, f32[256,512]{1,0:T(8,128)S(1)}, u32[]{:S(2)}, u32[]{:S(2)}) collective-permute-start(f32[256,512]{1,0:T(8,128)S(1)} %collective-permute-done.9), channel_id=1, source_target_pairs={{0,1},{1,0},{2,3},{3,2},{4,5},{5,4},{6,7},{7,6},{8,9},{9,8},{10,11... | collective-permute-start | bytes 1572872 | tf_op jit(solution)/shard_map/ppermute | solution.py:19

commit v4 on v3

--- a/solution.py
+++ b/solution.py
@@ -47,17 +47,30 @@
     return update
 
 
+def column_half(matrix, core):
+    half = matrix.shape[1] // 2
+    return jnp.where(core == 0, matrix[:, :half], matrix[:, half:])
+
+
+def joined_columns(mine, other, core):
+    return jnp.where(
+        core == 0, jnp.concatenate([mine, other], axis=1), jnp.concatenate([other, mine], axis=1)
+    )
+
+
 def running_product(rotation, axis, core):
     count, mine = (lax.axis_size(axis), lax.axis_index(axis))
-    product = rotation
+    whole = rotation
+    own_columns = column_half(rotation, core)
     steps = 1
     while steps < count:
-        received = shifted(halves(product, core)[0], axis, steps)
-        earlier = joined(received, swapped(received, "core", 1), core)
-        longer = jnp.dot(product, earlier, precision=HIGHEST)
-        product = jnp.where(mine >= steps, longer, product)
+        received = shifted(own_columns, axis, steps)
+        longer = jnp.dot(whole, received, precision=HIGHEST)
+        own_columns = jnp.where(mine >= steps, longer, own_columns)
         steps *= 2
-    return product
+        if steps < count:
+            whole = joined_columns(own_columns, swapped(own_columns, "core", 1), core)
+    return own_columns
 
 
 def aligned_block(rows_ref, prefix_ref, out_ref):
@@ -98,8 +111,8 @@
     rotation = lax.fori_loop(ROUGH_ITERS, ITERS, newton_update(HIGHEST), iterate)
     identity_matrix = jnp.eye(width, dtype=jnp.float32)
     rotation = jnp.where(lax.axis_index("ver") == 0, identity_matrix, rotation)
-    prefix = running_product(rotation, "ver", core)
-    prefix_low = prefix.astype(jnp.bfloat16)
+    own_low = running_product(rotation, "ver", core).astype(jnp.bfloat16)
+    prefix_low = joined_columns(own_low, swapped(own_low, "core", 1), core)
     return aligned_rows(embedding, prefix_low)
 
 

time: 213 us -> 205 us (0.962)
  matrix products: 40.3 us -> 36 us
  waiting for transfers between devices: 74.4 us -> 70.4 us
    ppermute x6, waiting for transfers between devices: 9.22 us -> 4.24 us  [swapped(): lax.ppermute(value, axis, [(source, source ^ mask) for source in range(co...]
    dot_general x4, matrix products: 8.3 us -> 3.97 us  [running_product(): longer = jnp.dot(whole, received, precision=HIGHEST)]
  transfers between devices with their start and end apart: 11 -> 11, of which waited for: 11 -> 8; matrix products, arithmetic and copies ran while one was open for 0% -> 0% of each run, Pallas kernels for 0% -> 0%
where the time goes in v4:
time: 205 us; the launch traced here: 204 us
  waiting for transfers between devices  70.4 us (34%)
  blocking collectives  42.2 us (21%)
  starting transfers between devices  38.2 us (19%)
  matrix products  36 us (18%)
  local copies, waits for them, and re-layouts  7.41 us (4%)
  Pallas kernels  4.74 us (2%)
  other arithmetic  4.09 us (2%)
    ppermute x5, waiting for transfers between devices, shifted(): lax.ppermute(value, axis, [(source, source + steps) for source in range(c...  66.2 us
    ppermute x5, starting transfers between devices, shifted(): lax.ppermute(value, axis, [(source, source + steps) for source in range(c...  28.9 us
    all_to_all x1, blocking collectives, summed_over(): reduced = lax.all_to_all(pieces, axis, 0, 0, tiled=False).sum(0)  24.7 us
    all_to_all x1, blocking collectives, summed_over(): mine = lax.all_to_all(copies, axis, 0, 0, tiled=False).reshape(mine.shape)  17.5 us
    dot_general x12, matrix products, update(): square = jnp.dot(iterate.T, iterate, precision=precision)  15.6 us
    dot_general x12, matrix products, update(): return 1.5 * iterate - 0.5 * jnp.dot(iterate, square, precision=precision)  15.6 us
    ppermute x6, starting transfers between devices, swapped(): lax.ppermute(value, axis, [(source, source ^ mask) for source in range(co...  9.34 us
    gather x1, local copies, waits for them, and re-layouts, per_device(): own_slab = jnp.take(own_rows, positions, axis=0)  5.85 us
  transfers between devices with their start and end apart: 11, of which 8 were waited for; matrix products, arithmetic and copies ran while one was open for 0% of the time, Pallas kernels for 0%

profile of v4, /device:TPU:1, one launch (start us, length us, event | category | flops | bytes accessed | tf_op | source)
XLA Modules:
  0.0 204.5 jit_solution(9441082855025683499)
XLA Ops:
  1.4 5.8 %gather_fusion = bf16[1024,512]{1,0:T(8,128)(2,1)S(1)} fusion(bf16[2048,512]{1,0:T(8,128)(2,1)} %bitcast.46, s32[1024]{0:T(1024)S(1)} %fusion.24), kind=kCustom, calls=%fused_computation | custom fusion | bytes 2101248 | tf_op jit(solution)/shard_map/jit(_take)/gather | solution.py:102
  7.5 4.0 %collective-permute-start = (bf16[1024,512]{1,0:T(8,128)(2,1)S(1)}, bf16[1024,512]{1,0:T(8,128)(2,1)S(1)}, u32[]{:S(2)}, u32[]{:S(2)}) collective-permute-start(bf16[1024,512]{1,0:T(8,128)(2,1)S(1)} %broadcast_select_fusion), channel_id=1, source_target_pairs={{0,16},{16,32},{32,48},{48,64},{64,80},{80,96},{96,112},{112,128},... | collective-permute-start | bytes 3145736 | tf_op jit(solution)/shard_map/ppermute | solution.py:14
  11.5 21.8 %collective-permute-done = bf16[1024,512]{1,0:T(8,128)(2,1)S(1)} collective-permute-done((bf16[1024,512]{1,0:T(8,128)(2,1)S(1)}, bf16[1024,512]{1,0:T(8,128)(2,1)S(1)}, u32[]{:S(2)}, u32[]{:S(2)}) %collective-permute-start) | collective-permute-done | bytes 1048608 | tf_op jit(solution)/shard_map/ppermute | solution.py:14
  37.3 24.7 %all_to_all.10 = f32[8,32,512]{2,1,0:T(8,128)S(1)} all-to-all(f32[8,32,512]{2,1,0:T(8,128)S(1)} %bitcast.50), channel_id=1, replica_groups=mesh['ver'=16,'z'=8,'core'=2] {'z'}, dimensions={0} | all-to-all | bytes 1048576 | tf_op jit(solution)/shard_map/all_to_all | solution.py:36
  62.2 17.5 %all_to_all.11 = f32[8,32,512]{2,1,0:T(8,128)S(1)} all-to-all(f32[8,32,512]{2,1,0:T(8,128)S(1)} %broadcast_in_dim.21), channel_id=1, replica_groups=mesh['ver'=16,'z'=8,'core'=2] {'z'}, dimensions={0} | all-to-all | bytes 1048576 | tf_op jit(solution)/shard_map/all_to_all | solution.py:38
  79.7 3.3 %collective-permute-start.2 = (f32[256,512]{1,0:T(8,128)S(1)}, f32[256,512]{1,0:T(8,128)S(1)}, u32[]{:S(2)}, u32[]{:S(2)}) collective-permute-start(f32[256,512]{1,0:T(8,128)S(1)} %bitcast.47), channel_id=1, source_target_pairs={{0,1},{1,0},{2,3},{3,2},{4,5},{5,4},{6,7},{7,6},{8,9},{9,8},{10,11... | collective-permute-start | bytes 1572872 | tf_op jit(solution)/shard_map/ppermute | solution.py:19
  86.7 17.3 %while.20 = (s32[]{:T(128)}, f32[512,512]{0,1:T(8,128)S(1)}, s32[]{:T(128)}) while((s32[]{:T(128)}, f32[512,512]{0,1:T(8,128)S(1)}, s32[]{:T(128)}) %tuple.32), condition=%wide.region_3.4_spmd, body=%wide.region_2.3_spmd.sunk | while | flops 1611399168 | bytes 7340077 | solution.py:110
  104.1 15.3 %while.21 = (s32[]{:T(128)}, f32[512,512]{0,1:T(8,128)S(1)}, s32[]{:T(128)}) while((s32[]{:T(128)}, f32[512,512]{0,1:T(8,128)S(1)}, s32[]{:T(128)}) %tuple.35), condition=%wide.region_5.6_spmd, body=%wide.region_4.5_spmd.sunk | while | flops 3222011904 | bytes 7340077 | solution.py:111
  104.2 1.9 fusion.68
  106.0 1.9 fusion.69
  108.0 1.9 fusion.68
  109.8 1.9 fusion.69
  111.8 1.9 fusion.68
  115.6 1.9 fusion.68
  117.5 1.9 fusion.69
  119.9 4.1 %collective-permute-start.3 = (f32[512,256]{1,0:T(8,128)S(1)}, f32[512,256]{1,0:T(8,128)S(1)}, u32[]{:S(2)}, u32[]{:S(2)}) collective-permute-start(f32[512,256]{1,0:T(8,128)S(1)} %slice_select_fusion), channel_id=1, source_target_pairs={{0,16},{16,32},{32,48},{48,64},{64,80},{80,96},{96,112},{112,128},... | collective-permute-start | bytes 1572872 | tf_op jit(solution)/shard_map/ppermute | solution.py:14
  124.1 10.9 %collective-permute-done.3 = f32[512,256]{1,0:T(8,128)S(1)} collective-permute-done((f32[512,256]{1,0:T(8,128)S(1)}, f32[512,256]{1,0:T(8,128)S(1)}, u32[]{:S(2)}, u32[]{:S(2)}) %collective-permute-start.3) | collective-permute-done | bytes 524320 | tf_op jit(solution)/shard_map/ppermute | solution.py:14
  137.4 5.6 %collective-permute-start.5 = (f32[512,256]{1,0:T(8,128)S(1)}, f32[512,256]{1,0:T(8,128)S(1)}, u32[]{:S(2)}, u32[]{:S(2)}) collective-permute-start(f32[512,256]{1,0:T(8,128)S(1)} %convolution_select_fusion.3), channel_id=1, source_target_pairs={{0,32},{16,48},{32,64},{48,80},{64,96},{80,112},{96,128},{112,144}... | collective-permute-start | bytes 1572872 | tf_op jit(solution)/shard_map/ppermute | solution.py:14
  143.1 11.2 %collective-permute-done.5 = f32[512,256]{1,0:T(8,128)S(1)} collective-permute-done((f32[512,256]{1,0:T(8,128)S(1)}, f32[512,256]{1,0:T(8,128)S(1)}, u32[]{:S(2)}, u32[]{:S(2)}) %collective-permute-start.5) | collective-permute-done | bytes 524320 | tf_op jit(solution)/shard_map/ppermute | solution.py:14
  156.2 9.3 %collective-permute-start.7 = (f32[512,256]{1,0:T(8,128)S(1)}, f32[512,256]{1,0:T(8,128)S(1)}, u32[]{:S(2)}, u32[]{:S(2)}) collective-permute-start(f32[512,256]{1,0:T(8,128)S(1)} %convolution_select_fusion.2), channel_id=1, source_target_pairs={{0,64},{16,80},{32,96},{48,112},{64,128},{80,144},{96,160},{112,17... | collective-permute-start | bytes 1572872 | tf_op jit(solution)/shard_map/ppermute | solution.py:14
  165.6 11.2 %collective-permute-done.7 = f32[512,256]{1,0:T(8,128)S(1)} collective-permute-done((f32[512,256]{1,0:T(8,128)S(1)}, f32[512,256]{1,0:T(8,128)S(1)}, u32[]{:S(2)}, u32[]{:S(2)}) %collective-permute-start.7) | collective-permute-done | bytes 524320 | tf_op jit(solution)/shard_map/ppermute | solution.py:14
  178.7 5.8 %collective-permute-start.9 = (f32[512,256]{1,0:T(8,128)S(1)}, f32[512,256]{1,0:T(8,128)S(1)}, u32[]{:S(2)}, u32[]{:S(2)}) collective-permute-start(f32[512,256]{1,0:T(8,128)S(1)} %convolution_select_fusion.1), channel_id=1, source_target_pairs={{0,128},{16,144},{32,160},{48,176},{64,192},{80,208},{96,224},{112... | collective-permute-start | bytes 1572872 | tf_op jit(solution)/shard_map/ppermute | solution.py:14
  184.5 11.2 %collective-permute-done.9 = f32[512,256]{1,0:T(8,128)S(1)} collective-permute-done((f32[512,256]{1,0:T(8,128)S(1)}, f32[512,256]{1,0:T(8,128)S(1)}, u32[]{:S(2)}, u32[]{:S(2)}) %collective-permute-start.9) | collective-permute-done | bytes 524320 | tf_op jit(solution)/shard_map/ppermute | solution.py:14
  199.7 4.7 %shard_map.28 = bf16[1,2048,512]{2,1,0:T(8,128)(2,1)} custom-call(bf16[1,2048,512]{2,1,0:T(8,128)(2,1)} %rows_ref.1, bf16[512,512]{1,0:T(8,128)(2,1)} %maximum_select_fusion.7.prefix_ref), custom_call_target="tpu_custom_call" | custom-call | tf_op jit(solution)/shard_map/pallas_call | solution.py:84
  (59 shorter events, 38.9 us)
Async XLA Ops:
  7.5 25.8 %collective-permute-start = (bf16[1024,512]{1,0:T(8,128)(2,1)S(1)}, bf16[1024,512]{1,0:T(8,128)(2,1)S(1)}, u32[]{:S(2)}, u32[]{:S(2)}) collective-permute-start(bf16[1024,512]{1,0:T(8,128)(2,1)S(1)} %broadcast_select_fusion), channel_id=1, source_target_pairs={{0,16},{16,32},{32,48},{48,64},{64,80},{80,96},{96,112},{112,128},... | collective-permute-start | bytes 3145736 | tf_op jit(solution)/shard_map/ppermute | solution.py:14
  34.0 3.2 %collective-permute-start.1 = (f32[256,512]{1,0:T(8,128)S(1)}, f32[256,512]{1,0:T(8,128)S(1)}, u32[]{:S(2)}, u32[]{:S(2)}) collective-permute-start(f32[256,512]{1,0:T(8,128)S(1)} %slice_select_fusion.1), channel_id=1, source_target_pairs={{0,1},{1,0},{2,3},{3,2},{4,5},{5,4},{6,7},{7,6},{8,9},{9,8},{10,11... | collective-permute-start | bytes 1572872 | tf_op jit(solution)/shard_map/ppermute | solution.py:19
  79.7 4.9 %collective-permute-start.2 = (f32[256,512]{1,0:T(8,128)S(1)}, f32[256,512]{1,0:T(8,128)S(1)}, u32[]{:S(2)}, u32[]{:S(2)}) collective-permute-start(f32[256,512]{1,0:T(8,128)S(1)} %bitcast.47), channel_id=1, source_target_pairs={{0,1},{1,0},{2,3},{3,2},{4,5},{5,4},{6,7},{7,6},{8,9},{9,8},{10,11... | collective-permute-start | bytes 1572872 | tf_op jit(solution)/shard_map/ppermute | solution.py:19
  119.9 15.0 %collective-permute-start.3 = (f32[512,256]{1,0:T(8,128)S(1)}, f32[512,256]{1,0:T(8,128)S(1)}, u32[]{:S(2)}, u32[]{:S(2)}) collective-permute-start(f32[512,256]{1,0:T(8,128)S(1)} %slice_select_fusion), channel_id=1, source_target_pairs={{0,16},{16,32},{32,48},{48,64},{64,80},{80,96},{96,112},{112,128},... | collective-permute-start | bytes 1572872 | tf_op jit(solution)/shard_map/ppermute | solution.py:14
  135.9 7.2 %collective-permute-start.4 = (f32[512,256]{1,0:T(8,128)S(1)}, f32[512,256]{1,0:T(8,128)S(1)}, u32[]{:S(2)}, u32[]{:S(2)}) collective-permute-start(f32[512,256]{1,0:T(8,128)S(1)} %convolution_select_fusion.3), channel_id=1, source_target_pairs={{0,1},{1,0},{2,3},{3,2},{4,5},{5,4},{6,7},{7,6},{8,9},{9,8},{10,11... | collective-permute-start | bytes 1572872 | tf_op jit(solution)/shard_map/ppermute | solution.py:19
  137.4 16.9 %collective-permute-start.5 = (f32[512,256]{1,0:T(8,128)S(1)}, f32[512,256]{1,0:T(8,128)S(1)}, u32[]{:S(2)}, u32[]{:S(2)}) collective-permute-start(f32[512,256]{1,0:T(8,128)S(1)} %convolution_select_fusion.3), channel_id=1, source_target_pairs={{0,32},{16,48},{32,64},{48,80},{64,96},{80,112},{96,128},{112,144}... | collective-permute-start | bytes 1572872 | tf_op jit(solution)/shard_map/ppermute | solution.py:14
  155.3 10.3 %collective-permute-start.6 = (f32[512,256]{1,0:T(8,128)S(1)}, f32[512,256]{1,0:T(8,128)S(1)}, u32[]{:S(2)}, u32[]{:S(2)}) collective-permute-start(f32[512,256]{1,0:T(8,128)S(1)} %convolution_select_fusion.2), channel_id=1, source_target_pairs={{0,1},{1,0},{2,3},{3,2},{4,5},{5,4},{6,7},{7,6},{8,9},{9,8},{10,11... | collective-permute-start | bytes 1572872 | tf_op jit(solution)/shard_map/ppermute | solution.py:19
  156.2 20.5 %collective-permute-start.7 = (f32[512,256]{1,0:T(8,128)S(1)}, f32[512,256]{1,0:T(8,128)S(1)}, u32[]{:S(2)}, u32[]{:S(2)}) collective-permute-start(f32[512,256]{1,0:T(8,128)S(1)} %convolution_select_fusion.2), channel_id=1, source_target_pairs={{0,64},{16,80},{32,96},{48,112},{64,128},{80,144},{96,160},{112,17... | collective-permute-start | bytes 1572872 | tf_op jit(solution)/shard_map/ppermute | solution.py:14
  177.7 6.7 %collective-permute-start.8 = (f32[512,256]{1,0:T(8,128)S(1)}, f32[512,256]{1,0:T(8,128)S(1)}, u32[]{:S(2)}, u32[]{:S(2)}) collective-permute-start(f32[512,256]{1,0:T(8,128)S(1)} %convolution_select_fusion.1), channel_id=1, source_target_pairs={{0,1},{1,0},{2,3},{3,2},{4,5},{5,4},{6,7},{7,6},{8,9},{9,8},{10,11... | collective-permute-start | bytes 1572872 | tf_op jit(solution)/shard_map/ppermute | solution.py:19
  178.7 17.0 %collective-permute-start.9 = (f32[512,256]{1,0:T(8,128)S(1)}, f32[512,256]{1,0:T(8,128)S(1)}, u32[]{:S(2)}, u32[]{:S(2)}) collective-permute-start(f32[512,256]{1,0:T(8,128)S(1)} %convolution_select_fusion.1), channel_id=1, source_target_pairs={{0,128},{16,144},{32,160},{48,176},{64,192},{80,208},{96,224},{112... | collective-permute-start | bytes 1572872 | tf_op jit(solution)/shard_map/ppermute | solution.py:14
  196.7 2.1 %collective-permute-start.10 = (bf16[512,256]{1,0:T(8,128)(2,1)S(1)}, bf16[512,256]{1,0:T(8,128)(2,1)S(1)}, u32[]{:S(2)}, u32[]{:S(2)}) collective-permute-start(bf16[512,256]{1,0:T(8,128)(2,1)S(1)} %fusion.4), channel_id=1, source_target_pairs={{0,1},{1,0},{2,3},{3,2},{4,5},{5,4},{6,7},{7,6},{8,9},{9,8},{10,11... | collective-permute-start | bytes 786440 | tf_op jit(solution)/shard_map/ppermute | solution.py:19

commit v5 on v4

--- a/solution.py
+++ b/solution.py
@@ -5,7 +5,7 @@
 from jax.sharding import Mesh, PartitionSpec as P
 
 ITERS = 12
-ROUGH_ITERS = 8
+ROUGH_ITERS = 10
 HIGHEST = lax.Precision.HIGHEST
 
 

time: 205 us -> 202 us (0.985)
  matrix products: 36 us -> 32.7 us
where the time goes in v5:
time: 202 us; the launch traced here: 201 us
  waiting for transfers between devices  70.4 us (35%)
  blocking collectives  42.2 us (21%)
  starting transfers between devices  38.2 us (19%)
  matrix products  32.7 us (16%)
  local copies, waits for them, and re-layouts  7.41 us (4%)
  Pallas kernels  4.74 us (2%)
  other arithmetic  4.09 us (2%)
    ppermute x5, waiting for transfers between devices, shifted(): lax.ppermute(value, axis, [(source, source + steps) for source in range(c...  66.2 us
    ppermute x5, starting transfers between devices, shifted(): lax.ppermute(value, axis, [(source, source + steps) for source in range(c...  28.9 us
    all_to_all x1, blocking collectives, summed_over(): reduced = lax.all_to_all(pieces, axis, 0, 0, tiled=False).sum(0)  24.7 us
    all_to_all x1, blocking collectives, summed_over(): mine = lax.all_to_all(copies, axis, 0, 0, tiled=False).reshape(mine.shape)  17.5 us
    dot_general x12, matrix products, update(): return 1.5 * iterate - 0.5 * jnp.dot(iterate, square, precision=precision)  14 us
    dot_general x12, matrix products, update(): square = jnp.dot(iterate.T, iterate, precision=precision)  14 us
    ppermute x6, starting transfers between devices, swapped(): lax.ppermute(value, axis, [(source, source ^ mask) for source in range(co...  9.34 us
    gather x1, local copies, waits for them, and re-layouts, per_device(): own_slab = jnp.take(own_rows, positions, axis=0)  5.85 us
  transfers between devices with their start and end apart: 11, of which 8 were waited for; matrix products, arithmetic and copies ran while one was open for 0% of the time, Pallas kernels for 0%

profile of v5, /device:TPU:1, one launch (start us, length us, event | category | flops | bytes accessed | tf_op | source)
XLA Modules:
  0.0 201.2 jit_solution(16141781626092625354)
XLA Ops:
  1.4 5.8 %gather_fusion = bf16[1024,512]{1,0:T(8,128)(2,1)S(1)} fusion(bf16[2048,512]{1,0:T(8,128)(2,1)} %bitcast.46, s32[1024]{0:T(1024)S(1)} %fusion.24), kind=kCustom, calls=%fused_computation | custom fusion | bytes 2101248 | tf_op jit(solution)/shard_map/jit(_take)/gather | solution.py:102
  7.5 4.0 %collective-permute-start = (bf16[1024,512]{1,0:T(8,128)(2,1)S(1)}, bf16[1024,512]{1,0:T(8,128)(2,1)S(1)}, u32[]{:S(2)}, u32[]{:S(2)}) collective-permute-start(bf16[1024,512]{1,0:T(8,128)(2,1)S(1)} %broadcast_select_fusion), channel_id=1, source_target_pairs={{0,16},{16,32},{32,48},{48,64},{64,80},{80,96},{96,112},{112,128},... | collective-permute-start | bytes 3145736 | tf_op jit(solution)/shard_map/ppermute | solution.py:14
  11.5 21.8 %collective-permute-done = bf16[1024,512]{1,0:T(8,128)(2,1)S(1)} collective-permute-done((bf16[1024,512]{1,0:T(8,128)(2,1)S(1)}, bf16[1024,512]{1,0:T(8,128)(2,1)S(1)}, u32[]{:S(2)}, u32[]{:S(2)}) %collective-permute-start) | collective-permute-done | bytes 1048608 | tf_op jit(solution)/shard_map/ppermute | solution.py:14
  34.0 1.6 collective-permute-start.1
  35.7 1.5 collective-permute-done.1
  37.3 24.7 %all_to_all.10 = f32[8,32,512]{2,1,0:T(8,128)S(1)} all-to-all(f32[8,32,512]{2,1,0:T(8,128)S(1)} %bitcast.50), channel_id=1, replica_groups=mesh['ver'=16,'z'=8,'core'=2] {'z'}, dimensions={0} | all-to-all | bytes 1048576 | tf_op jit(solution)/shard_map/all_to_all | solution.py:36
  62.2 17.5 %all_to_all.11 = f32[8,32,512]{2,1,0:T(8,128)S(1)} all-to-all(f32[8,32,512]{2,1,0:T(8,128)S(1)} %broadcast_in_dim.21), channel_id=1, replica_groups=mesh['ver'=16,'z'=8,'core'=2] {'z'}, dimensions={0} | all-to-all | bytes 1048576 | tf_op jit(solution)/shard_map/all_to_all | solution.py:38
  79.7 3.3 %collective-permute-start.2 = (f32[256,512]{1,0:T(8,128)S(1)}, f32[256,512]{1,0:T(8,128)S(1)}, u32[]{:S(2)}, u32[]{:S(2)}) collective-permute-start(f32[256,512]{1,0:T(8,128)S(1)} %bitcast.47), channel_id=1, source_target_pairs={{0,1},{1,0},{2,3},{3,2},{4,5},{5,4},{6,7},{7,6},{8,9},{9,8},{10,11... | collective-permute-start | bytes 1572872 | tf_op jit(solution)/shard_map/ppermute | solution.py:19
  83.0 1.5 collective-permute-done.2
  86.7 21.6 %while.20 = (s32[]{:T(128)}, f32[512,512]{0,1:T(8,128)S(1)}, s32[]{:T(128)}) while((s32[]{:T(128)}, f32[512,512]{0,1:T(8,128)S(1)}, s32[]{:T(128)}) %tuple.32), condition=%wide.region_3.4_spmd, body=%wide.region_2.3_spmd.sunk | while | flops 1611399168 | bytes 7340077 | solution.py:110
  108.4 7.6 %while.21 = (s32[]{:T(128)}, f32[512,512]{0,1:T(8,128)S(1)}, s32[]{:T(128)}) while((s32[]{:T(128)}, f32[512,512]{0,1:T(8,128)S(1)}, s32[]{:T(128)}) %tuple.35), condition=%wide.region_5.6_spmd, body=%wide.region_4.5_spmd.sunk | while | flops 3222011904 | bytes 7340077 | solution.py:111
  108.5 1.9 fusion.68
  110.4 1.9 fusion.69
  112.3 1.9 fusion.68
  114.2 1.9 fusion.69
  116.6 4.1 %collective-permute-start.3 = (f32[512,256]{1,0:T(8,128)S(1)}, f32[512,256]{1,0:T(8,128)S(1)}, u32[]{:S(2)}, u32[]{:S(2)}) collective-permute-start(f32[512,256]{1,0:T(8,128)S(1)} %slice_select_fusion), channel_id=1, source_target_pairs={{0,16},{16,32},{32,48},{48,64},{64,80},{80,96},{96,112},{112,128},... | collective-permute-start | bytes 1572872 | tf_op jit(solution)/shard_map/ppermute | solution.py:14
  120.7 10.9 %collective-permute-done.3 = f32[512,256]{1,0:T(8,128)S(1)} collective-permute-done((f32[512,256]{1,0:T(8,128)S(1)}, f32[512,256]{1,0:T(8,128)S(1)}, u32[]{:S(2)}, u32[]{:S(2)}) %collective-permute-start.3) | collective-permute-done | bytes 524320 | tf_op jit(solution)/shard_map/ppermute | solution.py:14
  134.1 5.6 %collective-permute-start.5 = (f32[512,256]{1,0:T(8,128)S(1)}, f32[512,256]{1,0:T(8,128)S(1)}, u32[]{:S(2)}, u32[]{:S(2)}) collective-permute-start(f32[512,256]{1,0:T(8,128)S(1)} %convolution_select_fusion.3), channel_id=1, source_target_pairs={{0,32},{16,48},{32,64},{48,80},{64,96},{80,112},{96,128},{112,144}... | collective-permute-start | bytes 1572872 | tf_op jit(solution)/shard_map/ppermute | solution.py:14
  139.8 11.2 %collective-permute-done.5 = f32[512,256]{1,0:T(8,128)S(1)} collective-permute-done((f32[512,256]{1,0:T(8,128)S(1)}, f32[512,256]{1,0:T(8,128)S(1)}, u32[]{:S(2)}, u32[]{:S(2)}) %collective-permute-start.5) | collective-permute-done | bytes 524320 | tf_op jit(solution)/shard_map/ppermute | solution.py:14
  152.9 9.3 %collective-permute-start.7 = (f32[512,256]{1,0:T(8,128)S(1)}, f32[512,256]{1,0:T(8,128)S(1)}, u32[]{:S(2)}, u32[]{:S(2)}) collective-permute-start(f32[512,256]{1,0:T(8,128)S(1)} %convolution_select_fusion.2), channel_id=1, source_target_pairs={{0,64},{16,80},{32,96},{48,112},{64,128},{80,144},{96,160},{112,17... | collective-permute-start | bytes 1572872 | tf_op jit(solution)/shard_map/ppermute | solution.py:14
  162.2 11.2 %collective-permute-done.7 = f32[512,256]{1,0:T(8,128)S(1)} collective-permute-done((f32[512,256]{1,0:T(8,128)S(1)}, f32[512,256]{1,0:T(8,128)S(1)}, u32[]{:S(2)}, u32[]{:S(2)}) %collective-permute-start.7) | collective-permute-done | bytes 524320 | tf_op jit(solution)/shard_map/ppermute | solution.py:14
  175.4 5.8 %collective-permute-start.9 = (f32[512,256]{1,0:T(8,128)S(1)}, f32[512,256]{1,0:T(8,128)S(1)}, u32[]{:S(2)}, u32[]{:S(2)}) collective-permute-start(f32[512,256]{1,0:T(8,128)S(1)} %convolution_select_fusion.1), channel_id=1, source_target_pairs={{0,128},{16,144},{32,160},{48,176},{64,192},{80,208},{96,224},{112... | collective-permute-start | bytes 1572872 | tf_op jit(solution)/shard_map/ppermute | solution.py:14
  181.2 11.2 %collective-permute-done.9 = f32[512,256]{1,0:T(8,128)S(1)} collective-permute-done((f32[512,256]{1,0:T(8,128)S(1)}, f32[512,256]{1,0:T(8,128)S(1)}, u32[]{:S(2)}, u32[]{:S(2)}) %collective-permute-start.9) | collective-permute-done | bytes 524320 | tf_op jit(solution)/shard_map/ppermute | solution.py:14
  196.4 4.7 %shard_map.28 = bf16[1,2048,512]{2,1,0:T(8,128)(2,1)} custom-call(bf16[1,2048,512]{2,1,0:T(8,128)(2,1)} %rows_ref.1, bf16[512,512]{1,0:T(8,128)(2,1)} %maximum_select_fusion.7.prefix_ref), custom_call_target="tpu_custom_call" | custom-call | tf_op jit(solution)/shard_map/pallas_call | solution.py:84
  (59 shorter events, 36.5 us)
Async XLA Ops:
  7.5 25.8 %collective-permute-start = (bf16[1024,512]{1,0:T(8,128)(2,1)S(1)}, bf16[1024,512]{1,0:T(8,128)(2,1)S(1)}, u32[]{:S(2)}, u32[]{:S(2)}) collective-permute-start(bf16[1024,512]{1,0:T(8,128)(2,1)S(1)} %broadcast_select_fusion), channel_id=1, source_target_pairs={{0,16},{16,32},{32,48},{48,64},{64,80},{80,96},{96,112},{112,128},... | collective-permute-start | bytes 3145736 | tf_op jit(solution)/shard_map/ppermute | solution.py:14
  34.0 3.2 %collective-permute-start.1 = (f32[256,512]{1,0:T(8,128)S(1)}, f32[256,512]{1,0:T(8,128)S(1)}, u32[]{:S(2)}, u32[]{:S(2)}) collective-permute-start(f32[256,512]{1,0:T(8,128)S(1)} %slice_select_fusion.1), channel_id=1, source_target_pairs={{0,1},{1,0},{2,3},{3,2},{4,5},{5,4},{6,7},{7,6},{8,9},{9,8},{10,11... | collective-permute-start | bytes 1572872 | tf_op jit(solution)/shard_map/ppermute | solution.py:19
  79.7 4.9 %collective-permute-start.2 = (f32[256,512]{1,0:T(8,128)S(1)}, f32[256,512]{1,0:T(8,128)S(1)}, u32[]{:S(2)}, u32[]{:S(2)}) collective-permute-start(f32[256,512]{1,0:T(8,128)S(1)} %bitcast.47), channel_id=1, source_target_pairs={{0,1},{1,0},{2,3},{3,2},{4,5},{5,4},{6,7},{7,6},{8,9},{9,8},{10,11... | collective-permute-start | bytes 1572872 | tf_op jit(solution)/shard_map/ppermute | solution.py:19
  116.6 15.0 %collective-permute-start.3 = (f32[512,256]{1,0:T(8,128)S(1)}, f32[512,256]{1,0:T(8,128)S(1)}, u32[]{:S(2)}, u32[]{:S(2)}) collective-permute-start(f32[512,256]{1,0:T(8,128)S(1)} %slice_select_fusion), channel_id=1, source_target_pairs={{0,16},{16,32},{32,48},{48,64},{64,80},{80,96},{96,112},{112,128},... | collective-permute-start | bytes 1572872 | tf_op jit(solution)/shard_map/ppermute | solution.py:14
  132.6 7.2 %collective-permute-start.4 = (f32[512,256]{1,0:T(8,128)S(1)}, f32[512,256]{1,0:T(8,128)S(1)}, u32[]{:S(2)}, u32[]{:S(2)}) collective-permute-start(f32[512,256]{1,0:T(8,128)S(1)} %convolution_select_fusion.3), channel_id=1, source_target_pairs={{0,1},{1,0},{2,3},{3,2},{4,5},{5,4},{6,7},{7,6},{8,9},{9,8},{10,11... | collective-permute-start | bytes 1572872 | tf_op jit(solution)/shard_map/ppermute | solution.py:19
  134.1 16.9 %collective-permute-start.5 = (f32[512,256]{1,0:T(8,128)S(1)}, f32[512,256]{1,0:T(8,128)S(1)}, u32[]{:S(2)}, u32[]{:S(2)}) collective-permute-start(f32[512,256]{1,0:T(8,128)S(1)} %convolution_select_fusion.3), channel_id=1, source_target_pairs={{0,32},{16,48},{32,64},{48,80},{64,96},{80,112},{96,128},{112,144}... | collective-permute-start | bytes 1572872 | tf_op jit(solution)/shard_map/ppermute | solution.py:14
  151.9 10.3 %collective-permute-start.6 = (f32[512,256]{1,0:T(8,128)S(1)}, f32[512,256]{1,0:T(8,128)S(1)}, u32[]{:S(2)}, u32[]{:S(2)}) collective-permute-start(f32[512,256]{1,0:T(8,128)S(1)} %convolution_select_fusion.2), channel_id=1, source_target_pairs={{0,1},{1,0},{2,3},{3,2},{4,5},{5,4},{6,7},{7,6},{8,9},{9,8},{10,11... | collective-permute-start | bytes 1572872 | tf_op jit(solution)/shard_map/ppermute | solution.py:19
  152.9 20.5 %collective-permute-start.7 = (f32[512,256]{1,0:T(8,128)S(1)}, f32[512,256]{1,0:T(8,128)S(1)}, u32[]{:S(2)}, u32[]{:S(2)}) collective-permute-start(f32[512,256]{1,0:T(8,128)S(1)} %convolution_select_fusion.2), channel_id=1, source_target_pairs={{0,64},{16,80},{32,96},{48,112},{64,128},{80,144},{96,160},{112,17... | collective-permute-start | bytes 1572872 | tf_op jit(solution)/shard_map/ppermute | solution.py:14
  174.4 6.7 %collective-permute-start.8 = (f32[512,256]{1,0:T(8,128)S(1)}, f32[512,256]{1,0:T(8,128)S(1)}, u32[]{:S(2)}, u32[]{:S(2)}) collective-permute-start(f32[512,256]{1,0:T(8,128)S(1)} %convolution_select_fusion.1), channel_id=1, source_target_pairs={{0,1},{1,0},{2,3},{3,2},{4,5},{5,4},{6,7},{7,6},{8,9},{9,8},{10,11... | collective-permute-start | bytes 1572872 | tf_op jit(solution)/shard_map/ppermute | solution.py:19
  175.4 17.0 %collective-permute-start.9 = (f32[512,256]{1,0:T(8,128)S(1)}, f32[512,256]{1,0:T(8,128)S(1)}, u32[]{:S(2)}, u32[]{:S(2)}) collective-permute-start(f32[512,256]{1,0:T(8,128)S(1)} %convolution_select_fusion.1), channel_id=1, source_target_pairs={{0,128},{16,144},{32,160},{48,176},{64,192},{80,208},{96,224},{112... | collective-permute-start | bytes 1572872 | tf_op jit(solution)/shard_map/ppermute | solution.py:14
  193.4 2.1 %collective-permute-start.10 = (bf16[512,256]{1,0:T(8,128)(2,1)S(1)}, bf16[512,256]{1,0:T(8,128)(2,1)S(1)}, u32[]{:S(2)}, u32[]{:S(2)}) collective-permute-start(bf16[512,256]{1,0:T(8,128)(2,1)S(1)} %fusion.4), channel_id=1, source_target_pairs={{0,1},{1,0},{2,3},{3,2},{4,5},{5,4},{6,7},{7,6},{8,9},{9,8},{10,11... | collective-permute-start | bytes 786440 | tf_op jit(solution)/shard_map/ppermute | solution.py:19

commit v6 on v5

--- a/solution.py
+++ b/solution.py
@@ -100,11 +100,15 @@
     row_index = lax.axis_index("z") * lax.axis_size("core") + core
     positions = anchor_rows - row_index * own_rows.shape[0]
     own_slab = jnp.take(own_rows, positions, axis=0)
-    previous_slab = shifted(own_slab, "ver", 1)
-    partial_gram = lax.dot_general(
-        own_slab, previous_slab, (((0,), (0,)), ((), ())), preferred_element_type=jnp.float32
-    )
-    cross_gram = summed_over(partial_gram, "z", core)
+    half = width // 2
+    column_grams = []
+    for start in (0, half):
+        previous_columns = shifted(own_slab[:, start : start + half], "ver", 1)
+        partial_gram = lax.dot_general(
+            own_slab, previous_columns, (((0,), (0,)), ((), ())), preferred_element_type=jnp.float32
+        )
+        column_grams.append(summed_over(partial_gram, "z", core))
+    cross_gram = jnp.concatenate(column_grams, axis=1)
     frobenius = jnp.sqrt(jnp.sum(cross_gram * cross_gram) + 1e-06)
     iterate = cross_gram / frobenius
     iterate = lax.fori_loop(0, ROUGH_ITERS, newton_update(lax.Precision.HIGH), iterate)

time: 202 us -> 222 us (1.099)
  blocking collectives: 42.2 us -> 0 us
  waiting for transfers between devices: 70.4 us -> 104 us
  starting transfers between devices: 38.2 us -> 63.9 us
    all_to_all x0 -> x4, waiting for transfers between devices: none -> 44.2 us  [the longest x2 23.7 us: summed_over(): reduced = lax.all_to_all(pieces, axis, 0, 0, tiled=False).sum(0)]
    all_to_all x2 -> x0, blocking collectives: 42.2 us -> none  [the longest x1 24.7 us: summed_over(): reduced = lax.all_to_all(pieces, axis, 0, 0, tiled=False).sum(0)]
    all_to_all x0 -> x4, starting transfers between devices: none -> 18.4 us  [the longest x2 11.6 us: summed_over(): reduced = lax.all_to_all(pieces, axis, 0, 0, tiled=False).sum(0)]
    ppermute x5 -> x6, waiting for transfers between devices: 66.2 us -> 57.7 us  [shifted(): lax.ppermute(value, axis, [(source, source + steps) for source in range(c...]
    ppermute x6 -> x8, starting transfers between devices: 9.34 us -> 13.5 us  [swapped(): lax.ppermute(value, axis, [(source, source ^ mask) for source in range(co...]
    ppermute x5 -> x6, starting transfers between devices: 28.9 us -> 31.9 us  [shifted(): lax.ppermute(value, axis, [(source, source + steps) for source in range(c...]
  transfers between devices with their start and end apart: 11 -> 18, of which waited for: 8 -> 12; matrix products, arithmetic and copies ran while one was open for 0% -> 1% of each run, Pallas kernels for 0% -> 0%
where the time goes in v6:
time: 222 us; the launch traced here: 221 us
  waiting for transfers between devices  104 us (47%)
  starting transfers between devices  63.9 us (29%)
  matrix products  32.9 us (15%)
  local copies, waits for them, and re-layouts  8.88 us (4%)
  other arithmetic  5.42 us (2%)
  Pallas kernels  4.74 us (2%)
    ppermute x6, waiting for transfers between devices, shifted(): lax.ppermute(value, axis, [(source, source + steps) for source in range(c...  57.7 us
    ppermute x6, starting transfers between devices, shifted(): lax.ppermute(value, axis, [(source, source + steps) for source in range(c...  31.9 us
    all_to_all x2, waiting for transfers between devices, summed_over(): reduced = lax.all_to_all(pieces, axis, 0, 0, tiled=False).sum(0)  23.7 us
    all_to_all x2, waiting for transfers between devices, summed_over(): mine = lax.all_to_all(copies, axis, 0, 0, tiled=False).reshape(mine.shape)  20.5 us
    dot_general x12, matrix products, update(): return 1.5 * iterate - 0.5 * jnp.dot(iterate, square, precision=precision)  14 us
    dot_general x12, matrix products, update(): square = jnp.dot(iterate.T, iterate, precision=precision)  14 us
    ppermute x8, starting transfers between devices, swapped(): lax.ppermute(value, axis, [(source, source ^ mask) for source in range(co...  13.5 us
    all_to_all x2, starting transfers between devices, summed_over(): reduced = lax.all_to_all(pieces, axis, 0, 0, tiled=False).sum(0)  11.6 us
  transfers between devices with their start and end apart: 18, of which 12 were waited for; matrix products, arithmetic and copies ran while one was open for 1% of the time, Pallas kernels for 0%

profile of v6, /device:TPU:1, one launch (start us, length us, event | category | flops | bytes accessed | tf_op | source)
XLA Modules:
  0.0 221.5 jit_solution(4376717466050427546)
XLA Ops:
  1.4 5.8 %gather_fusion = bf16[1024,512]{1,0:T(8,128)(2,1)S(1)} fusion(bf16[2048,512]{1,0:T(8,128)(2,1)} %bitcast.50, s32[1024]{0:T(1024)S(1)} %fusion.24), kind=kCustom, calls=%fused_computation | custom fusion | bytes 2101248 | tf_op jit(solution)/shard_map/jit(_take)/gather | solution.py:102
  7.5 4.0 %collective-permute-start = (bf16[1024,256]{1,0:T(8,128)(2,1)S(1)}, bf16[1024,256]{1,0:T(8,128)(2,1)S(1)}, u32[]{:S(2)}, u32[]{:S(2)}) collective-permute-start(bf16[1024,256]{1,0:T(8,128)(2,1)S(1)} %get-tuple-element.41), channel_id=1, source_target_pairs={{0,16},{16,32},{32,48},{48,64},{64,80},{80,96},{96,112},{112,128},... | collective-permute-start | bytes 1572872 | tf_op jit(solution)/shard_map/ppermute | solution.py:14
  11.5 3.1 %collective-permute-start.3 = (bf16[1024,256]{1,0:T(8,128)(2,1)S(1)}, bf16[1024,256]{1,0:T(8,128)(2,1)S(1)}, u32[]{:S(2)}, u32[]{:S(2)}) collective-permute-start(bf16[1024,256]{1,0:T(8,128)(2,1)S(1)} %get-tuple-element.42), channel_id=1, source_target_pairs={{0,16},{16,32},{32,48},{48,64},{64,80},{80,96},{96,112},{112,128},... | collective-permute-start | bytes 1572872 | tf_op jit(solution)/shard_map/ppermute | solution.py:14
  14.6 7.4 %collective-permute-done = bf16[1024,256]{1,0:T(8,128)(2,1)S(1)} collective-permute-done((bf16[1024,256]{1,0:T(8,128)(2,1)S(1)}, bf16[1024,256]{1,0:T(8,128)(2,1)S(1)}, u32[]{:S(2)}, u32[]{:S(2)}) %collective-permute-start) | collective-permute-done | bytes 524320 | tf_op jit(solution)/shard_map/ppermute | solution.py:14
  25.3 8.0 %collective-permute-done.3 = bf16[1024,256]{1,0:T(8,128)(2,1)S(1)} collective-permute-done((bf16[1024,256]{1,0:T(8,128)(2,1)S(1)}, bf16[1024,256]{1,0:T(8,128)(2,1)S(1)}, u32[]{:S(2)}, u32[]{:S(2)}) %collective-permute-start.3) | collective-permute-done | bytes 524320 | tf_op jit(solution)/shard_map/ppermute | solution.py:14
  36.2 8.2 %all-to-all-start = ((f32[8,32,256]{2,1,0:T(8,128)}), f32[8,32,256]{2,1,0:T(8,128)S(1)}, u32[]{:S(2)}, u32[]{:S(2)}) async-start(f32[8,32,256]{2,1,0:T(8,128)} %bitcast.3), calls=%async_computation | async-start | bytes 524288 | tf_op jit(solution)/shard_map/all_to_all | solution.py:36
  45.1 11.6 %all-to-all-done = f32[8,32,256]{2,1,0:T(8,128)S(1)} async-done(((f32[8,32,256]{2,1,0:T(8,128)}), f32[8,32,256]{2,1,0:T(8,128)S(1)}, u32[]{:S(2)}, u32[]{:S(2)}) %all-to-all-start) | async-done | bytes 262176 | tf_op jit(solution)/shard_map/all_to_all | solution.py:36
  56.7 3.4 %all-to-all-start.2 = ((f32[8,32,256]{2,1,0:T(8,128)}), f32[8,32,256]{2,1,0:T(8,128)S(1)}, u32[]{:S(2)}, u32[]{:S(2)}) async-start(f32[8,32,256]{2,1,0:T(8,128)} %bitcast.5), calls=%async_computation.2 | async-start | bytes 524288 | tf_op jit(solution)/shard_map/all_to_all | solution.py:36
  60.2 12.1 %all-to-all-done.2 = f32[8,32,256]{2,1,0:T(8,128)S(1)} async-done(((f32[8,32,256]{2,1,0:T(8,128)}), f32[8,32,256]{2,1,0:T(8,128)S(1)}, u32[]{:S(2)}, u32[]{:S(2)}) %all-to-all-start.2) | async-done | bytes 262176 | tf_op jit(solution)/shard_map/all_to_all | solution.py:36
  73.0 3.4 %all-to-all-start.1 = ((f32[8,32,256]{2,1,0:T(8,128)}), f32[8,32,256]{2,1,0:T(8,128)S(1)}, u32[]{:S(2)}, u32[]{:S(2)}) async-start(f32[8,32,256]{2,1,0:T(8,128)} %broadcast_in_dim.27), calls=%async_computation.1 | async-start | bytes 524288 | tf_op jit(solution)/shard_map/all_to_all | solution.py:38
  76.5 11.5 %all-to-all-done.1 = f32[8,32,256]{2,1,0:T(8,128)S(1)} async-done(((f32[8,32,256]{2,1,0:T(8,128)}), f32[8,32,256]{2,1,0:T(8,128)S(1)}, u32[]{:S(2)}, u32[]{:S(2)}) %all-to-all-start.1) | async-done | bytes 262176 | tf_op jit(solution)/shard_map/all_to_all | solution.py:38
  88.7 3.4 %all-to-all-start.3 = ((f32[8,32,256]{2,1,0:T(8,128)}), f32[8,32,256]{2,1,0:T(8,128)S(1)}, u32[]{:S(2)}, u32[]{:S(2)}) async-start(f32[8,32,256]{2,1,0:T(8,128)} %broadcast_in_dim.28), calls=%async_computation.3 | async-start | bytes 524288 | tf_op jit(solution)/shard_map/all_to_all | solution.py:38
  93.4 8.9 %all-to-all-done.3 = f32[8,32,256]{2,1,0:T(8,128)S(1)} async-done(((f32[8,32,256]{2,1,0:T(8,128)}), f32[8,32,256]{2,1,0:T(8,128)S(1)}, u32[]{:S(2)}, u32[]{:S(2)}) %all-to-all-start.3) | async-done | bytes 262176 | tf_op jit(solution)/shard_map/all_to_all | solution.py:38
  108.2 21.6 %while.20 = (s32[]{:T(128)}, f32[512,512]{0,1:T(8,128)S(1)}, s32[]{:T(128)}) while((s32[]{:T(128)}, f32[512,512]{0,1:T(8,128)S(1)}, s32[]{:T(128)}) %tuple.33), condition=%wide.region_4.5_spmd, body=%wide.region_3.4_spmd.sunk | while | flops 1611399168 | bytes 7340077 | solution.py:114
  129.8 7.6 %while.21 = (s32[]{:T(128)}, f32[512,512]{0,1:T(8,128)S(1)}, s32[]{:T(128)}) while((s32[]{:T(128)}, f32[512,512]{0,1:T(8,128)S(1)}, s32[]{:T(128)}) %tuple.36), condition=%wide.region_6.7_spmd, body=%wide.region_5.6_spmd.sunk | while | flops 3222011904 | bytes 7340077 | solution.py:115
  138.0 4.1 %collective-permute-start.6 = (f32[512,256]{1,0:T(8,128)S(1)}, f32[512,256]{1,0:T(8,128)S(1)}, u32[]{:S(2)}, u32[]{:S(2)}) collective-permute-start(f32[512,256]{1,0:T(8,128)S(1)} %slice_select_fusion), channel_id=1, source_target_pairs={{0,16},{16,32},{32,48},{48,64},{64,80},{80,96},{96,112},{112,128},... | collective-permute-start | bytes 1572872 | tf_op jit(solution)/shard_map/ppermute | solution.py:14
  142.2 10.9 %collective-permute-done.6 = f32[512,256]{1,0:T(8,128)S(1)} collective-permute-done((f32[512,256]{1,0:T(8,128)S(1)}, f32[512,256]{1,0:T(8,128)S(1)}, u32[]{:S(2)}, u32[]{:S(2)}) %collective-permute-start.6) | collective-permute-done | bytes 524320 | tf_op jit(solution)/shard_map/ppermute | solution.py:14
  155.3 5.7 %collective-permute-start.8 = (f32[512,256]{1,0:T(8,128)S(1)}, f32[512,256]{1,0:T(8,128)S(1)}, u32[]{:S(2)}, u32[]{:S(2)}) collective-permute-start(f32[512,256]{1,0:T(8,128)S(1)} %convolution_select_fusion.3), channel_id=1, source_target_pairs={{0,32},{16,48},{32,64},{48,80},{64,96},{80,112},{96,128},{112,144}... | collective-permute-start | bytes 1572872 | tf_op jit(solution)/shard_map/ppermute | solution.py:14
  161.0 11.2 %collective-permute-done.8 = f32[512,256]{1,0:T(8,128)S(1)} collective-permute-done((f32[512,256]{1,0:T(8,128)S(1)}, f32[512,256]{1,0:T(8,128)S(1)}, u32[]{:S(2)}, u32[]{:S(2)}) %collective-permute-start.8) | collective-permute-done | bytes 524320 | tf_op jit(solution)/shard_map/ppermute | solution.py:14
  173.2 9.3 %collective-permute-start.10 = (f32[512,256]{1,0:T(8,128)S(1)}, f32[512,256]{1,0:T(8,128)S(1)}, u32[]{:S(2)}, u32[]{:S(2)}) collective-permute-start(f32[512,256]{1,0:T(8,128)S(1)} %convolution_select_fusion.2), channel_id=1, source_target_pairs={{0,64},{16,80},{32,96},{48,112},{64,128},{80,144},{96,160},{112,17... | collective-permute-start | bytes 1572872 | tf_op jit(solution)/shard_map/ppermute | solution.py:14
  183.8 9.1 %collective-permute-done.10 = f32[512,256]{1,0:T(8,128)S(1)} collective-permute-done((f32[512,256]{1,0:T(8,128)S(1)}, f32[512,256]{1,0:T(8,128)S(1)}, u32[]{:S(2)}, u32[]{:S(2)}) %collective-permute-start.10) | collective-permute-done | bytes 524320 | tf_op jit(solution)/shard_map/ppermute | solution.py:14
  195.7 5.7 %collective-permute-start.12 = (f32[512,256]{1,0:T(8,128)S(1)}, f32[512,256]{1,0:T(8,128)S(1)}, u32[]{:S(2)}, u32[]{:S(2)}) collective-permute-start(f32[512,256]{1,0:T(8,128)S(1)} %convolution_select_fusion.1), channel_id=1, source_target_pairs={{0,128},{16,144},{32,160},{48,176},{64,192},{80,208},{96,224},{112... | collective-permute-start | bytes 1572872 | tf_op jit(solution)/shard_map/ppermute | solution.py:14
  201.5 11.2 %collective-permute-done.12 = f32[512,256]{1,0:T(8,128)S(1)} collective-permute-done((f32[512,256]{1,0:T(8,128)S(1)}, f32[512,256]{1,0:T(8,128)S(1)}, u32[]{:S(2)}, u32[]{:S(2)}) %collective-permute-start.12) | collective-permute-done | bytes 524320 | tf_op jit(solution)/shard_map/ppermute | solution.py:14
  216.7 4.7 %shard_map.28 = bf16[1,2048,512]{2,1,0:T(8,128)(2,1)} custom-call(bf16[1,2048,512]{2,1,0:T(8,128)(2,1)} %rows_ref.1, bf16[512,512]{1,0:T(8,128)(2,1)} %maximum_select_fusion.8.prefix_ref), custom_call_target="tpu_custom_call" | custom-call | tf_op jit(solution)/shard_map/pallas_call | solution.py:84
  (79 shorter events, 57.2 us)
Async XLA Ops:
  7.5 14.5 %collective-permute-start = (bf16[1024,256]{1,0:T(8,128)(2,1)S(1)}, bf16[1024,256]{1,0:T(8,128)(2,1)S(1)}, u32[]{:S(2)}, u32[]{:S(2)}) collective-permute-start(bf16[1024,256]{1,0:T(8,128)(2,1)S(1)} %get-tuple-element.41), channel_id=1, source_target_pairs={{0,16},{16,32},{32,48},{48,64},{64,80},{80,96},{96,112},{112,128},... | collective-permute-start | bytes 1572872 | tf_op jit(solution)/shard_map/ppermute | solution.py:14
  11.5 21.8 %collective-permute-start.3 = (bf16[1024,256]{1,0:T(8,128)(2,1)S(1)}, bf16[1024,256]{1,0:T(8,128)(2,1)S(1)}, u32[]{:S(2)}, u32[]{:S(2)}) collective-permute-start(bf16[1024,256]{1,0:T(8,128)(2,1)S(1)} %get-tuple-element.42), channel_id=1, source_target_pairs={{0,16},{16,32},{32,48},{48,64},{64,80},{80,96},{96,112},{112,128},... | collective-permute-start | bytes 1572872 | tf_op jit(solution)/shard_map/ppermute | solution.py:14
  22.6 12.9 %collective-permute-start.1 = (f32[256,256]{1,0:T(8,128)S(1)}, f32[256,256]{1,0:T(8,128)S(1)}, u32[]{:S(2)}, u32[]{:S(2)}) collective-permute-start(f32[256,256]{1,0:T(8,128)S(1)} %slice_select_fusion.2), channel_id=1, source_target_pairs={{0,1},{1,0},{2,3},{3,2},{4,5},{5,4},{6,7},{7,6},{8,9},{9,8},{10,11... | collective-permute-start | bytes 786440 | tf_op jit(solution)/shard_map/ppermute | solution.py:19
  33.8 10.6 %collective-permute-start.4 = (f32[256,256]{1,0:T(8,128)S(1)}, f32[256,256]{1,0:T(8,128)S(1)}, u32[]{:S(2)}, u32[]{:S(2)}) collective-permute-start(f32[256,256]{1,0:T(8,128)S(1)} %slice_select_fusion.1), channel_id=1, source_target_pairs={{0,1},{1,0},{2,3},{3,2},{4,5},{5,4},{6,7},{7,6},{8,9},{9,8},{10,11... | collective-permute-start | bytes 786440 | tf_op jit(solution)/shard_map/ppermute | solution.py:19
  36.2 20.6 %all-to-all-start = ((f32[8,32,256]{2,1,0:T(8,128)}), f32[8,32,256]{2,1,0:T(8,128)S(1)}, u32[]{:S(2)}, u32[]{:S(2)}) async-start(f32[8,32,256]{2,1,0:T(8,128)} %bitcast.3), calls=%async_computation | async-start | bytes 524288 | tf_op jit(solution)/shard_map/all_to_all | solution.py:36
  56.7 15.6 %all-to-all-start.2 = ((f32[8,32,256]{2,1,0:T(8,128)}), f32[8,32,256]{2,1,0:T(8,128)S(1)}, u32[]{:S(2)}, u32[]{:S(2)}) async-start(f32[8,32,256]{2,1,0:T(8,128)} %bitcast.5), calls=%async_computation.2 | async-start | bytes 524288 | tf_op jit(solution)/shard_map/all_to_all | solution.py:36
  73.0 15.0 %all-to-all-start.1 = ((f32[8,32,256]{2,1,0:T(8,128)}), f32[8,32,256]{2,1,0:T(8,128)S(1)}, u32[]{:S(2)}, u32[]{:S(2)}) async-start(f32[8,32,256]{2,1,0:T(8,128)} %broadcast_in_dim.27), calls=%async_computation.1 | async-start | bytes 524288 | tf_op jit(solution)/shard_map/all_to_all | solution.py:38
  88.7 13.6 %all-to-all-start.3 = ((f32[8,32,256]{2,1,0:T(8,128)}), f32[8,32,256]{2,1,0:T(8,128)S(1)}, u32[]{:S(2)}, u32[]{:S(2)}) async-start(f32[8,32,256]{2,1,0:T(8,128)} %broadcast_in_dim.28), calls=%async_computation.3 | async-start | bytes 524288 | tf_op jit(solution)/shard_map/all_to_all | solution.py:38
  92.2 12.7 %collective-permute-start.2 = (f32[256,256]{1,0:T(8,128)S(1)}, f32[256,256]{1,0:T(8,128)S(1)}, u32[]{:S(2)}, u32[]{:S(2)}) collective-permute-start(f32[256,256]{1,0:T(8,128)S(1)} %bitcast.51), channel_id=1, source_target_pairs={{0,1},{1,0},{2,3},{3,2},{4,5},{5,4},{6,7},{7,6},{8,9},{9,8},{10,11... | collective-permute-start | bytes 786440 | tf_op jit(solution)/shard_map/ppermute | solution.py:19
  102.4 3.7 %collective-permute-start.5 = (f32[256,256]{1,0:T(8,128)S(1)}, f32[256,256]{1,0:T(8,128)S(1)}, u32[]{:S(2)}, u32[]{:S(2)}) collective-permute-start(f32[256,256]{1,0:T(8,128)S(1)} %bitcast.53), channel_id=1, source_target_pairs={{0,1},{1,0},{2,3},{3,2},{4,5},{5,4},{6,7},{7,6},{8,9},{9,8},{10,11... | collective-permute-start | bytes 786440 | tf_op jit(solution)/shard_map/ppermute | solution.py:19
  138.0 15.0 %collective-permute-start.6 = (f32[512,256]{1,0:T(8,128)S(1)}, f32[512,256]{1,0:T(8,128)S(1)}, u32[]{:S(2)}, u32[]{:S(2)}) collective-permute-start(f32[512,256]{1,0:T(8,128)S(1)} %slice_select_fusion), channel_id=1, source_target_pairs={{0,16},{16,32},{32,48},{48,64},{64,80},{80,96},{96,112},{112,128},... | collective-permute-start | bytes 1572872 | tf_op jit(solution)/shard_map/ppermute | solution.py:14
  154.0 7.0 %collective-permute-start.7 = (f32[512,256]{1,0:T(8,128)S(1)}, f32[512,256]{1,0:T(8,128)S(1)}, u32[]{:S(2)}, u32[]{:S(2)}) collective-permute-start(f32[512,256]{1,0:T(8,128)S(1)} %convolution_select_fusion.3), channel_id=1, source_target_pairs={{0,1},{1,0},{2,3},{3,2},{4,5},{5,4},{6,7},{7,6},{8,9},{9,8},{10,11... | collective-permute-start | bytes 1572872 | tf_op jit(solution)/shard_map/ppermute | solution.py:19
  155.3 16.9 %collective-permute-start.8 = (f32[512,256]{1,0:T(8,128)S(1)}, f32[512,256]{1,0:T(8,128)S(1)}, u32[]{:S(2)}, u32[]{:S(2)}) collective-permute-start(f32[512,256]{1,0:T(8,128)S(1)} %convolution_select_fusion.3), channel_id=1, source_target_pairs={{0,32},{16,48},{32,64},{48,80},{64,96},{80,112},{96,128},{112,144}... | collective-permute-start | bytes 1572872 | tf_op jit(solution)/shard_map/ppermute | solution.py:14
  173.2 19.7 %collective-permute-start.10 = (f32[512,256]{1,0:T(8,128)S(1)}, f32[512,256]{1,0:T(8,128)S(1)}, u32[]{:S(2)}, u32[]{:S(2)}) collective-permute-start(f32[512,256]{1,0:T(8,128)S(1)} %convolution_select_fusion.2), channel_id=1, source_target_pairs={{0,64},{16,80},{32,96},{48,112},{64,128},{80,144},{96,160},{112,17... | collective-permute-start | bytes 1572872 | tf_op jit(solution)/shard_map/ppermute | solution.py:14
  182.5 10.4 %collective-permute-start.9 = (f32[512,256]{1,0:T(8,128)S(1)}, f32[512,256]{1,0:T(8,128)S(1)}, u32[]{:S(2)}, u32[]{:S(2)}) collective-permute-start(f32[512,256]{1,0:T(8,128)S(1)} %convolution_select_fusion.2), channel_id=1, source_target_pairs={{0,1},{1,0},{2,3},{3,2},{4,5},{5,4},{6,7},{7,6},{8,9},{9,8},{10,11... | collective-permute-start | bytes 1572872 | tf_op jit(solution)/shard_map/ppermute | solution.py:19
  193.9 7.6 %collective-permute-start.11 = (f32[512,256]{1,0:T(8,128)S(1)}, f32[512,256]{1,0:T(8,128)S(1)}, u32[]{:S(2)}, u32[]{:S(2)}) collective-permute-start(f32[512,256]{1,0:T(8,128)S(1)} %convolution_select_fusion.1), channel_id=1, source_target_pairs={{0,1},{1,0},{2,3},{3,2},{4,5},{5,4},{6,7},{7,6},{8,9},{9,8},{10,11... | collective-permute-start | bytes 1572872 | tf_op jit(solution)/shard_map/ppermute | solution.py:19
  195.7 16.9 %collective-permute-start.12 = (f32[512,256]{1,0:T(8,128)S(1)}, f32[512,256]{1,0:T(8,128)S(1)}, u32[]{:S(2)}, u32[]{:S(2)}) collective-permute-start(f32[512,256]{1,0:T(8,128)S(1)} %convolution_select_fusion.1), channel_id=1, source_target_pairs={{0,128},{16,144},{32,160},{48,176},{64,192},{80,208},{96,224},{112... | collective-permute-start | bytes 1572872 | tf_op jit(solution)/shard_map/ppermute | solution.py:14
  213.7 2.1 collective-permute-start.13

commit v7 on v5

--- a/solution.py
+++ b/solution.py
@@ -99,7 +99,10 @@
     core = lax.axis_index("core")
     row_index = lax.axis_index("z") * lax.axis_size("core") + core
     positions = anchor_rows - row_index * own_rows.shape[0]
-    own_slab = jnp.take(own_rows, positions, axis=0)
+    picks = (positions[:, None] == jnp.arange(own_rows.shape[0], dtype=positions.dtype)[None, :])
+    own_slab = jnp.dot(
+        picks.astype(own_rows.dtype), own_rows, preferred_element_type=jnp.float32
+    ).astype(own_rows.dtype)
     previous_slab = shifted(own_slab, "ver", 1)
     partial_gram = lax.dot_general(
         own_slab, previous_slab, (((0,), (0,)), ((), ())), preferred_element_type=jnp.float32

time: 202 us -> 199 us (0.985)
  local copies, waits for them, and re-layouts: 7.41 us -> 1.56 us
  matrix products: 32.7 us -> 36.6 us
    gather x1 -> x0, local copies, waits for them, and re-layouts: 5.85 us -> none  [per_device(): own_slab = jnp.take(own_rows, positions, axis=0)]
    dot_general x0 -> x1, matrix products: none -> 3.96 us  [per_device(): jnp.dot(picks.astype(own_rows.dtype), own_rows, preferred_element_type=jn...]
where the time goes in v7:
time: 199 us; the launch traced here: 198 us
  waiting for transfers between devices  70.4 us (35%)
  blocking collectives  42.2 us (21%)
  starting transfers between devices  38 us (19%)
  matrix products  36.6 us (18%)
  Pallas kernels  4.74 us (2%)
  other arithmetic  3.18 us (2%)
    ppermute x5, waiting for transfers between devices, shifted(): lax.ppermute(value, axis, [(source, source + steps) for source in range(c...  66.2 us
    ppermute x5, starting transfers between devices, shifted(): lax.ppermute(value, axis, [(source, source + steps) for source in range(c...  28.8 us
    all_to_all x1, blocking collectives, summed_over(): reduced = lax.all_to_all(pieces, axis, 0, 0, tiled=False).sum(0)  24.7 us
    all_to_all x1, blocking collectives, summed_over(): mine = lax.all_to_all(copies, axis, 0, 0, tiled=False).reshape(mine.shape)  17.5 us
    dot_general x12, matrix products, update(): return 1.5 * iterate - 0.5 * jnp.dot(iterate, square, precision=precision)  14 us
    dot_general x12, matrix products, update(): square = jnp.dot(iterate.T, iterate, precision=precision)  14 us
    ppermute x6, starting transfers between devices, swapped(): lax.ppermute(value, axis, [(source, source ^ mask) for source in range(co...  9.16 us
    pallas_call x1, Pallas kernels, aligned_rows(): pl.pallas_call(aligned_block, grid=(rows // block,), in_specs=[pl.BlockSp...  4.74 us
  transfers between devices with their start and end apart: 11, of which 8 were waited for; matrix products, arithmetic and copies ran while one was open for 0% of the time, Pallas kernels for 0%

profile of v7, /device:TPU:1, one launch (start us, length us, event | category | flops | bytes accessed | tf_op | source)
XLA Modules:
  0.0 198.2 jit_solution(16011157676132716012)
XLA Ops:
  0.7 4.0 %fusion.7 = bf16[1024,512]{1,0:T(8,128)(2,1)S(1)} fusion(bf16[1,2048,512]{2,1,0:T(8,128)(2,1)} %rows_ref.1, s32[1024]{0:T(1024)S(1)} %broadcast_subtract_fusion), kind=kOutput, calls=%fused_computation.10 | convolution fusion | flops 2150105088 | bytes 3149824 | tf_op jit(solution)/shard_map/dot_general | solution.py:103
  4.7 4.0 %collective-permute-start = (bf16[1024,512]{1,0:T(8,128)(2,1)S(1)}, bf16[1024,512]{1,0:T(8,128)(2,1)S(1)}, u32[]{:S(2)}, u32[]{:S(2)}) collective-permute-start(bf16[1024,512]{1,0:T(8,128)(2,1)S(1)} %fusion.7), channel_id=1, source_target_pairs={{0,16},{16,32},{32,48},{48,64},{64,80},{80,96},{96,112},{112,128},... | collective-permute-start | bytes 3145736 | tf_op jit(solution)/shard_map/ppermute | solution.py:14
  8.7 21.8 %collective-permute-done = bf16[1024,512]{1,0:T(8,128)(2,1)S(1)} collective-permute-done((bf16[1024,512]{1,0:T(8,128)(2,1)S(1)}, bf16[1024,512]{1,0:T(8,128)(2,1)S(1)}, u32[]{:S(2)}, u32[]{:S(2)}) %collective-permute-start) | collective-permute-done | bytes 1048608 | tf_op jit(solution)/shard_map/ppermute | solution.py:14
  31.2 1.6 collective-permute-start.1
  32.9 1.5 collective-permute-done.1
  34.5 24.7 %all_to_all.10 = f32[8,32,512]{2,1,0:T(8,128)S(1)} all-to-all(f32[8,32,512]{2,1,0:T(8,128)S(1)} %bitcast.53), channel_id=1, replica_groups=mesh['ver'=16,'z'=8,'core'=2] {'z'}, dimensions={0} | all-to-all | bytes 1048576 | tf_op jit(solution)/shard_map/all_to_all | solution.py:36
  59.4 17.5 %all_to_all.11 = f32[8,32,512]{2,1,0:T(8,128)S(1)} all-to-all(f32[8,32,512]{2,1,0:T(8,128)S(1)} %broadcast_in_dim.2), channel_id=1, replica_groups=mesh['ver'=16,'z'=8,'core'=2] {'z'}, dimensions={0} | all-to-all | bytes 1048576 | tf_op jit(solution)/shard_map/all_to_all | solution.py:38
  76.9 3.3 %collective-permute-start.2 = (f32[256,512]{1,0:T(8,128)S(1)}, f32[256,512]{1,0:T(8,128)S(1)}, u32[]{:S(2)}, u32[]{:S(2)}) collective-permute-start(f32[256,512]{1,0:T(8,128)S(1)} %bitcast.50), channel_id=1, source_target_pairs={{0,1},{1,0},{2,3},{3,2},{4,5},{5,4},{6,7},{7,6},{8,9},{9,8},{10,11... | collective-permute-start | bytes 1572872 | tf_op jit(solution)/shard_map/ppermute | solution.py:19
  80.2 1.5 collective-permute-done.2
  83.9 21.6 %while.20 = (s32[]{:T(128)}, f32[512,512]{0,1:T(8,128)S(1)}, s32[]{:T(128)}) while((s32[]{:T(128)}, f32[512,512]{0,1:T(8,128)S(1)}, s32[]{:T(128)}) %tuple.32), condition=%wide.region_3.4_spmd, body=%wide.region_2.3_spmd.sunk | while | flops 1611399168 | bytes 7340077 | solution.py:113
  105.6 7.6 %while.21 = (s32[]{:T(128)}, f32[512,512]{0,1:T(8,128)S(1)}, s32[]{:T(128)}) while((s32[]{:T(128)}, f32[512,512]{0,1:T(8,128)S(1)}, s32[]{:T(128)}) %tuple.35), condition=%wide.region_5.6_spmd, body=%wide.region_4.5_spmd.sunk | while | flops 3222011904 | bytes 7340077 | solution.py:114
  105.7 1.9 fusion.73
  107.6 1.9 fusion.74
  109.5 1.9 fusion.73
  111.4 1.9 fusion.74
  113.8 4.2 %collective-permute-start.3 = (f32[512,256]{1,0:T(8,128)S(1)}, f32[512,256]{1,0:T(8,128)S(1)}, u32[]{:S(2)}, u32[]{:S(2)}) collective-permute-start(f32[512,256]{1,0:T(8,128)S(1)} %slice_select_fusion), channel_id=1, source_target_pairs={{0,16},{16,32},{32,48},{48,64},{64,80},{80,96},{96,112},{112,128},... | collective-permute-start | bytes 1572872 | tf_op jit(solution)/shard_map/ppermute | solution.py:14
  117.9 10.9 %collective-permute-done.3 = f32[512,256]{1,0:T(8,128)S(1)} collective-permute-done((f32[512,256]{1,0:T(8,128)S(1)}, f32[512,256]{1,0:T(8,128)S(1)}, u32[]{:S(2)}, u32[]{:S(2)}) %collective-permute-start.3) | collective-permute-done | bytes 524320 | tf_op jit(solution)/shard_map/ppermute | solution.py:14
  131.1 5.6 %collective-permute-start.5 = (f32[512,256]{1,0:T(8,128)S(1)}, f32[512,256]{1,0:T(8,128)S(1)}, u32[]{:S(2)}, u32[]{:S(2)}) collective-permute-start(f32[512,256]{1,0:T(8,128)S(1)} %convolution_select_fusion.3), channel_id=1, source_target_pairs={{0,32},{16,48},{32,64},{48,80},{64,96},{80,112},{96,128},{112,144}... | collective-permute-start | bytes 1572872 | tf_op jit(solution)/shard_map/ppermute | solution.py:14
  136.8 11.2 %collective-permute-done.5 = f32[512,256]{1,0:T(8,128)S(1)} collective-permute-done((f32[512,256]{1,0:T(8,128)S(1)}, f32[512,256]{1,0:T(8,128)S(1)}, u32[]{:S(2)}, u32[]{:S(2)}) %collective-permute-start.5) | collective-permute-done | bytes 524320 | tf_op jit(solution)/shard_map/ppermute | solution.py:14
  149.9 9.3 %collective-permute-start.7 = (f32[512,256]{1,0:T(8,128)S(1)}, f32[512,256]{1,0:T(8,128)S(1)}, u32[]{:S(2)}, u32[]{:S(2)}) collective-permute-start(f32[512,256]{1,0:T(8,128)S(1)} %convolution_select_fusion.2), channel_id=1, source_target_pairs={{0,64},{16,80},{32,96},{48,112},{64,128},{80,144},{96,160},{112,17... | collective-permute-start | bytes 1572872 | tf_op jit(solution)/shard_map/ppermute | solution.py:14
  159.3 11.2 %collective-permute-done.7 = f32[512,256]{1,0:T(8,128)S(1)} collective-permute-done((f32[512,256]{1,0:T(8,128)S(1)}, f32[512,256]{1,0:T(8,128)S(1)}, u32[]{:S(2)}, u32[]{:S(2)}) %collective-permute-start.7) | collective-permute-done | bytes 524320 | tf_op jit(solution)/shard_map/ppermute | solution.py:14
  172.4 5.7 %collective-permute-start.9 = (f32[512,256]{1,0:T(8,128)S(1)}, f32[512,256]{1,0:T(8,128)S(1)}, u32[]{:S(2)}, u32[]{:S(2)}) collective-permute-start(f32[512,256]{1,0:T(8,128)S(1)} %convolution_select_fusion.1), channel_id=1, source_target_pairs={{0,128},{16,144},{32,160},{48,176},{64,192},{80,208},{96,224},{112... | collective-permute-start | bytes 1572872 | tf_op jit(solution)/shard_map/ppermute | solution.py:14
  178.2 11.2 %collective-permute-done.9 = f32[512,256]{1,0:T(8,128)S(1)} collective-permute-done((f32[512,256]{1,0:T(8,128)S(1)}, f32[512,256]{1,0:T(8,128)S(1)}, u32[]{:S(2)}, u32[]{:S(2)}) %collective-permute-start.9) | collective-permute-done | bytes 524320 | tf_op jit(solution)/shard_map/ppermute | solution.py:14
  193.4 4.7 %shard_map.28 = bf16[1,2048,512]{2,1,0:T(8,128)(2,1)} custom-call(bf16[1,2048,512]{2,1,0:T(8,128)(2,1)} %rows_ref.1, bf16[512,512]{1,0:T(8,128)(2,1)} %maximum_select_fusion.7.prefix_ref), custom_call_target="tpu_custom_call" | custom-call | tf_op jit(solution)/shard_map/pallas_call | solution.py:84
  (57 shorter events, 35.4 us)
Async XLA Ops:
  4.7 25.8 %collective-permute-start = (bf16[1024,512]{1,0:T(8,128)(2,1)S(1)}, bf16[1024,512]{1,0:T(8,128)(2,1)S(1)}, u32[]{:S(2)}, u32[]{:S(2)}) collective-permute-start(bf16[1024,512]{1,0:T(8,128)(2,1)S(1)} %fusion.7), channel_id=1, source_target_pairs={{0,16},{16,32},{32,48},{48,64},{64,80},{80,96},{96,112},{112,128},... | collective-permute-start | bytes 3145736 | tf_op jit(solution)/shard_map/ppermute | solution.py:14
  31.2 3.2 %collective-permute-start.1 = (f32[256,512]{1,0:T(8,128)S(1)}, f32[256,512]{1,0:T(8,128)S(1)}, u32[]{:S(2)}, u32[]{:S(2)}) collective-permute-start(f32[256,512]{1,0:T(8,128)S(1)} %slice_select_fusion.1), channel_id=1, source_target_pairs={{0,1},{1,0},{2,3},{3,2},{4,5},{5,4},{6,7},{7,6},{8,9},{9,8},{10,11... | collective-permute-start | bytes 1572872 | tf_op jit(solution)/shard_map/ppermute | solution.py:19
  76.9 4.9 %collective-permute-start.2 = (f32[256,512]{1,0:T(8,128)S(1)}, f32[256,512]{1,0:T(8,128)S(1)}, u32[]{:S(2)}, u32[]{:S(2)}) collective-permute-start(f32[256,512]{1,0:T(8,128)S(1)} %bitcast.50), channel_id=1, source_target_pairs={{0,1},{1,0},{2,3},{3,2},{4,5},{5,4},{6,7},{7,6},{8,9},{9,8},{10,11... | collective-permute-start | bytes 1572872 | tf_op jit(solution)/shard_map/ppermute | solution.py:19
  113.8 15.0 %collective-permute-start.3 = (f32[512,256]{1,0:T(8,128)S(1)}, f32[512,256]{1,0:T(8,128)S(1)}, u32[]{:S(2)}, u32[]{:S(2)}) collective-permute-start(f32[512,256]{1,0:T(8,128)S(1)} %slice_select_fusion), channel_id=1, source_target_pairs={{0,16},{16,32},{32,48},{48,64},{64,80},{80,96},{96,112},{112,128},... | collective-permute-start | bytes 1572872 | tf_op jit(solution)/shard_map/ppermute | solution.py:14
  129.8 7.0 %collective-permute-start.4 = (f32[512,256]{1,0:T(8,128)S(1)}, f32[512,256]{1,0:T(8,128)S(1)}, u32[]{:S(2)}, u32[]{:S(2)}) collective-permute-start(f32[512,256]{1,0:T(8,128)S(1)} %convolution_select_fusion.3), channel_id=1, source_target_pairs={{0,1},{1,0},{2,3},{3,2},{4,5},{5,4},{6,7},{7,6},{8,9},{9,8},{10,11... | collective-permute-start | bytes 1572872 | tf_op jit(solution)/shard_map/ppermute | solution.py:19
  131.1 16.9 %collective-permute-start.5 = (f32[512,256]{1,0:T(8,128)S(1)}, f32[512,256]{1,0:T(8,128)S(1)}, u32[]{:S(2)}, u32[]{:S(2)}) collective-permute-start(f32[512,256]{1,0:T(8,128)S(1)} %convolution_select_fusion.3), channel_id=1, source_target_pairs={{0,32},{16,48},{32,64},{48,80},{64,96},{80,112},{96,128},{112,144}... | collective-permute-start | bytes 1572872 | tf_op jit(solution)/shard_map/ppermute | solution.py:14
  149.0 10.3 %collective-permute-start.6 = (f32[512,256]{1,0:T(8,128)S(1)}, f32[512,256]{1,0:T(8,128)S(1)}, u32[]{:S(2)}, u32[]{:S(2)}) collective-permute-start(f32[512,256]{1,0:T(8,128)S(1)} %convolution_select_fusion.2), channel_id=1, source_target_pairs={{0,1},{1,0},{2,3},{3,2},{4,5},{5,4},{6,7},{7,6},{8,9},{9,8},{10,11... | collective-permute-start | bytes 1572872 | tf_op jit(solution)/shard_map/ppermute | solution.py:19
  149.9 20.5 %collective-permute-start.7 = (f32[512,256]{1,0:T(8,128)S(1)}, f32[512,256]{1,0:T(8,128)S(1)}, u32[]{:S(2)}, u32[]{:S(2)}) collective-permute-start(f32[512,256]{1,0:T(8,128)S(1)} %convolution_select_fusion.2), channel_id=1, source_target_pairs={{0,64},{16,80},{32,96},{48,112},{64,128},{80,144},{96,160},{112,17... | collective-permute-start | bytes 1572872 | tf_op jit(solution)/shard_map/ppermute | solution.py:14
  171.5 6.7 %collective-permute-start.8 = (f32[512,256]{1,0:T(8,128)S(1)}, f32[512,256]{1,0:T(8,128)S(1)}, u32[]{:S(2)}, u32[]{:S(2)}) collective-permute-start(f32[512,256]{1,0:T(8,128)S(1)} %convolution_select_fusion.1), channel_id=1, source_target_pairs={{0,1},{1,0},{2,3},{3,2},{4,5},{5,4},{6,7},{7,6},{8,9},{9,8},{10,11... | collective-permute-start | bytes 1572872 | tf_op jit(solution)/shard_map/ppermute | solution.py:19
  172.4 16.9 %collective-permute-start.9 = (f32[512,256]{1,0:T(8,128)S(1)}, f32[512,256]{1,0:T(8,128)S(1)}, u32[]{:S(2)}, u32[]{:S(2)}) collective-permute-start(f32[512,256]{1,0:T(8,128)S(1)} %convolution_select_fusion.1), channel_id=1, source_target_pairs={{0,128},{16,144},{32,160},{48,176},{64,192},{80,208},{96,224},{112... | collective-permute-start | bytes 1572872 | tf_op jit(solution)/shard_map/ppermute | solution.py:14
  190.4 2.1 %collective-permute-start.10 = (bf16[512,256]{1,0:T(8,128)(2,1)S(1)}, bf16[512,256]{1,0:T(8,128)(2,1)S(1)}, u32[]{:S(2)}, u32[]{:S(2)}) collective-permute-start(bf16[512,256]{1,0:T(8,128)(2,1)S(1)} %fusion.10), channel_id=1, source_target_pairs={{0,1},{1,0},{2,3},{3,2},{4,5},{5,4},{6,7},{7,6},{8,9},{9,8},{10,11... | collective-permute-start | bytes 786440 | tf_op jit(solution)/shard_map/ppermute | solution.py:19

commit v8 on v7

--- a/solution.py
+++ b/solution.py
@@ -80,7 +80,7 @@
 
 def aligned_rows(embedding, prefix_low):
     _, rows, width = embedding.shape
-    block = 512
+    block = 256
     return pl.pallas_call(
         aligned_block,
         grid=(rows // block,),

time: 199 us -> 201 us (1.010)
  Pallas kernels: 4.74 us -> 6.86 us
    pallas_call x1, Pallas kernels: 4.74 us -> 6.86 us  [aligned_rows(): pl.pallas_call(aligned_block, grid=(rows // block,), in_specs=[pl.BlockSp...]
where the time goes in v8:
time: 201 us; the launch traced here: 200 us
  waiting for transfers between devices  70.4 us (35%)
  blocking collectives  42.2 us (21%)
  starting transfers between devices  38 us (19%)
  matrix products  36.6 us (18%)
  Pallas kernels  6.86 us (3%)
  other arithmetic  3.18 us (2%)
    ppermute x5, waiting for transfers between devices, shifted(): lax.ppermute(value, axis, [(source, source + steps) for source in range(c...  66.2 us
    ppermute x5, starting transfers between devices, shifted(): lax.ppermute(value, axis, [(source, source + steps) for source in range(c...  28.8 us
    all_to_all x1, blocking collectives, summed_over(): reduced = lax.all_to_all(pieces, axis, 0, 0, tiled=False).sum(0)  24.7 us
    all_to_all x1, blocking collectives, summed_over(): mine = lax.all_to_all(copies, axis, 0, 0, tiled=False).reshape(mine.shape)  17.5 us
    dot_general x12, matrix products, update(): return 1.5 * iterate - 0.5 * jnp.dot(iterate, square, precision=precision)  14 us
    dot_general x12, matrix products, update(): square = jnp.dot(iterate.T, iterate, precision=precision)  14 us
    ppermute x6, starting transfers between devices, swapped(): lax.ppermute(value, axis, [(source, source ^ mask) for source in range(co...  9.16 us
    pallas_call x1, Pallas kernels, aligned_rows(): pl.pallas_call(aligned_block, grid=(rows // block,), in_specs=[pl.BlockSp...  6.86 us
  transfers between devices with their start and end apart: 11, of which 8 were waited for; matrix products, arithmetic and copies ran while one was open for 0% of the time, Pallas kernels for 0%

profile of v8, /device:TPU:1, one launch (start us, length us, event | category | flops | bytes accessed | tf_op | source)
XLA Modules:
  0.0 200.3 jit_solution(14446543042314794216)
XLA Ops:
  0.7 4.0 %fusion.7 = bf16[1024,512]{1,0:T(8,128)(2,1)S(1)} fusion(bf16[1,2048,512]{2,1,0:T(8,128)(2,1)} %rows_ref.1, s32[1024]{0:T(1024)S(1)} %broadcast_subtract_fusion), kind=kOutput, calls=%fused_computation.10 | convolution fusion | flops 2150105088 | bytes 3149824 | tf_op jit(solution)/shard_map/dot_general | solution.py:103
  4.7 4.0 %collective-permute-start = (bf16[1024,512]{1,0:T(8,128)(2,1)S(1)}, bf16[1024,512]{1,0:T(8,128)(2,1)S(1)}, u32[]{:S(2)}, u32[]{:S(2)}) collective-permute-start(bf16[1024,512]{1,0:T(8,128)(2,1)S(1)} %fusion.7), channel_id=1, source_target_pairs={{0,16},{16,32},{32,48},{48,64},{64,80},{80,96},{96,112},{112,128},... | collective-permute-start | bytes 3145736 | tf_op jit(solution)/shard_map/ppermute | solution.py:14
  8.7 21.8 %collective-permute-done = bf16[1024,512]{1,0:T(8,128)(2,1)S(1)} collective-permute-done((bf16[1024,512]{1,0:T(8,128)(2,1)S(1)}, bf16[1024,512]{1,0:T(8,128)(2,1)S(1)}, u32[]{:S(2)}, u32[]{:S(2)}) %collective-permute-start) | collective-permute-done | bytes 1048608 | tf_op jit(solution)/shard_map/ppermute | solution.py:14
  31.2 1.6 collective-permute-start.1
  32.9 1.5 collective-permute-done.1
  34.5 24.7 %all_to_all.10 = f32[8,32,512]{2,1,0:T(8,128)S(1)} all-to-all(f32[8,32,512]{2,1,0:T(8,128)S(1)} %bitcast.53), channel_id=1, replica_groups=mesh['ver'=16,'z'=8,'core'=2] {'z'}, dimensions={0} | all-to-all | bytes 1048576 | tf_op jit(solution)/shard_map/all_to_all | solution.py:36
  59.4 17.5 %all_to_all.11 = f32[8,32,512]{2,1,0:T(8,128)S(1)} all-to-all(f32[8,32,512]{2,1,0:T(8,128)S(1)} %broadcast_in_dim.2), channel_id=1, replica_groups=mesh['ver'=16,'z'=8,'core'=2] {'z'}, dimensions={0} | all-to-all | bytes 1048576 | tf_op jit(solution)/shard_map/all_to_all | solution.py:38
  76.9 3.3 %collective-permute-start.2 = (f32[256,512]{1,0:T(8,128)S(1)}, f32[256,512]{1,0:T(8,128)S(1)}, u32[]{:S(2)}, u32[]{:S(2)}) collective-permute-start(f32[256,512]{1,0:T(8,128)S(1)} %bitcast.50), channel_id=1, source_target_pairs={{0,1},{1,0},{2,3},{3,2},{4,5},{5,4},{6,7},{7,6},{8,9},{9,8},{10,11... | collective-permute-start | bytes 1572872 | tf_op jit(solution)/shard_map/ppermute | solution.py:19
  80.2 1.5 collective-permute-done.2
  83.9 21.6 %while.20 = (s32[]{:T(128)}, f32[512,512]{0,1:T(8,128)S(1)}, s32[]{:T(128)}) while((s32[]{:T(128)}, f32[512,512]{0,1:T(8,128)S(1)}, s32[]{:T(128)}) %tuple.32), condition=%wide.region_3.4_spmd, body=%wide.region_2.3_spmd.sunk | while | flops 1611399168 | bytes 7340077 | solution.py:113
  105.6 7.6 %while.21 = (s32[]{:T(128)}, f32[512,512]{0,1:T(8,128)S(1)}, s32[]{:T(128)}) while((s32[]{:T(128)}, f32[512,512]{0,1:T(8,128)S(1)}, s32[]{:T(128)}) %tuple.35), condition=%wide.region_5.6_spmd, body=%wide.region_4.5_spmd.sunk | while | flops 3222011904 | bytes 7340077 | solution.py:114
  105.7 1.9 fusion.73
  107.6 1.9 fusion.74
  109.5 1.9 fusion.73
  111.4 1.9 fusion.74
  113.8 4.2 %collective-permute-start.3 = (f32[512,256]{1,0:T(8,128)S(1)}, f32[512,256]{1,0:T(8,128)S(1)}, u32[]{:S(2)}, u32[]{:S(2)}) collective-permute-start(f32[512,256]{1,0:T(8,128)S(1)} %slice_select_fusion), channel_id=1, source_target_pairs={{0,16},{16,32},{32,48},{48,64},{64,80},{80,96},{96,112},{112,128},... | collective-permute-start | bytes 1572872 | tf_op jit(solution)/shard_map/ppermute | solution.py:14
  117.9 10.9 %collective-permute-done.3 = f32[512,256]{1,0:T(8,128)S(1)} collective-permute-done((f32[512,256]{1,0:T(8,128)S(1)}, f32[512,256]{1,0:T(8,128)S(1)}, u32[]{:S(2)}, u32[]{:S(2)}) %collective-permute-start.3) | collective-permute-done | bytes 524320 | tf_op jit(solution)/shard_map/ppermute | solution.py:14
  131.1 5.6 %collective-permute-start.5 = (f32[512,256]{1,0:T(8,128)S(1)}, f32[512,256]{1,0:T(8,128)S(1)}, u32[]{:S(2)}, u32[]{:S(2)}) collective-permute-start(f32[512,256]{1,0:T(8,128)S(1)} %convolution_select_fusion.3), channel_id=1, source_target_pairs={{0,32},{16,48},{32,64},{48,80},{64,96},{80,112},{96,128},{112,144}... | collective-permute-start | bytes 1572872 | tf_op jit(solution)/shard_map/ppermute | solution.py:14
  136.8 11.2 %collective-permute-done.5 = f32[512,256]{1,0:T(8,128)S(1)} collective-permute-done((f32[512,256]{1,0:T(8,128)S(1)}, f32[512,256]{1,0:T(8,128)S(1)}, u32[]{:S(2)}, u32[]{:S(2)}) %collective-permute-start.5) | collective-permute-done | bytes 524320 | tf_op jit(solution)/shard_map/ppermute | solution.py:14
  149.9 9.3 %collective-permute-start.7 = (f32[512,256]{1,0:T(8,128)S(1)}, f32[512,256]{1,0:T(8,128)S(1)}, u32[]{:S(2)}, u32[]{:S(2)}) collective-permute-start(f32[512,256]{1,0:T(8,128)S(1)} %convolution_select_fusion.2), channel_id=1, source_target_pairs={{0,64},{16,80},{32,96},{48,112},{64,128},{80,144},{96,160},{112,17... | collective-permute-start | bytes 1572872 | tf_op jit(solution)/shard_map/ppermute | solution.py:14
  159.3 11.2 %collective-permute-done.7 = f32[512,256]{1,0:T(8,128)S(1)} collective-permute-done((f32[512,256]{1,0:T(8,128)S(1)}, f32[512,256]{1,0:T(8,128)S(1)}, u32[]{:S(2)}, u32[]{:S(2)}) %collective-permute-start.7) | collective-permute-done | bytes 524320 | tf_op jit(solution)/shard_map/ppermute | solution.py:14
  172.4 5.7 %collective-permute-start.9 = (f32[512,256]{1,0:T(8,128)S(1)}, f32[512,256]{1,0:T(8,128)S(1)}, u32[]{:S(2)}, u32[]{:S(2)}) collective-permute-start(f32[512,256]{1,0:T(8,128)S(1)} %convolution_select_fusion.1), channel_id=1, source_target_pairs={{0,128},{16,144},{32,160},{48,176},{64,192},{80,208},{96,224},{112... | collective-permute-start | bytes 1572872 | tf_op jit(solution)/shard_map/ppermute | solution.py:14
  178.2 11.2 %collective-permute-done.9 = f32[512,256]{1,0:T(8,128)S(1)} collective-permute-done((f32[512,256]{1,0:T(8,128)S(1)}, f32[512,256]{1,0:T(8,128)S(1)}, u32[]{:S(2)}, u32[]{:S(2)}) %collective-permute-start.9) | collective-permute-done | bytes 524320 | tf_op jit(solution)/shard_map/ppermute | solution.py:14
  193.4 6.9 %shard_map.28 = bf16[1,2048,512]{2,1,0:T(8,128)(2,1)} custom-call(bf16[1,2048,512]{2,1,0:T(8,128)(2,1)} %rows_ref.1, bf16[512,512]{1,0:T(8,128)(2,1)} %maximum_select_fusion.7.prefix_ref), custom_call_target="tpu_custom_call" | custom-call | tf_op jit(solution)/shard_map/pallas_call | solution.py:84
  (57 shorter events, 35.4 us)
Async XLA Ops:
  4.7 25.8 %collective-permute-start = (bf16[1024,512]{1,0:T(8,128)(2,1)S(1)}, bf16[1024,512]{1,0:T(8,128)(2,1)S(1)}, u32[]{:S(2)}, u32[]{:S(2)}) collective-permute-start(bf16[1024,512]{1,0:T(8,128)(2,1)S(1)} %fusion.7), channel_id=1, source_target_pairs={{0,16},{16,32},{32,48},{48,64},{64,80},{80,96},{96,112},{112,128},... | collective-permute-start | bytes 3145736 | tf_op jit(solution)/shard_map/ppermute | solution.py:14
  31.2 3.2 %collective-permute-start.1 = (f32[256,512]{1,0:T(8,128)S(1)}, f32[256,512]{1,0:T(8,128)S(1)}, u32[]{:S(2)}, u32[]{:S(2)}) collective-permute-start(f32[256,512]{1,0:T(8,128)S(1)} %slice_select_fusion.1), channel_id=1, source_target_pairs={{0,1},{1,0},{2,3},{3,2},{4,5},{5,4},{6,7},{7,6},{8,9},{9,8},{10,11... | collective-permute-start | bytes 1572872 | tf_op jit(solution)/shard_map/ppermute | solution.py:19
  76.9 4.9 %collective-permute-start.2 = (f32[256,512]{1,0:T(8,128)S(1)}, f32[256,512]{1,0:T(8,128)S(1)}, u32[]{:S(2)}, u32[]{:S(2)}) collective-permute-start(f32[256,512]{1,0:T(8,128)S(1)} %bitcast.50), channel_id=1, source_target_pairs={{0,1},{1,0},{2,3},{3,2},{4,5},{5,4},{6,7},{7,6},{8,9},{9,8},{10,11... | collective-permute-start | bytes 1572872 | tf_op jit(solution)/shard_map/ppermute | solution.py:19
  113.8 15.0 %collective-permute-start.3 = (f32[512,256]{1,0:T(8,128)S(1)}, f32[512,256]{1,0:T(8,128)S(1)}, u32[]{:S(2)}, u32[]{:S(2)}) collective-permute-start(f32[512,256]{1,0:T(8,128)S(1)} %slice_select_fusion), channel_id=1, source_target_pairs={{0,16},{16,32},{32,48},{48,64},{64,80},{80,96},{96,112},{112,128},... | collective-permute-start | bytes 1572872 | tf_op jit(solution)/shard_map/ppermute | solution.py:14
  129.8 7.0 %collective-permute-start.4 = (f32[512,256]{1,0:T(8,128)S(1)}, f32[512,256]{1,0:T(8,128)S(1)}, u32[]{:S(2)}, u32[]{:S(2)}) collective-permute-start(f32[512,256]{1,0:T(8,128)S(1)} %convolution_select_fusion.3), channel_id=1, source_target_pairs={{0,1},{1,0},{2,3},{3,2},{4,5},{5,4},{6,7},{7,6},{8,9},{9,8},{10,11... | collective-permute-start | bytes 1572872 | tf_op jit(solution)/shard_map/ppermute | solution.py:19
  131.1 16.9 %collective-permute-start.5 = (f32[512,256]{1,0:T(8,128)S(1)}, f32[512,256]{1,0:T(8,128)S(1)}, u32[]{:S(2)}, u32[]{:S(2)}) collective-permute-start(f32[512,256]{1,0:T(8,128)S(1)} %convolution_select_fusion.3), channel_id=1, source_target_pairs={{0,32},{16,48},{32,64},{48,80},{64,96},{80,112},{96,128},{112,144}... | collective-permute-start | bytes 1572872 | tf_op jit(solution)/shard_map/ppermute | solution.py:14
  149.0 10.3 %collective-permute-start.6 = (f32[512,256]{1,0:T(8,128)S(1)}, f32[512,256]{1,0:T(8,128)S(1)}, u32[]{:S(2)}, u32[]{:S(2)}) collective-permute-start(f32[512,256]{1,0:T(8,128)S(1)} %convolution_select_fusion.2), channel_id=1, source_target_pairs={{0,1},{1,0},{2,3},{3,2},{4,5},{5,4},{6,7},{7,6},{8,9},{9,8},{10,11... | collective-permute-start | bytes 1572872 | tf_op jit(solution)/shard_map/ppermute | solution.py:19
  149.9 20.5 %collective-permute-start.7 = (f32[512,256]{1,0:T(8,128)S(1)}, f32[512,256]{1,0:T(8,128)S(1)}, u32[]{:S(2)}, u32[]{:S(2)}) collective-permute-start(f32[512,256]{1,0:T(8,128)S(1)} %convolution_select_fusion.2), channel_id=1, source_target_pairs={{0,64},{16,80},{32,96},{48,112},{64,128},{80,144},{96,160},{112,17... | collective-permute-start | bytes 1572872 | tf_op jit(solution)/shard_map/ppermute | solution.py:14
  171.5 6.7 %collective-permute-start.8 = (f32[512,256]{1,0:T(8,128)S(1)}, f32[512,256]{1,0:T(8,128)S(1)}, u32[]{:S(2)}, u32[]{:S(2)}) collective-permute-start(f32[512,256]{1,0:T(8,128)S(1)} %convolution_select_fusion.1), channel_id=1, source_target_pairs={{0,1},{1,0},{2,3},{3,2},{4,5},{5,4},{6,7},{7,6},{8,9},{9,8},{10,11... | collective-permute-start | bytes 1572872 | tf_op jit(solution)/shard_map/ppermute | solution.py:19
  172.4 16.9 %collective-permute-start.9 = (f32[512,256]{1,0:T(8,128)S(1)}, f32[512,256]{1,0:T(8,128)S(1)}, u32[]{:S(2)}, u32[]{:S(2)}) collective-permute-start(f32[512,256]{1,0:T(8,128)S(1)} %convolution_select_fusion.1), channel_id=1, source_target_pairs={{0,128},{16,144},{32,160},{48,176},{64,192},{80,208},{96,224},{112... | collective-permute-start | bytes 1572872 | tf_op jit(solution)/shard_map/ppermute | solution.py:14
  190.4 2.1 %collective-permute-start.10 = (bf16[512,256]{1,0:T(8,128)(2,1)S(1)}, bf16[512,256]{1,0:T(8,128)(2,1)S(1)}, u32[]{:S(2)}, u32[]{:S(2)}) collective-permute-start(bf16[512,256]{1,0:T(8,128)(2,1)S(1)} %fusion.10), channel_id=1, source_target_pairs={{0,1},{1,0},{2,3},{3,2},{4,5},{5,4},{6,7},{7,6},{8,9},{9,8},{10,11... | collective-permute-start | bytes 786440 | tf_op jit(solution)/shard_map/ppermute | solution.py:19

commit v9 on v8

--- a/solution.py
+++ b/solution.py
@@ -80,7 +80,7 @@
 
 def aligned_rows(embedding, prefix_low):
     _, rows, width = embedding.shape
-    block = 256
+    block = 1024
     return pl.pallas_call(
         aligned_block,
         grid=(rows // block,),

time: 201 us -> 198 us (0.985)
  Pallas kernels: 6.86 us -> 3.76 us
    pallas_call x1, Pallas kernels: 6.86 us -> 3.76 us  [aligned_rows(): pl.pallas_call(aligned_block, grid=(rows // block,), in_specs=[pl.BlockSp...]
where the time goes in v9:
time: 198 us; the launch traced here: 197 us
  waiting for transfers between devices  70.4 us (36%)
  blocking collectives  42.2 us (21%)
  starting transfers between devices  38.2 us (19%)
  matrix products  36.6 us (18%)
  Pallas kernels  3.76 us (2%)
  other arithmetic  3.18 us (2%)
    ppermute x5, waiting for transfers between devices, shifted(): lax.ppermute(value, axis, [(source, source + steps) for source in range(c...  66.2 us
    ppermute x5, starting transfers between devices, shifted(): lax.ppermute(value, axis, [(source, source + steps) for source in range(c...  28.8 us
    all_to_all x1, blocking collectives, summed_over(): reduced = lax.all_to_all(pieces, axis, 0, 0, tiled=False).sum(0)  24.7 us
    all_to_all x1, blocking collectives, summed_over(): mine = lax.all_to_all(copies, axis, 0, 0, tiled=False).reshape(mine.shape)  17.5 us
    dot_general x12, matrix products, update(): return 1.5 * iterate - 0.5 * jnp.dot(iterate, square, precision=precision)  14 us
    dot_general x12, matrix products, update(): square = jnp.dot(iterate.T, iterate, precision=precision)  14 us
    ppermute x6, starting transfers between devices, swapped(): lax.ppermute(value, axis, [(source, source ^ mask) for source in range(co...  9.39 us
    ppermute x6, waiting for transfers between devices, swapped(): lax.ppermute(value, axis, [(source, source ^ mask) for source in range(co...  4.24 us
  transfers between devices with their start and end apart: 11, of which 8 were waited for; matrix products, arithmetic and copies ran while one was open for 0% of the time, Pallas kernels for 0%

profile of v9, /device:TPU:1, one launch (start us, length us, event | category | flops | bytes accessed | tf_op | source)
XLA Modules:
  0.0 197.4 jit_solution(7048150800740518526)
XLA Ops:
  0.7 4.0 %fusion.7 = bf16[1024,512]{1,0:T(8,128)(2,1)S(1)} fusion(bf16[1,2048,512]{2,1,0:T(8,128)(2,1)} %rows_ref.1, s32[1024]{0:T(1024)S(1)} %broadcast_subtract_fusion), kind=kOutput, calls=%fused_computation.10 | convolution fusion | flops 2150105088 | bytes 3149824 | tf_op jit(solution)/shard_map/dot_general | solution.py:103
  4.7 4.0 %collective-permute-start = (bf16[1024,512]{1,0:T(8,128)(2,1)S(1)}, bf16[1024,512]{1,0:T(8,128)(2,1)S(1)}, u32[]{:S(2)}, u32[]{:S(2)}) collective-permute-start(bf16[1024,512]{1,0:T(8,128)(2,1)S(1)} %fusion.7), channel_id=1, source_target_pairs={{0,16},{16,32},{32,48},{48,64},{64,80},{80,96},{96,112},{112,128},... | collective-permute-start | bytes 3145736 | tf_op jit(solution)/shard_map/ppermute | solution.py:14
  8.7 21.8 %collective-permute-done = bf16[1024,512]{1,0:T(8,128)(2,1)S(1)} collective-permute-done((bf16[1024,512]{1,0:T(8,128)(2,1)S(1)}, bf16[1024,512]{1,0:T(8,128)(2,1)S(1)}, u32[]{:S(2)}, u32[]{:S(2)}) %collective-permute-start) | collective-permute-done | bytes 1048608 | tf_op jit(solution)/shard_map/ppermute | solution.py:14
  31.2 1.6 collective-permute-start.1
  32.9 1.5 collective-permute-done.1
  34.5 24.7 %all_to_all.10 = f32[8,32,512]{2,1,0:T(8,128)S(1)} all-to-all(f32[8,32,512]{2,1,0:T(8,128)S(1)} %bitcast.53), channel_id=1, replica_groups=mesh['ver'=16,'z'=8,'core'=2] {'z'}, dimensions={0} | all-to-all | bytes 1048576 | tf_op jit(solution)/shard_map/all_to_all | solution.py:36
  59.4 17.5 %all_to_all.11 = f32[8,32,512]{2,1,0:T(8,128)S(1)} all-to-all(f32[8,32,512]{2,1,0:T(8,128)S(1)} %broadcast_in_dim.2), channel_id=1, replica_groups=mesh['ver'=16,'z'=8,'core'=2] {'z'}, dimensions={0} | all-to-all | bytes 1048576 | tf_op jit(solution)/shard_map/all_to_all | solution.py:38
  76.9 3.3 %collective-permute-start.2 = (f32[256,512]{1,0:T(8,128)S(1)}, f32[256,512]{1,0:T(8,128)S(1)}, u32[]{:S(2)}, u32[]{:S(2)}) collective-permute-start(f32[256,512]{1,0:T(8,128)S(1)} %bitcast.50), channel_id=1, source_target_pairs={{0,1},{1,0},{2,3},{3,2},{4,5},{5,4},{6,7},{7,6},{8,9},{9,8},{10,11... | collective-permute-start | bytes 1572872 | tf_op jit(solution)/shard_map/ppermute | solution.py:19
  80.2 1.5 collective-permute-done.2
  83.9 21.6 %while.20 = (s32[]{:T(128)}, f32[512,512]{0,1:T(8,128)S(1)}, s32[]{:T(128)}) while((s32[]{:T(128)}, f32[512,512]{0,1:T(8,128)S(1)}, s32[]{:T(128)}) %tuple.32), condition=%wide.region_3.4_spmd, body=%wide.region_2.3_spmd.sunk | while | flops 1611399168 | bytes 7340077 | solution.py:113
  105.6 7.6 %while.21 = (s32[]{:T(128)}, f32[512,512]{0,1:T(8,128)S(1)}, s32[]{:T(128)}) while((s32[]{:T(128)}, f32[512,512]{0,1:T(8,128)S(1)}, s32[]{:T(128)}) %tuple.35), condition=%wide.region_5.6_spmd, body=%wide.region_4.5_spmd.sunk | while | flops 3222011904 | bytes 7340077 | solution.py:114
  105.7 1.9 fusion.73
  107.6 1.9 fusion.74
  109.5 1.9 fusion.73
  111.4 1.9 fusion.74
  113.8 4.2 %collective-permute-start.3 = (f32[512,256]{1,0:T(8,128)S(1)}, f32[512,256]{1,0:T(8,128)S(1)}, u32[]{:S(2)}, u32[]{:S(2)}) collective-permute-start(f32[512,256]{1,0:T(8,128)S(1)} %slice_select_fusion), channel_id=1, source_target_pairs={{0,16},{16,32},{32,48},{48,64},{64,80},{80,96},{96,112},{112,128},... | collective-permute-start | bytes 1572872 | tf_op jit(solution)/shard_map/ppermute | solution.py:14
  117.9 10.9 %collective-permute-done.3 = f32[512,256]{1,0:T(8,128)S(1)} collective-permute-done((f32[512,256]{1,0:T(8,128)S(1)}, f32[512,256]{1,0:T(8,128)S(1)}, u32[]{:S(2)}, u32[]{:S(2)}) %collective-permute-start.3) | collective-permute-done | bytes 524320 | tf_op jit(solution)/shard_map/ppermute | solution.py:14
  131.1 5.6 %collective-permute-start.5 = (f32[512,256]{1,0:T(8,128)S(1)}, f32[512,256]{1,0:T(8,128)S(1)}, u32[]{:S(2)}, u32[]{:S(2)}) collective-permute-start(f32[512,256]{1,0:T(8,128)S(1)} %convolution_select_fusion.3), channel_id=1, source_target_pairs={{0,32},{16,48},{32,64},{48,80},{64,96},{80,112},{96,128},{112,144}... | collective-permute-start | bytes 1572872 | tf_op jit(solution)/shard_map/ppermute | solution.py:14
  136.8 11.2 %collective-permute-done.5 = f32[512,256]{1,0:T(8,128)S(1)} collective-permute-done((f32[512,256]{1,0:T(8,128)S(1)}, f32[512,256]{1,0:T(8,128)S(1)}, u32[]{:S(2)}, u32[]{:S(2)}) %collective-permute-start.5) | collective-permute-done | bytes 524320 | tf_op jit(solution)/shard_map/ppermute | solution.py:14
  149.9 9.3 %collective-permute-start.7 = (f32[512,256]{1,0:T(8,128)S(1)}, f32[512,256]{1,0:T(8,128)S(1)}, u32[]{:S(2)}, u32[]{:S(2)}) collective-permute-start(f32[512,256]{1,0:T(8,128)S(1)} %convolution_select_fusion.2), channel_id=1, source_target_pairs={{0,64},{16,80},{32,96},{48,112},{64,128},{80,144},{96,160},{112,17... | collective-permute-start | bytes 1572872 | tf_op jit(solution)/shard_map/ppermute | solution.py:14
  159.3 11.2 %collective-permute-done.7 = f32[512,256]{1,0:T(8,128)S(1)} collective-permute-done((f32[512,256]{1,0:T(8,128)S(1)}, f32[512,256]{1,0:T(8,128)S(1)}, u32[]{:S(2)}, u32[]{:S(2)}) %collective-permute-start.7) | collective-permute-done | bytes 524320 | tf_op jit(solution)/shard_map/ppermute | solution.py:14
  172.7 5.7 %collective-permute-start.9 = (f32[512,256]{1,0:T(8,128)S(1)}, f32[512,256]{1,0:T(8,128)S(1)}, u32[]{:S(2)}, u32[]{:S(2)}) collective-permute-start(f32[512,256]{1,0:T(8,128)S(1)} %convolution_select_fusion.1), channel_id=1, source_target_pairs={{0,128},{16,144},{32,160},{48,176},{64,192},{80,208},{96,224},{112... | collective-permute-start | bytes 1572872 | tf_op jit(solution)/shard_map/ppermute | solution.py:14
  178.4 11.2 %collective-permute-done.9 = f32[512,256]{1,0:T(8,128)S(1)} collective-permute-done((f32[512,256]{1,0:T(8,128)S(1)}, f32[512,256]{1,0:T(8,128)S(1)}, u32[]{:S(2)}, u32[]{:S(2)}) %collective-permute-start.9) | collective-permute-done | bytes 524320 | tf_op jit(solution)/shard_map/ppermute | solution.py:14
  193.6 3.8 %shard_map.28 = bf16[1,2048,512]{2,1,0:T(8,128)(2,1)} custom-call(bf16[1,2048,512]{2,1,0:T(8,128)(2,1)} %rows_ref.1, bf16[512,512]{1,0:T(8,128)(2,1)} %maximum_select_fusion.7.prefix_ref), custom_call_target="tpu_custom_call" | custom-call | tf_op jit(solution)/shard_map/pallas_call | solution.py:84
  (57 shorter events, 35.6 us)
Async XLA Ops:
  4.7 25.8 %collective-permute-start = (bf16[1024,512]{1,0:T(8,128)(2,1)S(1)}, bf16[1024,512]{1,0:T(8,128)(2,1)S(1)}, u32[]{:S(2)}, u32[]{:S(2)}) collective-permute-start(bf16[1024,512]{1,0:T(8,128)(2,1)S(1)} %fusion.7), channel_id=1, source_target_pairs={{0,16},{16,32},{32,48},{48,64},{64,80},{80,96},{96,112},{112,128},... | collective-permute-start | bytes 3145736 | tf_op jit(solution)/shard_map/ppermute | solution.py:14
  31.2 3.2 %collective-permute-start.1 = (f32[256,512]{1,0:T(8,128)S(1)}, f32[256,512]{1,0:T(8,128)S(1)}, u32[]{:S(2)}, u32[]{:S(2)}) collective-permute-start(f32[256,512]{1,0:T(8,128)S(1)} %slice_select_fusion.1), channel_id=1, source_target_pairs={{0,1},{1,0},{2,3},{3,2},{4,5},{5,4},{6,7},{7,6},{8,9},{9,8},{10,11... | collective-permute-start | bytes 1572872 | tf_op jit(solution)/shard_map/ppermute | solution.py:19
  76.9 4.9 %collective-permute-start.2 = (f32[256,512]{1,0:T(8,128)S(1)}, f32[256,512]{1,0:T(8,128)S(1)}, u32[]{:S(2)}, u32[]{:S(2)}) collective-permute-start(f32[256,512]{1,0:T(8,128)S(1)} %bitcast.50), channel_id=1, source_target_pairs={{0,1},{1,0},{2,3},{3,2},{4,5},{5,4},{6,7},{7,6},{8,9},{9,8},{10,11... | collective-permute-start | bytes 1572872 | tf_op jit(solution)/shard_map/ppermute | solution.py:19
  113.8 15.0 %collective-permute-start.3 = (f32[512,256]{1,0:T(8,128)S(1)}, f32[512,256]{1,0:T(8,128)S(1)}, u32[]{:S(2)}, u32[]{:S(2)}) collective-permute-start(f32[512,256]{1,0:T(8,128)S(1)} %slice_select_fusion), channel_id=1, source_target_pairs={{0,16},{16,32},{32,48},{48,64},{64,80},{80,96},{96,112},{112,128},... | collective-permute-start | bytes 1572872 | tf_op jit(solution)/shard_map/ppermute | solution.py:14
  129.8 7.0 %collective-permute-start.4 = (f32[512,256]{1,0:T(8,128)S(1)}, f32[512,256]{1,0:T(8,128)S(1)}, u32[]{:S(2)}, u32[]{:S(2)}) collective-permute-start(f32[512,256]{1,0:T(8,128)S(1)} %convolution_select_fusion.3), channel_id=1, source_target_pairs={{0,1},{1,0},{2,3},{3,2},{4,5},{5,4},{6,7},{7,6},{8,9},{9,8},{10,11... | collective-permute-start | bytes 1572872 | tf_op jit(solution)/shard_map/ppermute | solution.py:19
  131.1 16.9 %collective-permute-start.5 = (f32[512,256]{1,0:T(8,128)S(1)}, f32[512,256]{1,0:T(8,128)S(1)}, u32[]{:S(2)}, u32[]{:S(2)}) collective-permute-start(f32[512,256]{1,0:T(8,128)S(1)} %convolution_select_fusion.3), channel_id=1, source_target_pairs={{0,32},{16,48},{32,64},{48,80},{64,96},{80,112},{96,128},{112,144}... | collective-permute-start | bytes 1572872 | tf_op jit(solution)/shard_map/ppermute | solution.py:14
  149.0 10.3 %collective-permute-start.6 = (f32[512,256]{1,0:T(8,128)S(1)}, f32[512,256]{1,0:T(8,128)S(1)}, u32[]{:S(2)}, u32[]{:S(2)}) collective-permute-start(f32[512,256]{1,0:T(8,128)S(1)} %convolution_select_fusion.2), channel_id=1, source_target_pairs={{0,1},{1,0},{2,3},{3,2},{4,5},{5,4},{6,7},{7,6},{8,9},{9,8},{10,11... | collective-permute-start | bytes 1572872 | tf_op jit(solution)/shard_map/ppermute | solution.py:19
  149.9 20.5 %collective-permute-start.7 = (f32[512,256]{1,0:T(8,128)S(1)}, f32[512,256]{1,0:T(8,128)S(1)}, u32[]{:S(2)}, u32[]{:S(2)}) collective-permute-start(f32[512,256]{1,0:T(8,128)S(1)} %convolution_select_fusion.2), channel_id=1, source_target_pairs={{0,64},{16,80},{32,96},{48,112},{64,128},{80,144},{96,160},{112,17... | collective-permute-start | bytes 1572872 | tf_op jit(solution)/shard_map/ppermute | solution.py:14
  171.5 6.9 %collective-permute-start.8 = (f32[512,256]{1,0:T(8,128)S(1)}, f32[512,256]{1,0:T(8,128)S(1)}, u32[]{:S(2)}, u32[]{:S(2)}) collective-permute-start(f32[512,256]{1,0:T(8,128)S(1)} %convolution_select_fusion.1), channel_id=1, source_target_pairs={{0,1},{1,0},{2,3},{3,2},{4,5},{5,4},{6,7},{7,6},{8,9},{9,8},{10,11... | collective-permute-start | bytes 1572872 | tf_op jit(solution)/shard_map/ppermute | solution.py:19
  172.7 16.9 %collective-permute-start.9 = (f32[512,256]{1,0:T(8,128)S(1)}, f32[512,256]{1,0:T(8,128)S(1)}, u32[]{:S(2)}, u32[]{:S(2)}) collective-permute-start(f32[512,256]{1,0:T(8,128)S(1)} %convolution_select_fusion.1), channel_id=1, source_target_pairs={{0,128},{16,144},{32,160},{48,176},{64,192},{80,208},{96,224},{112... | collective-permute-start | bytes 1572872 | tf_op jit(solution)/shard_map/ppermute | solution.py:14
  190.6 2.1 %collective-permute-start.10 = (bf16[512,256]{1,0:T(8,128)(2,1)S(1)}, bf16[512,256]{1,0:T(8,128)(2,1)S(1)}, u32[]{:S(2)}, u32[]{:S(2)}) collective-permute-start(bf16[512,256]{1,0:T(8,128)(2,1)S(1)} %fusion.10), channel_id=1, source_target_pairs={{0,1},{1,0},{2,3},{3,2},{4,5},{5,4},{6,7},{7,6},{8,9},{9,8},{10,11... | collective-permute-start | bytes 786440 | tf_op jit(solution)/shard_map/ppermute | solution.py:19

commit v10 on v7

--- a/solution.py
+++ b/solution.py
@@ -2,6 +2,7 @@
 import jax.numpy as jnp
 from jax import lax
 from jax.experimental import pallas as pl
+from jax.experimental.pallas import tpu as pltpu
 from jax.sharding import Mesh, PartitionSpec as P
 
 ITERS = 12
@@ -73,24 +74,41 @@
     return own_columns
 
 
-def aligned_block(rows_ref, prefix_ref, out_ref):
-    product = jnp.dot(rows_ref[...], prefix_ref[...], preferred_element_type=jnp.float32)
-    out_ref[...] = product.astype(out_ref.dtype)
+def aligned_block(core_ref, rows_ref, own_ref, other_ref, out_ref):
+    half = own_ref.shape[1]
+    rows = rows_ref[...]
+
+    def store(left_ref, right_ref):
+        out_ref[:, :half] = jnp.dot(rows, left_ref[...], preferred_element_type=jnp.float32).astype(out_ref.dtype)
+        out_ref[:, half:] = jnp.dot(rows, right_ref[...], preferred_element_type=jnp.float32).astype(out_ref.dtype)
+
+    @pl.when(core_ref[0] == 0)
+    def _():
+        store(own_ref, other_ref)
+
+    @pl.when(core_ref[0] != 0)
+    def _():
+        store(other_ref, own_ref)
 
 
-def aligned_rows(embedding, prefix_low):
+def aligned_rows(embedding, own_low, other_low, core):
     _, rows, width = embedding.shape
+    half = own_low.shape[1]
     block = 512
     return pl.pallas_call(
         aligned_block,
-        grid=(rows // block,),
-        in_specs=[
-            pl.BlockSpec((None, block, width), lambda i: (0, i, 0)),
-            pl.BlockSpec((width, width), lambda i: (0, 0)),
-        ],
-        out_specs=pl.BlockSpec((None, block, width), lambda i: (0, i, 0)),
+        grid_spec=pltpu.PrefetchScalarGridSpec(
+            num_scalar_prefetch=1,
+            grid=(rows // block,),
+            in_specs=[
+                pl.BlockSpec((None, block, width), lambda i, c: (0, i, 0)),
+                pl.BlockSpec((width, half), lambda i, c: (0, 0)),
+                pl.BlockSpec((width, half), lambda i, c: (0, 0)),
+            ],
+            out_specs=pl.BlockSpec((None, block, width), lambda i, c: (0, i, 0)),
+        ),
         out_shape=jax.ShapeDtypeStruct(embedding.shape, embedding.dtype),
-    )(embedding, prefix_low)
+    )(jnp.reshape(core, (1,)).astype(jnp.int32), embedding, own_low, other_low)
 
 
 def per_device(embedding, anchor_rows):
@@ -115,8 +133,7 @@
     identity_matrix = jnp.eye(width, dtype=jnp.float32)
     rotation = jnp.where(lax.axis_index("ver") == 0, identity_matrix, rotation)
     own_low = running_product(rotation, "ver", core).astype(jnp.bfloat16)
-    prefix_low = joined_columns(own_low, swapped(own_low, "core", 1), core)
-    return aligned_rows(embedding, prefix_low)
+    return aligned_rows(embedding, own_low, swapped(own_low, "core", 1), core)
 
 
 def solution(mesh):

time: 199 us -> 199 us (level)
  no operation moved by 1% of the time
where the time goes in v10:
time: 199 us; the launch traced here: 198 us
  waiting for transfers between devices  70.4 us (35%)
  blocking collectives  42.2 us (21%)
  starting transfers between devices  38.2 us (19%)
  matrix products  36.6 us (18%)
  Pallas kernels  4.79 us (2%)
  local copies, waits for them, and re-layouts  2.26 us (1%)
  other arithmetic  2.22 us (1%)
    ppermute x5, waiting for transfers between devices, shifted(): lax.ppermute(value, axis, [(source, source + steps) for source in range(c...  66.2 us
    ppermute x5, starting transfers between devices, shifted(): lax.ppermute(value, axis, [(source, source + steps) for source in range(c...  28.8 us
    all_to_all x1, blocking collectives, summed_over(): reduced = lax.all_to_all(pieces, axis, 0, 0, tiled=False).sum(0)  24.7 us
    all_to_all x1, blocking collectives, summed_over(): mine = lax.all_to_all(copies, axis, 0, 0, tiled=False).reshape(mine.shape)  17.5 us
    dot_general x12, matrix products, update(): return 1.5 * iterate - 0.5 * jnp.dot(iterate, square, precision=precision)  14 us
    dot_general x12, matrix products, update(): square = jnp.dot(iterate.T, iterate, precision=precision)  14 us
    ppermute x6, starting transfers between devices, swapped(): lax.ppermute(value, axis, [(source, source ^ mask) for source in range(co...  9.39 us
    pallas_call x1, Pallas kernels, aligned_rows(): pl.pallas_call(aligned_block, grid_spec=pltpu.PrefetchScalarGridSpec(num_...  4.79 us
  transfers between devices with their start and end apart: 11, of which 8 were waited for; matrix products, arithmetic and copies ran while one was open for 0% of the time, Pallas kernels for 0%

profile of v10, /device:TPU:1, one launch (start us, length us, event | category | flops | bytes accessed | tf_op | source)
XLA Modules:
  0.0 198.1 jit_solution(13296206255513680820)
XLA Ops:
  0.7 4.0 %fusion.7 = bf16[1024,512]{1,0:T(8,128)(2,1)S(1)} fusion(bf16[1,2048,512]{2,1,0:T(8,128)(2,1)} %rows_ref.1, s32[1024]{0:T(1024)S(1)} %broadcast_subtract_fusion), kind=kOutput, calls=%fused_computation.10 | convolution fusion | flops 2150105088 | bytes 3149824 | tf_op jit(solution)/shard_map/dot_general | solution.py:121
  4.7 4.0 %collective-permute-start = (bf16[1024,512]{1,0:T(8,128)(2,1)S(1)}, bf16[1024,512]{1,0:T(8,128)(2,1)S(1)}, u32[]{:S(2)}, u32[]{:S(2)}) collective-permute-start(bf16[1024,512]{1,0:T(8,128)(2,1)S(1)} %fusion.7), channel_id=1, source_target_pairs={{0,16},{16,32},{32,48},{48,64},{64,80},{80,96},{96,112},{112,128},... | collective-permute-start | bytes 3145736 | tf_op jit(solution)/shard_map/ppermute | solution.py:15
  8.7 21.8 %collective-permute-done = bf16[1024,512]{1,0:T(8,128)(2,1)S(1)} collective-permute-done((bf16[1024,512]{1,0:T(8,128)(2,1)S(1)}, bf16[1024,512]{1,0:T(8,128)(2,1)S(1)}, u32[]{:S(2)}, u32[]{:S(2)}) %collective-permute-start) | collective-permute-done | bytes 1048608 | tf_op jit(solution)/shard_map/ppermute | solution.py:15
  31.2 1.6 collective-permute-start.1
  32.9 1.5 collective-permute-done.1
  34.5 24.7 %all_to_all.10 = f32[8,32,512]{2,1,0:T(8,128)S(1)} all-to-all(f32[8,32,512]{2,1,0:T(8,128)S(1)} %bitcast.54), channel_id=1, replica_groups=mesh['ver'=16,'z'=8,'core'=2] {'z'}, dimensions={0} | all-to-all | bytes 1048576 | tf_op jit(solution)/shard_map/all_to_all | solution.py:37
  59.4 17.5 %all_to_all.11 = f32[8,32,512]{2,1,0:T(8,128)S(1)} all-to-all(f32[8,32,512]{2,1,0:T(8,128)S(1)} %broadcast_in_dim.2), channel_id=1, replica_groups=mesh['ver'=16,'z'=8,'core'=2] {'z'}, dimensions={0} | all-to-all | bytes 1048576 | tf_op jit(solution)/shard_map/all_to_all | solution.py:39
  76.9 3.3 %collective-permute-start.2 = (f32[256,512]{1,0:T(8,128)S(1)}, f32[256,512]{1,0:T(8,128)S(1)}, u32[]{:S(2)}, u32[]{:S(2)}) collective-permute-start(f32[256,512]{1,0:T(8,128)S(1)} %bitcast.51), channel_id=1, source_target_pairs={{0,1},{1,0},{2,3},{3,2},{4,5},{5,4},{6,7},{7,6},{8,9},{9,8},{10,11... | collective-permute-start | bytes 1572872 | tf_op jit(solution)/shard_map/ppermute | solution.py:20
  80.2 1.5 collective-permute-done.2
  83.9 21.6 %while.20 = (s32[]{:T(128)}, f32[512,512]{0,1:T(8,128)S(1)}, s32[]{:T(128)}) while((s32[]{:T(128)}, f32[512,512]{0,1:T(8,128)S(1)}, s32[]{:T(128)}) %tuple.32), condition=%wide.region_3.4_spmd, body=%wide.region_2.3_spmd.sunk | while | flops 1611399168 | bytes 7340077 | solution.py:131
  105.5 7.6 %while.21 = (s32[]{:T(128)}, f32[512,512]{0,1:T(8,128)S(1)}, s32[]{:T(128)}) while((s32[]{:T(128)}, f32[512,512]{0,1:T(8,128)S(1)}, s32[]{:T(128)}) %tuple.35), condition=%wide.region_5.6_spmd, body=%wide.region_4.5_spmd.sunk | while | flops 3222011904 | bytes 7340077 | solution.py:132
  105.6 1.9 fusion.73
  107.5 1.9 fusion.74
  109.4 1.9 fusion.73
  111.3 1.9 fusion.74
  113.7 4.1 %collective-permute-start.3 = (f32[512,256]{1,0:T(8,128)S(1)}, f32[512,256]{1,0:T(8,128)S(1)}, u32[]{:S(2)}, u32[]{:S(2)}) collective-permute-start(f32[512,256]{1,0:T(8,128)S(1)} %slice_select_fusion), channel_id=1, source_target_pairs={{0,16},{16,32},{32,48},{48,64},{64,80},{80,96},{96,112},{112,128},... | collective-permute-start | bytes 1572872 | tf_op jit(solution)/shard_map/ppermute | solution.py:15
  117.8 10.9 %collective-permute-done.3 = f32[512,256]{1,0:T(8,128)S(1)} collective-permute-done((f32[512,256]{1,0:T(8,128)S(1)}, f32[512,256]{1,0:T(8,128)S(1)}, u32[]{:S(2)}, u32[]{:S(2)}) %collective-permute-start.3) | collective-permute-done | bytes 524320 | tf_op jit(solution)/shard_map/ppermute | solution.py:15
  131.0 5.7 %collective-permute-start.5 = (f32[512,256]{1,0:T(8,128)S(1)}, f32[512,256]{1,0:T(8,128)S(1)}, u32[]{:S(2)}, u32[]{:S(2)}) collective-permute-start(f32[512,256]{1,0:T(8,128)S(1)} %convolution_select_fusion.3), channel_id=1, source_target_pairs={{0,32},{16,48},{32,64},{48,80},{64,96},{80,112},{96,128},{112,144}... | collective-permute-start | bytes 1572872 | tf_op jit(solution)/shard_map/ppermute | solution.py:15
  136.7 11.2 %collective-permute-done.5 = f32[512,256]{1,0:T(8,128)S(1)} collective-permute-done((f32[512,256]{1,0:T(8,128)S(1)}, f32[512,256]{1,0:T(8,128)S(1)}, u32[]{:S(2)}, u32[]{:S(2)}) %collective-permute-start.5) | collective-permute-done | bytes 524320 | tf_op jit(solution)/shard_map/ppermute | solution.py:15
  149.8 9.3 %collective-permute-start.7 = (f32[512,256]{1,0:T(8,128)S(1)}, f32[512,256]{1,0:T(8,128)S(1)}, u32[]{:S(2)}, u32[]{:S(2)}) collective-permute-start(f32[512,256]{1,0:T(8,128)S(1)} %convolution_select_fusion.2), channel_id=1, source_target_pairs={{0,64},{16,80},{32,96},{48,112},{64,128},{80,144},{96,160},{112,17... | collective-permute-start | bytes 1572872 | tf_op jit(solution)/shard_map/ppermute | solution.py:15
  159.2 11.2 %collective-permute-done.7 = f32[512,256]{1,0:T(8,128)S(1)} collective-permute-done((f32[512,256]{1,0:T(8,128)S(1)}, f32[512,256]{1,0:T(8,128)S(1)}, u32[]{:S(2)}, u32[]{:S(2)}) %collective-permute-start.7) | collective-permute-done | bytes 524320 | tf_op jit(solution)/shard_map/ppermute | solution.py:15
  172.6 5.7 %collective-permute-start.9 = (f32[512,256]{1,0:T(8,128)S(1)}, f32[512,256]{1,0:T(8,128)S(1)}, u32[]{:S(2)}, u32[]{:S(2)}) collective-permute-start(f32[512,256]{1,0:T(8,128)S(1)} %convolution_select_fusion.1), channel_id=1, source_target_pairs={{0,128},{16,144},{32,160},{48,176},{64,192},{80,208},{96,224},{112... | collective-permute-start | bytes 1572872 | tf_op jit(solution)/shard_map/ppermute | solution.py:15
  178.3 11.2 %collective-permute-done.9 = f32[512,256]{1,0:T(8,128)S(1)} collective-permute-done((f32[512,256]{1,0:T(8,128)S(1)}, f32[512,256]{1,0:T(8,128)S(1)}, u32[]{:S(2)}, u32[]{:S(2)}) %collective-permute-start.9) | collective-permute-done | bytes 524320 | tf_op jit(solution)/shard_map/ppermute | solution.py:15
  193.3 4.8 %shard_map.28 = bf16[1,2048,512]{2,1,0:T(8,128)(2,1)} custom-call(s32[1]{0:T(128)} %bitcast.2.core_ref, bf16[1,2048,512]{2,1,0:T(8,128)(2,1)} %rows_ref.1, bf16[512,256]{1,0:T(8,128)(2,1)} %copy-done, bf16[512,256]{1,0:T(8,128)(2,1)} %copy-done.1), custom_call_target="tpu_custom_call" | custom-call | tf_op jit(solution)/shard_map/pallas_call | solution.py:98
  (60 shorter events, 35.3 us)
Async XLA Ops:
  4.7 25.8 %collective-permute-start = (bf16[1024,512]{1,0:T(8,128)(2,1)S(1)}, bf16[1024,512]{1,0:T(8,128)(2,1)S(1)}, u32[]{:S(2)}, u32[]{:S(2)}) collective-permute-start(bf16[1024,512]{1,0:T(8,128)(2,1)S(1)} %fusion.7), channel_id=1, source_target_pairs={{0,16},{16,32},{32,48},{48,64},{64,80},{80,96},{96,112},{112,128},... | collective-permute-start | bytes 3145736 | tf_op jit(solution)/shard_map/ppermute | solution.py:15
  31.2 3.2 %collective-permute-start.1 = (f32[256,512]{1,0:T(8,128)S(1)}, f32[256,512]{1,0:T(8,128)S(1)}, u32[]{:S(2)}, u32[]{:S(2)}) collective-permute-start(f32[256,512]{1,0:T(8,128)S(1)} %slice_select_fusion.1), channel_id=1, source_target_pairs={{0,1},{1,0},{2,3},{3,2},{4,5},{5,4},{6,7},{7,6},{8,9},{9,8},{10,11... | collective-permute-start | bytes 1572872 | tf_op jit(solution)/shard_map/ppermute | solution.py:20
  76.9 4.9 %collective-permute-start.2 = (f32[256,512]{1,0:T(8,128)S(1)}, f32[256,512]{1,0:T(8,128)S(1)}, u32[]{:S(2)}, u32[]{:S(2)}) collective-permute-start(f32[256,512]{1,0:T(8,128)S(1)} %bitcast.51), channel_id=1, source_target_pairs={{0,1},{1,0},{2,3},{3,2},{4,5},{5,4},{6,7},{7,6},{8,9},{9,8},{10,11... | collective-permute-start | bytes 1572872 | tf_op jit(solution)/shard_map/ppermute | solution.py:20
  113.7 15.0 %collective-permute-start.3 = (f32[512,256]{1,0:T(8,128)S(1)}, f32[512,256]{1,0:T(8,128)S(1)}, u32[]{:S(2)}, u32[]{:S(2)}) collective-permute-start(f32[512,256]{1,0:T(8,128)S(1)} %slice_select_fusion), channel_id=1, source_target_pairs={{0,16},{16,32},{32,48},{48,64},{64,80},{80,96},{96,112},{112,128},... | collective-permute-start | bytes 1572872 | tf_op jit(solution)/shard_map/ppermute | solution.py:15
  129.7 7.0 %collective-permute-start.4 = (f32[512,256]{1,0:T(8,128)S(1)}, f32[512,256]{1,0:T(8,128)S(1)}, u32[]{:S(2)}, u32[]{:S(2)}) collective-permute-start(f32[512,256]{1,0:T(8,128)S(1)} %convolution_select_fusion.3), channel_id=1, source_target_pairs={{0,1},{1,0},{2,3},{3,2},{4,5},{5,4},{6,7},{7,6},{8,9},{9,8},{10,11... | collective-permute-start | bytes 1572872 | tf_op jit(solution)/shard_map/ppermute | solution.py:20
  131.0 16.9 %collective-permute-start.5 = (f32[512,256]{1,0:T(8,128)S(1)}, f32[512,256]{1,0:T(8,128)S(1)}, u32[]{:S(2)}, u32[]{:S(2)}) collective-permute-start(f32[512,256]{1,0:T(8,128)S(1)} %convolution_select_fusion.3), channel_id=1, source_target_pairs={{0,32},{16,48},{32,64},{48,80},{64,96},{80,112},{96,128},{112,144}... | collective-permute-start | bytes 1572872 | tf_op jit(solution)/shard_map/ppermute | solution.py:15
  148.9 10.3 %collective-permute-start.6 = (f32[512,256]{1,0:T(8,128)S(1)}, f32[512,256]{1,0:T(8,128)S(1)}, u32[]{:S(2)}, u32[]{:S(2)}) collective-permute-start(f32[512,256]{1,0:T(8,128)S(1)} %convolution_select_fusion.2), channel_id=1, source_target_pairs={{0,1},{1,0},{2,3},{3,2},{4,5},{5,4},{6,7},{7,6},{8,9},{9,8},{10,11... | collective-permute-start | bytes 1572872 | tf_op jit(solution)/shard_map/ppermute | solution.py:20
  149.8 20.5 %collective-permute-start.7 = (f32[512,256]{1,0:T(8,128)S(1)}, f32[512,256]{1,0:T(8,128)S(1)}, u32[]{:S(2)}, u32[]{:S(2)}) collective-permute-start(f32[512,256]{1,0:T(8,128)S(1)} %convolution_select_fusion.2), channel_id=1, source_target_pairs={{0,64},{16,80},{32,96},{48,112},{64,128},{80,144},{96,160},{112,17... | collective-permute-start | bytes 1572872 | tf_op jit(solution)/shard_map/ppermute | solution.py:15
  171.4 6.9 %collective-permute-start.8 = (f32[512,256]{1,0:T(8,128)S(1)}, f32[512,256]{1,0:T(8,128)S(1)}, u32[]{:S(2)}, u32[]{:S(2)}) collective-permute-start(f32[512,256]{1,0:T(8,128)S(1)} %convolution_select_fusion.1), channel_id=1, source_target_pairs={{0,1},{1,0},{2,3},{3,2},{4,5},{5,4},{6,7},{7,6},{8,9},{9,8},{10,11... | collective-permute-start | bytes 1572872 | tf_op jit(solution)/shard_map/ppermute | solution.py:20
  172.6 16.9 %collective-permute-start.9 = (f32[512,256]{1,0:T(8,128)S(1)}, f32[512,256]{1,0:T(8,128)S(1)}, u32[]{:S(2)}, u32[]{:S(2)}) collective-permute-start(f32[512,256]{1,0:T(8,128)S(1)} %convolution_select_fusion.1), channel_id=1, source_target_pairs={{0,128},{16,144},{32,160},{48,176},{64,192},{80,208},{96,224},{112... | collective-permute-start | bytes 1572872 | tf_op jit(solution)/shard_map/ppermute | solution.py:15
  190.5 2.1 %copy-start = (bf16[512,256]{1,0:T(8,128)(2,1)}, bf16[512,256]{1,0:T(8,128)(2,1)S(1)}, u32[]{:S(2)}) copy-start(bf16[512,256]{1,0:T(8,128)(2,1)S(1)} %fusion.10.own_ref) | copy-start | bytes 786436
  190.5 2.1 %collective-permute-start.10 = (bf16[512,256]{1,0:T(8,128)(2,1)S(1)}, bf16[512,256]{1,0:T(8,128)(2,1)S(1)}, u32[]{:S(2)}, u32[]{:S(2)}) collective-permute-start(bf16[512,256]{1,0:T(8,128)(2,1)S(1)} %fusion.10.own_ref), channel_id=1, source_target_pairs={{0,1},{1,0},{2,3},{3,2},{4,5},{5,4},{6,7},{7,6},{8,9},{9,8},{10,11... | collective-permute-start | bytes 786440 | tf_op jit(solution)/shard_map/ppermute | solution.py:20
  192.6 0.7 copy-start.1

commit v11 on v5

--- a/solution.py
+++ b/solution.py
@@ -99,8 +99,15 @@
     core = lax.axis_index("core")
     row_index = lax.axis_index("z") * lax.axis_size("core") + core
     positions = anchor_rows - row_index * own_rows.shape[0]
-    own_slab = jnp.take(own_rows, positions, axis=0)
-    previous_slab = shifted(own_slab, "ver", 1)
+    table_index = jnp.arange(own_rows.shape[0], dtype=positions.dtype)[None, :]
+    own_parts, previous_parts = [], []
+    for part in jnp.split(positions, 2):
+        picks = (part[:, None] == table_index).astype(own_rows.dtype)
+        picked = jnp.dot(picks, own_rows, preferred_element_type=jnp.float32).astype(own_rows.dtype)
+        own_parts.append(picked)
+        previous_parts.append(shifted(picked, "ver", 1))
+    own_slab = jnp.concatenate(own_parts)
+    previous_slab = jnp.concatenate(previous_parts)
     partial_gram = lax.dot_general(
         own_slab, previous_slab, (((0,), (0,)), ((), ())), preferred_element_type=jnp.float32
     )

time: 202 us -> 197 us (0.975)
  waiting for transfers between devices: 70.4 us -> 63.9 us
  local copies, waits for them, and re-layouts: 7.41 us -> 1.57 us
  matrix products: 32.7 us -> 37 us
  starting transfers between devices: 38.2 us -> 42.2 us
    ppermute x5 -> x6, waiting for transfers between devices: 66.2 us -> 59.7 us  [shifted(): lax.ppermute(value, axis, [(source, source + steps) for source in range(c...]
    gather x1 -> x0, local copies, waits for them, and re-layouts: 5.85 us -> none  [per_device(): own_slab = jnp.take(own_rows, positions, axis=0)]
    dot_general x0 -> x2, matrix products: none -> 4.32 us  [per_device(): jnp.dot(picks, own_rows, preferred_element_type=jnp.float32)]
    ppermute x5 -> x6, starting transfers between devices: 28.9 us -> 31.9 us  [shifted(): lax.ppermute(value, axis, [(source, source + steps) for source in range(c...]
  transfers between devices with their start and end apart: 11 -> 12, of which waited for: 8 -> 9; matrix products, arithmetic and copies ran while one was open for 0% -> 1% of each run, Pallas kernels for 0% -> 0%
where the time goes in v11:
time: 197 us; the launch traced here: 196 us
  waiting for transfers between devices  63.9 us (32%)
  starting transfers between devices  42.2 us (21%)
  blocking collectives  42.2 us (21%)
  matrix products  37 us (19%)
  Pallas kernels  4.74 us (2%)
  other arithmetic  3.18 us (2%)
    ppermute x6, waiting for transfers between devices, shifted(): lax.ppermute(value, axis, [(source, source + steps) for source in range(c...  59.7 us
    ppermute x6, starting transfers between devices, shifted(): lax.ppermute(value, axis, [(source, source + steps) for source in range(c...  31.9 us
    all_to_all x1, blocking collectives, summed_over(): reduced = lax.all_to_all(pieces, axis, 0, 0, tiled=False).sum(0)  24.7 us
    all_to_all x1, blocking collectives, summed_over(): mine = lax.all_to_all(copies, axis, 0, 0, tiled=False).reshape(mine.shape)  17.5 us
    dot_general x12, matrix products, update(): return 1.5 * iterate - 0.5 * jnp.dot(iterate, square, precision=precision)  14 us
    dot_general x12, matrix products, update(): square = jnp.dot(iterate.T, iterate, precision=precision)  14 us
    ppermute x6, starting transfers between devices, swapped(): lax.ppermute(value, axis, [(source, source ^ mask) for source in range(co...  10.3 us
    pallas_call x1, Pallas kernels, aligned_rows(): pl.pallas_call(aligned_block, grid=(rows // block,), in_specs=[pl.BlockSp...  4.74 us
  transfers between devices with their start and end apart: 12, of which 9 were waited for; matrix products, arithmetic and copies ran while one was open for 1% of the time, Pallas kernels for 0%

profile of v11, /device:TPU:1, one launch (start us, length us, event | category | flops | bytes accessed | tf_op | source)
XLA Modules:
  0.0 196.2 jit_solution(236178938507022103)
XLA Ops:
  0.7 3.0 %fusion.13 = bf16[512,512]{1,0:T(8,128)(2,1)S(1)} fusion(bf16[1,2048,512]{2,1,0:T(8,128)(2,1)} %rows_ref.1, s32[512]{0:T(512)S(1)} %get-tuple-element.41), kind=kOutput, calls=%fused_computation.15 | convolution fusion | flops 1075052544 | bytes 2623488 | tf_op jit(solution)/shard_map/dot_general | solution.py:106
  3.7 4.0 %collective-permute-start = (bf16[512,512]{1,0:T(8,128)(2,1)S(1)}, bf16[512,512]{1,0:T(8,128)(2,1)S(1)}, u32[]{:S(2)}, u32[]{:S(2)}) collective-permute-start(bf16[512,512]{1,0:T(8,128)(2,1)S(1)} %fusion.13), channel_id=1, source_target_pairs={{0,16},{16,32},{32,48},{48,64},{64,80},{80,96},{96,112},{112,128},... | collective-permute-start | bytes 1572872 | tf_op jit(solution)/shard_map/ppermute | solution.py:14
  9.0 3.1 %collective-permute-start.1 = (bf16[512,512]{1,0:T(8,128)(2,1)S(1)}, bf16[512,512]{1,0:T(8,128)(2,1)S(1)}, u32[]{:S(2)}, u32[]{:S(2)}) collective-permute-start(bf16[512,512]{1,0:T(8,128)(2,1)S(1)} %fusion.10), channel_id=1, source_target_pairs={{0,16},{16,32},{32,48},{48,64},{64,80},{80,96},{96,112},{112,128},... | collective-permute-start | bytes 1572872 | tf_op jit(solution)/shard_map/ppermute | solution.py:14
  12.2 6.1 %collective-permute-done = bf16[512,512]{1,0:T(8,128)(2,1)S(1)} collective-permute-done((bf16[512,512]{1,0:T(8,128)(2,1)S(1)}, bf16[512,512]{1,0:T(8,128)(2,1)S(1)}, u32[]{:S(2)}, u32[]{:S(2)}) %collective-permute-start) | collective-permute-done | bytes 524320 | tf_op jit(solution)/shard_map/ppermute | solution.py:14
  18.3 11.2 %collective-permute-done.1 = bf16[512,512]{1,0:T(8,128)(2,1)S(1)} collective-permute-done((bf16[512,512]{1,0:T(8,128)(2,1)S(1)}, bf16[512,512]{1,0:T(8,128)(2,1)S(1)}, u32[]{:S(2)}, u32[]{:S(2)}) %collective-permute-start.1) | collective-permute-done | bytes 524320 | tf_op jit(solution)/shard_map/ppermute | solution.py:14
  33.6 24.7 %all_to_all.10 = f32[8,32,512]{2,1,0:T(8,128)S(1)} all-to-all(f32[8,32,512]{2,1,0:T(8,128)S(1)} %bitcast.55), channel_id=1, replica_groups=mesh['ver'=16,'z'=8,'core'=2] {'z'}, dimensions={0} | all-to-all | bytes 1048576 | tf_op jit(solution)/shard_map/all_to_all | solution.py:36
  58.4 17.5 %all_to_all.11 = f32[8,32,512]{2,1,0:T(8,128)S(1)} all-to-all(f32[8,32,512]{2,1,0:T(8,128)S(1)} %broadcast_in_dim.2), channel_id=1, replica_groups=mesh['ver'=16,'z'=8,'core'=2] {'z'}, dimensions={0} | all-to-all | bytes 1048576 | tf_op jit(solution)/shard_map/all_to_all | solution.py:38
  76.0 3.3 %collective-permute-start.3 = (f32[256,512]{1,0:T(8,128)S(1)}, f32[256,512]{1,0:T(8,128)S(1)}, u32[]{:S(2)}, u32[]{:S(2)}) collective-permute-start(f32[256,512]{1,0:T(8,128)S(1)} %bitcast.52), channel_id=1, source_target_pairs={{0,1},{1,0},{2,3},{3,2},{4,5},{5,4},{6,7},{7,6},{8,9},{9,8},{10,11... | collective-permute-start | bytes 1572872 | tf_op jit(solution)/shard_map/ppermute | solution.py:19
  83.0 21.6 %while.20 = (s32[]{:T(128)}, f32[512,512]{0,1:T(8,128)S(1)}, s32[]{:T(128)}) while((s32[]{:T(128)}, f32[512,512]{0,1:T(8,128)S(1)}, s32[]{:T(128)}) %tuple.33), condition=%wide.region_3.4_spmd, body=%wide.region_2.3_spmd.sunk | while | flops 1611399168 | bytes 7340077 | solution.py:117
  104.6 7.6 %while.21 = (s32[]{:T(128)}, f32[512,512]{0,1:T(8,128)S(1)}, s32[]{:T(128)}) while((s32[]{:T(128)}, f32[512,512]{0,1:T(8,128)S(1)}, s32[]{:T(128)}) %tuple.36), condition=%wide.region_5.6_spmd, body=%wide.region_4.5_spmd.sunk | while | flops 3222011904 | bytes 7340077 | solution.py:118
  104.7 1.9 fusion.85
  106.6 1.9 fusion.86
  108.5 1.9 fusion.85
  110.4 1.9 fusion.86
  112.8 4.1 %collective-permute-start.4 = (f32[512,256]{1,0:T(8,128)S(1)}, f32[512,256]{1,0:T(8,128)S(1)}, u32[]{:S(2)}, u32[]{:S(2)}) collective-permute-start(f32[512,256]{1,0:T(8,128)S(1)} %slice_select_fusion), channel_id=1, source_target_pairs={{0,16},{16,32},{32,48},{48,64},{64,80},{80,96},{96,112},{112,128},... | collective-permute-start | bytes 1572872 | tf_op jit(solution)/shard_map/ppermute | solution.py:14
  117.0 10.9 %collective-permute-done.4 = f32[512,256]{1,0:T(8,128)S(1)} collective-permute-done((f32[512,256]{1,0:T(8,128)S(1)}, f32[512,256]{1,0:T(8,128)S(1)}, u32[]{:S(2)}, u32[]{:S(2)}) %collective-permute-start.4) | collective-permute-done | bytes 524320 | tf_op jit(solution)/shard_map/ppermute | solution.py:14
  130.1 5.6 %collective-permute-start.6 = (f32[512,256]{1,0:T(8,128)S(1)}, f32[512,256]{1,0:T(8,128)S(1)}, u32[]{:S(2)}, u32[]{:S(2)}) collective-permute-start(f32[512,256]{1,0:T(8,128)S(1)} %convolution_select_fusion.3), channel_id=1, source_target_pairs={{0,32},{16,48},{32,64},{48,80},{64,96},{80,112},{96,128},{112,144}... | collective-permute-start | bytes 1572872 | tf_op jit(solution)/shard_map/ppermute | solution.py:14
  135.8 11.2 %collective-permute-done.6 = f32[512,256]{1,0:T(8,128)S(1)} collective-permute-done((f32[512,256]{1,0:T(8,128)S(1)}, f32[512,256]{1,0:T(8,128)S(1)}, u32[]{:S(2)}, u32[]{:S(2)}) %collective-permute-start.6) | collective-permute-done | bytes 524320 | tf_op jit(solution)/shard_map/ppermute | solution.py:14
  148.9 9.3 %collective-permute-start.8 = (f32[512,256]{1,0:T(8,128)S(1)}, f32[512,256]{1,0:T(8,128)S(1)}, u32[]{:S(2)}, u32[]{:S(2)}) collective-permute-start(f32[512,256]{1,0:T(8,128)S(1)} %convolution_select_fusion.2), channel_id=1, source_target_pairs={{0,64},{16,80},{32,96},{48,112},{64,128},{80,144},{96,160},{112,17... | collective-permute-start | bytes 1572872 | tf_op jit(solution)/shard_map/ppermute | solution.py:14
  158.3 11.2 %collective-permute-done.8 = f32[512,256]{1,0:T(8,128)S(1)} collective-permute-done((f32[512,256]{1,0:T(8,128)S(1)}, f32[512,256]{1,0:T(8,128)S(1)}, u32[]{:S(2)}, u32[]{:S(2)}) %collective-permute-start.8) | collective-permute-done | bytes 524320 | tf_op jit(solution)/shard_map/ppermute | solution.py:14
  170.5 5.8 %collective-permute-start.10 = (f32[512,256]{1,0:T(8,128)S(1)}, f32[512,256]{1,0:T(8,128)S(1)}, u32[]{:S(2)}, u32[]{:S(2)}) collective-permute-start(f32[512,256]{1,0:T(8,128)S(1)} %convolution_select_fusion.1), channel_id=1, source_target_pairs={{0,128},{16,144},{32,160},{48,176},{64,192},{80,208},{96,224},{112... | collective-permute-start | bytes 1572872 | tf_op jit(solution)/shard_map/ppermute | solution.py:14
  177.5 9.1 %collective-permute-done.10 = f32[512,256]{1,0:T(8,128)S(1)} collective-permute-done((f32[512,256]{1,0:T(8,128)S(1)}, f32[512,256]{1,0:T(8,128)S(1)}, u32[]{:S(2)}, u32[]{:S(2)}) %collective-permute-start.10) | collective-permute-done | bytes 524320 | tf_op jit(solution)/shard_map/ppermute | solution.py:14
  187.6 1.8 collective-permute-start.11
  191.5 4.7 %shard_map.28 = bf16[1,2048,512]{2,1,0:T(8,128)(2,1)} custom-call(bf16[1,2048,512]{2,1,0:T(8,128)(2,1)} %rows_ref.1, bf16[512,512]{1,0:T(8,128)(2,1)} %maximum_select_fusion.7.prefix_ref), custom_call_target="tpu_custom_call" | custom-call | tf_op jit(solution)/shard_map/pallas_call | solution.py:84
  (63 shorter events, 40.7 us)
Async XLA Ops:
  0.7 7.0 %copy-start = (bf16[1,2048,512]{2,1,0:T(8,128)(2,1)S(1)}, bf16[1,2048,512]{2,1,0:T(8,128)(2,1)}, u32[]{:S(2)}) copy-start(bf16[1,2048,512]{2,1,0:T(8,128)(2,1)} %rows_ref.1) | copy-start | bytes 6291460
  3.7 14.5 %collective-permute-start = (bf16[512,512]{1,0:T(8,128)(2,1)S(1)}, bf16[512,512]{1,0:T(8,128)(2,1)S(1)}, u32[]{:S(2)}, u32[]{:S(2)}) collective-permute-start(bf16[512,512]{1,0:T(8,128)(2,1)S(1)} %fusion.13), channel_id=1, source_target_pairs={{0,16},{16,32},{32,48},{48,64},{64,80},{80,96},{96,112},{112,128},... | collective-permute-start | bytes 1572872 | tf_op jit(solution)/shard_map/ppermute | solution.py:14
  9.0 20.5 %collective-permute-start.1 = (bf16[512,512]{1,0:T(8,128)(2,1)S(1)}, bf16[512,512]{1,0:T(8,128)(2,1)S(1)}, u32[]{:S(2)}, u32[]{:S(2)}) collective-permute-start(bf16[512,512]{1,0:T(8,128)(2,1)S(1)} %fusion.10), channel_id=1, source_target_pairs={{0,16},{16,32},{32,48},{48,64},{64,80},{80,96},{96,112},{112,128},... | collective-permute-start | bytes 1572872 | tf_op jit(solution)/shard_map/ppermute | solution.py:14
  30.3 3.2 %collective-permute-start.2 = (f32[256,512]{1,0:T(8,128)S(1)}, f32[256,512]{1,0:T(8,128)S(1)}, u32[]{:S(2)}, u32[]{:S(2)}) collective-permute-start(f32[256,512]{1,0:T(8,128)S(1)} %slice_select_fusion.1), channel_id=1, source_target_pairs={{0,1},{1,0},{2,3},{3,2},{4,5},{5,4},{6,7},{7,6},{8,9},{9,8},{10,11... | collective-permute-start | bytes 1572872 | tf_op jit(solution)/shard_map/ppermute | solution.py:19
  76.0 4.9 %collective-permute-start.3 = (f32[256,512]{1,0:T(8,128)S(1)}, f32[256,512]{1,0:T(8,128)S(1)}, u32[]{:S(2)}, u32[]{:S(2)}) collective-permute-start(f32[256,512]{1,0:T(8,128)S(1)} %bitcast.52), channel_id=1, source_target_pairs={{0,1},{1,0},{2,3},{3,2},{4,5},{5,4},{6,7},{7,6},{8,9},{9,8},{10,11... | collective-permute-start | bytes 1572872 | tf_op jit(solution)/shard_map/ppermute | solution.py:19
  112.8 15.0 %collective-permute-start.4 = (f32[512,256]{1,0:T(8,128)S(1)}, f32[512,256]{1,0:T(8,128)S(1)}, u32[]{:S(2)}, u32[]{:S(2)}) collective-permute-start(f32[512,256]{1,0:T(8,128)S(1)} %slice_select_fusion), channel_id=1, source_target_pairs={{0,16},{16,32},{32,48},{48,64},{64,80},{80,96},{96,112},{112,128},... | collective-permute-start | bytes 1572872 | tf_op jit(solution)/shard_map/ppermute | solution.py:14
  128.8 7.0 %collective-permute-start.5 = (f32[512,256]{1,0:T(8,128)S(1)}, f32[512,256]{1,0:T(8,128)S(1)}, u32[]{:S(2)}, u32[]{:S(2)}) collective-permute-start(f32[512,256]{1,0:T(8,128)S(1)} %convolution_select_fusion.3), channel_id=1, source_target_pairs={{0,1},{1,0},{2,3},{3,2},{4,5},{5,4},{6,7},{7,6},{8,9},{9,8},{10,11... | collective-permute-start | bytes 1572872 | tf_op jit(solution)/shard_map/ppermute | solution.py:19
  130.1 16.9 %collective-permute-start.6 = (f32[512,256]{1,0:T(8,128)S(1)}, f32[512,256]{1,0:T(8,128)S(1)}, u32[]{:S(2)}, u32[]{:S(2)}) collective-permute-start(f32[512,256]{1,0:T(8,128)S(1)} %convolution_select_fusion.3), channel_id=1, source_target_pairs={{0,32},{16,48},{32,64},{48,80},{64,96},{80,112},{96,128},{112,144}... | collective-permute-start | bytes 1572872 | tf_op jit(solution)/shard_map/ppermute | solution.py:14
  148.0 10.3 %collective-permute-start.7 = (f32[512,256]{1,0:T(8,128)S(1)}, f32[512,256]{1,0:T(8,128)S(1)}, u32[]{:S(2)}, u32[]{:S(2)}) collective-permute-start(f32[512,256]{1,0:T(8,128)S(1)} %convolution_select_fusion.2), channel_id=1, source_target_pairs={{0,1},{1,0},{2,3},{3,2},{4,5},{5,4},{6,7},{7,6},{8,9},{9,8},{10,11... | collective-permute-start | bytes 1572872 | tf_op jit(solution)/shard_map/ppermute | solution.py:19
  148.9 20.5 %collective-permute-start.8 = (f32[512,256]{1,0:T(8,128)S(1)}, f32[512,256]{1,0:T(8,128)S(1)}, u32[]{:S(2)}, u32[]{:S(2)}) collective-permute-start(f32[512,256]{1,0:T(8,128)S(1)} %convolution_select_fusion.2), channel_id=1, source_target_pairs={{0,64},{16,80},{32,96},{48,112},{64,128},{80,144},{96,160},{112,17... | collective-permute-start | bytes 1572872 | tf_op jit(solution)/shard_map/ppermute | solution.py:14
  170.5 16.1 %collective-permute-start.10 = (f32[512,256]{1,0:T(8,128)S(1)}, f32[512,256]{1,0:T(8,128)S(1)}, u32[]{:S(2)}, u32[]{:S(2)}) collective-permute-start(f32[512,256]{1,0:T(8,128)S(1)} %convolution_select_fusion.1), channel_id=1, source_target_pairs={{0,128},{16,144},{32,160},{48,176},{64,192},{80,208},{96,224},{112... | collective-permute-start | bytes 1572872 | tf_op jit(solution)/shard_map/ppermute | solution.py:14
  176.2 10.4 %collective-permute-start.9 = (f32[512,256]{1,0:T(8,128)S(1)}, f32[512,256]{1,0:T(8,128)S(1)}, u32[]{:S(2)}, u32[]{:S(2)}) collective-permute-start(f32[512,256]{1,0:T(8,128)S(1)} %convolution_select_fusion.1), channel_id=1, source_target_pairs={{0,1},{1,0},{2,3},{3,2},{4,5},{5,4},{6,7},{7,6},{8,9},{9,8},{10,11... | collective-permute-start | bytes 1572872 | tf_op jit(solution)/shard_map/ppermute | solution.py:19
  187.6 3.0 %collective-permute-start.11 = (bf16[512,256]{1,0:T(8,128)(2,1)S(1)}, bf16[512,256]{1,0:T(8,128)(2,1)S(1)}, u32[]{:S(2)}, u32[]{:S(2)}) collective-permute-start(bf16[512,256]{1,0:T(8,128)(2,1)S(1)} %fusion.16), channel_id=1, source_target_pairs={{0,1},{1,0},{2,3},{3,2},{4,5},{5,4},{6,7},{7,6},{8,9},{9,8},{10,11... | collective-permute-start | bytes 786440 | tf_op jit(solution)/shard_map/ppermute | solution.py:19

commit v12 on v11

--- a/solution.py
+++ b/solution.py
@@ -115,7 +115,9 @@
     frobenius = jnp.sqrt(jnp.sum(cross_gram * cross_gram) + 1e-06)
     iterate = cross_gram / frobenius
     iterate = lax.fori_loop(0, ROUGH_ITERS, newton_update(lax.Precision.HIGH), iterate)
-    rotation = lax.fori_loop(ROUGH_ITERS, ITERS, newton_update(HIGHEST), iterate)
+    for sweep_index in range(ROUGH_ITERS, ITERS):
+        iterate = newton_update(HIGHEST)(sweep_index, iterate)
+    rotation = iterate
     identity_matrix = jnp.eye(width, dtype=jnp.float32)
     rotation = jnp.where(lax.axis_index("ver") == 0, identity_matrix, rotation)
     own_low = running_product(rotation, "ver", core).astype(jnp.bfloat16)

time: 197 us -> 197 us (level)
  no operation moved by 1% of the time
where the time goes in v12:
time: 197 us; the launch traced here: 196 us
  waiting for transfers between devices  63.9 us (32%)
  starting transfers between devices  42.5 us (22%)
  blocking collectives  42.2 us (21%)
  matrix products  37.1 us (19%)
  Pallas kernels  4.74 us (2%)
  other arithmetic  3.06 us (2%)
    ppermute x6, waiting for transfers between devices, shifted(): lax.ppermute(value, axis, [(source, source + steps) for source in range(c...  59.7 us
    ppermute x6, starting transfers between devices, shifted(): lax.ppermute(value, axis, [(source, source + steps) for source in range(c...  31.9 us
    all_to_all x1, blocking collectives, summed_over(): reduced = lax.all_to_all(pieces, axis, 0, 0, tiled=False).sum(0)  24.7 us
    all_to_all x1, blocking collectives, summed_over(): mine = lax.all_to_all(copies, axis, 0, 0, tiled=False).reshape(mine.shape)  17.5 us
    dot_general x12, matrix products, update(): return 1.5 * iterate - 0.5 * jnp.dot(iterate, square, precision=precision)  14 us
    dot_general x12, matrix products, update(): square = jnp.dot(iterate.T, iterate, precision=precision)  14 us
    ppermute x6, starting transfers between devices, swapped(): lax.ppermute(value, axis, [(source, source ^ mask) for source in range(co...  10.5 us
    pallas_call x1, Pallas kernels, aligned_rows(): pl.pallas_call(aligned_block, grid=(rows // block,), in_specs=[pl.BlockSp...  4.74 us
  transfers between devices with their start and end apart: 12, of which 9 were waited for; matrix products, arithmetic and copies ran while one was open for 1% of the time, Pallas kernels for 0%

profile of v12, /device:TPU:1, one launch (start us, length us, event | category | flops | bytes accessed | tf_op | source)
XLA Modules:
  0.0 196.2 jit_solution(14171515787518461286)
XLA Ops:
  0.7 3.0 %fusion.14 = bf16[512,512]{1,0:T(8,128)(2,1)S(1)} fusion(bf16[1,2048,512]{2,1,0:T(8,128)(2,1)} %rows_ref.1, s32[512]{0:T(512)S(1)} %get-tuple-element.24), kind=kOutput, calls=%fused_computation.17 | convolution fusion | flops 1075052544 | bytes 2623488 | tf_op jit(solution)/shard_map/dot_general | solution.py:106
  3.7 4.0 %collective-permute-start = (bf16[512,512]{1,0:T(8,128)(2,1)S(1)}, bf16[512,512]{1,0:T(8,128)(2,1)S(1)}, u32[]{:S(2)}, u32[]{:S(2)}) collective-permute-start(bf16[512,512]{1,0:T(8,128)(2,1)S(1)} %fusion.14), channel_id=1, source_target_pairs={{0,16},{16,32},{32,48},{48,64},{64,80},{80,96},{96,112},{112,128},... | collective-permute-start | bytes 1572872 | tf_op jit(solution)/shard_map/ppermute | solution.py:14
  9.0 3.1 %collective-permute-start.1 = (bf16[512,512]{1,0:T(8,128)(2,1)S(1)}, bf16[512,512]{1,0:T(8,128)(2,1)S(1)}, u32[]{:S(2)}, u32[]{:S(2)}) collective-permute-start(bf16[512,512]{1,0:T(8,128)(2,1)S(1)} %fusion.11), channel_id=1, source_target_pairs={{0,16},{16,32},{32,48},{48,64},{64,80},{80,96},{96,112},{112,128},... | collective-permute-start | bytes 1572872 | tf_op jit(solution)/shard_map/ppermute | solution.py:14
  12.2 6.1 %collective-permute-done = bf16[512,512]{1,0:T(8,128)(2,1)S(1)} collective-permute-done((bf16[512,512]{1,0:T(8,128)(2,1)S(1)}, bf16[512,512]{1,0:T(8,128)(2,1)S(1)}, u32[]{:S(2)}, u32[]{:S(2)}) %collective-permute-start) | collective-permute-done | bytes 524320 | tf_op jit(solution)/shard_map/ppermute | solution.py:14
  18.3 11.2 %collective-permute-done.1 = bf16[512,512]{1,0:T(8,128)(2,1)S(1)} collective-permute-done((bf16[512,512]{1,0:T(8,128)(2,1)S(1)}, bf16[512,512]{1,0:T(8,128)(2,1)S(1)}, u32[]{:S(2)}, u32[]{:S(2)}) %collective-permute-start.1) | collective-permute-done | bytes 524320 | tf_op jit(solution)/shard_map/ppermute | solution.py:14
  30.3 1.6 collective-permute-start.2
  33.6 24.7 %all_to_all.10 = f32[8,32,512]{2,1,0:T(8,128)S(1)} all-to-all(f32[8,32,512]{2,1,0:T(8,128)S(1)} %bitcast.45), channel_id=1, replica_groups=mesh['ver'=16,'z'=8,'core'=2] {'z'}, dimensions={0} | all-to-all | bytes 1048576 | tf_op jit(solution)/shard_map/all_to_all | solution.py:36
  58.4 17.5 %all_to_all.11 = f32[8,32,512]{2,1,0:T(8,128)S(1)} all-to-all(f32[8,32,512]{2,1,0:T(8,128)S(1)} %broadcast_in_dim.2), channel_id=1, replica_groups=mesh['ver'=16,'z'=8,'core'=2] {'z'}, dimensions={0} | all-to-all | bytes 1048576 | tf_op jit(solution)/shard_map/all_to_all | solution.py:38
  76.0 3.3 %collective-permute-start.3 = (f32[256,512]{1,0:T(8,128)S(1)}, f32[256,512]{1,0:T(8,128)S(1)}, u32[]{:S(2)}, u32[]{:S(2)}) collective-permute-start(f32[256,512]{1,0:T(8,128)S(1)} %bitcast.42), channel_id=1, source_target_pairs={{0,1},{1,0},{2,3},{3,2},{4,5},{5,4},{6,7},{7,6},{8,9},{9,8},{10,11... | collective-permute-start | bytes 1572872 | tf_op jit(solution)/shard_map/ppermute | solution.py:19
  83.0 21.6 %while.10 = (s32[]{:T(128)}, f32[512,512]{0,1:T(8,128)S(1)}, s32[]{:T(128)}) while((s32[]{:T(128)}, f32[512,512]{0,1:T(8,128)S(1)}, s32[]{:T(128)}) %tuple.20), condition=%wide.region_3.4_spmd, body=%wide.region_2.3_spmd.sunk | while | flops 1611399168 | bytes 7340077 | solution.py:117
  104.9 1.9 fusion.50
  106.8 1.9 fusion.9
  108.7 1.9 fusion.51
  110.5 1.9 fusion.10
  112.5 4.1 %collective-permute-start.4 = (f32[512,256]{1,0:T(8,128)S(1)}, f32[512,256]{1,0:T(8,128)S(1)}, u32[]{:S(2)}, u32[]{:S(2)}) collective-permute-start(f32[512,256]{1,0:T(8,128)S(1)} %slice_select_fusion), channel_id=1, source_target_pairs={{0,16},{16,32},{32,48},{48,64},{64,80},{80,96},{96,112},{112,128},... | collective-permute-start | bytes 1572872 | tf_op jit(solution)/shard_map/ppermute | solution.py:14
  116.7 10.8 %collective-permute-done.4 = f32[512,256]{1,0:T(8,128)S(1)} collective-permute-done((f32[512,256]{1,0:T(8,128)S(1)}, f32[512,256]{1,0:T(8,128)S(1)}, u32[]{:S(2)}, u32[]{:S(2)}) %collective-permute-start.4) | collective-permute-done | bytes 524320 | tf_op jit(solution)/shard_map/ppermute | solution.py:14
  130.1 5.6 %collective-permute-start.6 = (f32[512,256]{1,0:T(8,128)S(1)}, f32[512,256]{1,0:T(8,128)S(1)}, u32[]{:S(2)}, u32[]{:S(2)}) collective-permute-start(f32[512,256]{1,0:T(8,128)S(1)} %convolution_select_fusion.3), channel_id=1, source_target_pairs={{0,32},{16,48},{32,64},{48,80},{64,96},{80,112},{96,128},{112,144}... | collective-permute-start | bytes 1572872 | tf_op jit(solution)/shard_map/ppermute | solution.py:14
  135.7 11.2 %collective-permute-done.6 = f32[512,256]{1,0:T(8,128)S(1)} collective-permute-done((f32[512,256]{1,0:T(8,128)S(1)}, f32[512,256]{1,0:T(8,128)S(1)}, u32[]{:S(2)}, u32[]{:S(2)}) %collective-permute-start.6) | collective-permute-done | bytes 524320 | tf_op jit(solution)/shard_map/ppermute | solution.py:14
  148.9 9.3 %collective-permute-start.8 = (f32[512,256]{1,0:T(8,128)S(1)}, f32[512,256]{1,0:T(8,128)S(1)}, u32[]{:S(2)}, u32[]{:S(2)}) collective-permute-start(f32[512,256]{1,0:T(8,128)S(1)} %convolution_select_fusion.2), channel_id=1, source_target_pairs={{0,64},{16,80},{32,96},{48,112},{64,128},{80,144},{96,160},{112,17... | collective-permute-start | bytes 1572872 | tf_op jit(solution)/shard_map/ppermute | solution.py:14
  158.2 11.2 %collective-permute-done.8 = f32[512,256]{1,0:T(8,128)S(1)} collective-permute-done((f32[512,256]{1,0:T(8,128)S(1)}, f32[512,256]{1,0:T(8,128)S(1)}, u32[]{:S(2)}, u32[]{:S(2)}) %collective-permute-start.8) | collective-permute-done | bytes 524320 | tf_op jit(solution)/shard_map/ppermute | solution.py:14
  170.4 5.8 %collective-permute-start.10 = (f32[512,256]{1,0:T(8,128)S(1)}, f32[512,256]{1,0:T(8,128)S(1)}, u32[]{:S(2)}, u32[]{:S(2)}) collective-permute-start(f32[512,256]{1,0:T(8,128)S(1)} %convolution_select_fusion.1), channel_id=1, source_target_pairs={{0,128},{16,144},{32,160},{48,176},{64,192},{80,208},{96,224},{112... | collective-permute-start | bytes 1572872 | tf_op jit(solution)/shard_map/ppermute | solution.py:14
  177.4 9.1 %collective-permute-done.10 = f32[512,256]{1,0:T(8,128)S(1)} collective-permute-done((f32[512,256]{1,0:T(8,128)S(1)}, f32[512,256]{1,0:T(8,128)S(1)}, u32[]{:S(2)}, u32[]{:S(2)}) %collective-permute-start.10) | collective-permute-done | bytes 524320 | tf_op jit(solution)/shard_map/ppermute | solution.py:14
  187.5 1.8 collective-permute-start.11
  191.4 4.7 %shard_map.28 = bf16[1,2048,512]{2,1,0:T(8,128)(2,1)} custom-call(bf16[1,2048,512]{2,1,0:T(8,128)(2,1)} %rows_ref.1, bf16[512,512]{1,0:T(8,128)(2,1)} %maximum_select_fusion.7.prefix_ref), custom_call_target="tpu_custom_call" | custom-call | tf_op jit(solution)/shard_map/pallas_call | solution.py:84
  (59 shorter events, 39.0 us)
Async XLA Ops:
  0.7 7.0 %copy-start = (bf16[1,2048,512]{2,1,0:T(8,128)(2,1)S(1)}, bf16[1,2048,512]{2,1,0:T(8,128)(2,1)}, u32[]{:S(2)}) copy-start(bf16[1,2048,512]{2,1,0:T(8,128)(2,1)} %rows_ref.1) | copy-start | bytes 6291460
  3.7 14.5 %collective-permute-start = (bf16[512,512]{1,0:T(8,128)(2,1)S(1)}, bf16[512,512]{1,0:T(8,128)(2,1)S(1)}, u32[]{:S(2)}, u32[]{:S(2)}) collective-permute-start(bf16[512,512]{1,0:T(8,128)(2,1)S(1)} %fusion.14), channel_id=1, source_target_pairs={{0,16},{16,32},{32,48},{48,64},{64,80},{80,96},{96,112},{112,128},... | collective-permute-start | bytes 1572872 | tf_op jit(solution)/shard_map/ppermute | solution.py:14
  9.0 20.5 %collective-permute-start.1 = (bf16[512,512]{1,0:T(8,128)(2,1)S(1)}, bf16[512,512]{1,0:T(8,128)(2,1)S(1)}, u32[]{:S(2)}, u32[]{:S(2)}) collective-permute-start(bf16[512,512]{1,0:T(8,128)(2,1)S(1)} %fusion.11), channel_id=1, source_target_pairs={{0,16},{16,32},{32,48},{48,64},{64,80},{80,96},{96,112},{112,128},... | collective-permute-start | bytes 1572872 | tf_op jit(solution)/shard_map/ppermute | solution.py:14
  30.3 3.2 %collective-permute-start.2 = (f32[256,512]{1,0:T(8,128)S(1)}, f32[256,512]{1,0:T(8,128)S(1)}, u32[]{:S(2)}, u32[]{:S(2)}) collective-permute-start(f32[256,512]{1,0:T(8,128)S(1)} %slice_select_fusion.1), channel_id=1, source_target_pairs={{0,1},{1,0},{2,3},{3,2},{4,5},{5,4},{6,7},{7,6},{8,9},{9,8},{10,11... | collective-permute-start | bytes 1572872 | tf_op jit(solution)/shard_map/ppermute | solution.py:19
  76.0 4.9 %collective-permute-start.3 = (f32[256,512]{1,0:T(8,128)S(1)}, f32[256,512]{1,0:T(8,128)S(1)}, u32[]{:S(2)}, u32[]{:S(2)}) collective-permute-start(f32[256,512]{1,0:T(8,128)S(1)} %bitcast.42), channel_id=1, source_target_pairs={{0,1},{1,0},{2,3},{3,2},{4,5},{5,4},{6,7},{7,6},{8,9},{9,8},{10,11... | collective-permute-start | bytes 1572872 | tf_op jit(solution)/shard_map/ppermute | solution.py:19
  112.5 15.0 %collective-permute-start.4 = (f32[512,256]{1,0:T(8,128)S(1)}, f32[512,256]{1,0:T(8,128)S(1)}, u32[]{:S(2)}, u32[]{:S(2)}) collective-permute-start(f32[512,256]{1,0:T(8,128)S(1)} %slice_select_fusion), channel_id=1, source_target_pairs={{0,16},{16,32},{32,48},{48,64},{64,80},{80,96},{96,112},{112,128},... | collective-permute-start | bytes 1572872 | tf_op jit(solution)/shard_map/ppermute | solution.py:14
  128.5 7.2 %collective-permute-start.5 = (f32[512,256]{1,0:T(8,128)S(1)}, f32[512,256]{1,0:T(8,128)S(1)}, u32[]{:S(2)}, u32[]{:S(2)}) collective-permute-start(f32[512,256]{1,0:T(8,128)S(1)} %convolution_select_fusion.3), channel_id=1, source_target_pairs={{0,1},{1,0},{2,3},{3,2},{4,5},{5,4},{6,7},{7,6},{8,9},{9,8},{10,11... | collective-permute-start | bytes 1572872 | tf_op jit(solution)/shard_map/ppermute | solution.py:19
  130.1 16.9 %collective-permute-start.6 = (f32[512,256]{1,0:T(8,128)S(1)}, f32[512,256]{1,0:T(8,128)S(1)}, u32[]{:S(2)}, u32[]{:S(2)}) collective-permute-start(f32[512,256]{1,0:T(8,128)S(1)} %convolution_select_fusion.3), channel_id=1, source_target_pairs={{0,32},{16,48},{32,64},{48,80},{64,96},{80,112},{96,128},{112,144}... | collective-permute-start | bytes 1572872 | tf_op jit(solution)/shard_map/ppermute | solution.py:14
  147.9 10.3 %collective-permute-start.7 = (f32[512,256]{1,0:T(8,128)S(1)}, f32[512,256]{1,0:T(8,128)S(1)}, u32[]{:S(2)}, u32[]{:S(2)}) collective-permute-start(f32[512,256]{1,0:T(8,128)S(1)} %convolution_select_fusion.2), channel_id=1, source_target_pairs={{0,1},{1,0},{2,3},{3,2},{4,5},{5,4},{6,7},{7,6},{8,9},{9,8},{10,11... | collective-permute-start | bytes 1572872 | tf_op jit(solution)/shard_map/ppermute | solution.py:19
  148.9 20.5 %collective-permute-start.8 = (f32[512,256]{1,0:T(8,128)S(1)}, f32[512,256]{1,0:T(8,128)S(1)}, u32[]{:S(2)}, u32[]{:S(2)}) collective-permute-start(f32[512,256]{1,0:T(8,128)S(1)} %convolution_select_fusion.2), channel_id=1, source_target_pairs={{0,64},{16,80},{32,96},{48,112},{64,128},{80,144},{96,160},{112,17... | collective-permute-start | bytes 1572872 | tf_op jit(solution)/shard_map/ppermute | solution.py:14
  170.4 16.1 %collective-permute-start.10 = (f32[512,256]{1,0:T(8,128)S(1)}, f32[512,256]{1,0:T(8,128)S(1)}, u32[]{:S(2)}, u32[]{:S(2)}) collective-permute-start(f32[512,256]{1,0:T(8,128)S(1)} %convolution_select_fusion.1), channel_id=1, source_target_pairs={{0,128},{16,144},{32,160},{48,176},{64,192},{80,208},{96,224},{112... | collective-permute-start | bytes 1572872 | tf_op jit(solution)/shard_map/ppermute | solution.py:14
  176.2 10.4 %collective-permute-start.9 = (f32[512,256]{1,0:T(8,128)S(1)}, f32[512,256]{1,0:T(8,128)S(1)}, u32[]{:S(2)}, u32[]{:S(2)}) collective-permute-start(f32[512,256]{1,0:T(8,128)S(1)} %convolution_select_fusion.1), channel_id=1, source_target_pairs={{0,1},{1,0},{2,3},{3,2},{4,5},{5,4},{6,7},{7,6},{8,9},{9,8},{10,11... | collective-permute-start | bytes 1572872 | tf_op jit(solution)/shard_map/ppermute | solution.py:19
  187.5 3.0 %collective-permute-start.11 = (bf16[512,256]{1,0:T(8,128)(2,1)S(1)}, bf16[512,256]{1,0:T(8,128)(2,1)S(1)}, u32[]{:S(2)}, u32[]{:S(2)}) collective-permute-start(bf16[512,256]{1,0:T(8,128)(2,1)S(1)} %fusion.17), channel_id=1, source_target_pairs={{0,1},{1,0},{2,3},{3,2},{4,5},{5,4},{6,7},{7,6},{8,9},{9,8},{10,11... | collective-permute-start | bytes 786440 | tf_op jit(solution)/shard_map/ppermute | solution.py:19

commit v13 on v12

--- a/solution.py
+++ b/solution.py
@@ -101,7 +101,7 @@
     positions = anchor_rows - row_index * own_rows.shape[0]
     table_index = jnp.arange(own_rows.shape[0], dtype=positions.dtype)[None, :]
     own_parts, previous_parts = [], []
-    for part in jnp.split(positions, 2):
+    for part in jnp.split(positions, 4):
         picks = (part[:, None] == table_index).astype(own_rows.dtype)
         picked = jnp.dot(picks, own_rows, preferred_element_type=jnp.float32).astype(own_rows.dtype)
         own_parts.append(picked)

time: 197 us -> 197 us (level)
  waiting for transfers between devices: 63.9 us -> 56.4 us
  starting transfers between devices: 42.5 us -> 48.3 us
  matrix products: 37.1 us -> 39.1 us
    ppermute x6 -> x8, waiting for transfers between devices: 59.7 us -> 52.2 us  [shifted(): lax.ppermute(value, axis, [(source, source + steps) for source in range(c...]
    ppermute x6 -> x8, starting transfers between devices: 31.9 us -> 37.8 us  [shifted(): lax.ppermute(value, axis, [(source, source + steps) for source in range(c...]
    dot_general x2 -> x4, matrix products: 4.32 us -> 5.3 us  [per_device(): jnp.dot(picks, own_rows, preferred_element_type=jnp.float32)]
  transfers between devices with their start and end apart: 12 -> 14, of which waited for: 9 -> 9; matrix products, arithmetic and copies ran while one was open for 1% -> 2% of each run, Pallas kernels for 0% -> 0%
where the time goes in v13:
time: 197 us
  waiting for transfers between devices  56.4 us (29%)
  starting transfers between devices  48.3 us (25%)
  blocking collectives  42.2 us (21%)
  matrix products  39.1 us (20%)
  Pallas kernels  4.74 us (2%)
  other arithmetic  3.17 us (2%)
    ppermute x8, waiting for transfers between devices, shifted(): lax.ppermute(value, axis, [(source, source + steps) for source in range(c...  52.2 us
    ppermute x8, starting transfers between devices, shifted(): lax.ppermute(value, axis, [(source, source + steps) for source in range(c...  37.8 us
    all_to_all x1, blocking collectives, summed_over(): reduced = lax.all_to_all(pieces, axis, 0, 0, tiled=False).sum(0)  24.7 us
    all_to_all x1, blocking collectives, summed_over(): mine = lax.all_to_all(copies, axis, 0, 0, tiled=False).reshape(mine.shape)  17.5 us
    dot_general x12, matrix products, update(): return 1.5 * iterate - 0.5 * jnp.dot(iterate, square, precision=precision)  14 us
    dot_general x12, matrix products, update(): square = jnp.dot(iterate.T, iterate, precision=precision)  14 us
    ppermute x6, starting transfers between devices, swapped(): lax.ppermute(value, axis, [(source, source ^ mask) for source in range(co...  10.5 us
    dot_general x4, matrix products, per_device(): jnp.dot(picks, own_rows, preferred_element_type=jnp.float32)  5.3 us
  transfers between devices with their start and end apart: 14, of which 9 were waited for; matrix products, arithmetic and copies ran while one was open for 2% of the time, Pallas kernels for 0%

profile of v13, /device:TPU:1, one launch (start us, length us, event | category | flops | bytes accessed | tf_op | source)
XLA Modules:
  0.0 196.6 jit_solution(9662574800794955786)
XLA Ops:
  0.8 2.3 %fusion.13 = bf16[256,512]{1,0:T(8,128)(2,1)S(1)} fusion(bf16[1,2048,512]{2,1,0:T(8,128)(2,1)} %rows_ref.1, s32[256]{0:T(256)S(1)} %get-tuple-element.24), kind=kOutput, calls=%fused_computation.24 | convolution fusion | flops 537526272 | bytes 2360320 | tf_op jit(solution)/shard_map/dot_general | solution.py:106
  3.2 3.9 %collective-permute-start = (bf16[256,512]{1,0:T(8,128)(2,1)S(1)}, bf16[256,512]{1,0:T(8,128)(2,1)S(1)}, u32[]{:S(2)}, u32[]{:S(2)}) collective-permute-start(bf16[256,512]{1,0:T(8,128)(2,1)S(1)} %fusion.13), channel_id=1, source_target_pairs={{0,16},{16,32},{32,48},{48,64},{64,80},{80,96},{96,112},{112,128},... | collective-permute-start | bytes 786440 | tf_op jit(solution)/shard_map/ppermute | solution.py:14
  7.9 3.1 %collective-permute-start.1 = (bf16[256,512]{1,0:T(8,128)(2,1)S(1)}, bf16[256,512]{1,0:T(8,128)(2,1)S(1)}, u32[]{:S(2)}, u32[]{:S(2)}) collective-permute-start(bf16[256,512]{1,0:T(8,128)(2,1)S(1)} %fusion.16), channel_id=1, source_target_pairs={{0,16},{16,32},{32,48},{48,64},{64,80},{80,96},{96,112},{112,128},... | collective-permute-start | bytes 786440 | tf_op jit(solution)/shard_map/ppermute | solution.py:14
  11.8 3.5 %collective-permute-start.2 = (bf16[256,512]{1,0:T(8,128)(2,1)S(1)}, bf16[256,512]{1,0:T(8,128)(2,1)}, u32[]{:S(2)}, u32[]{:S(2)}) collective-permute-start(bf16[256,512]{1,0:T(8,128)(2,1)S(1)} %fusion.19), channel_id=1, source_target_pairs={{0,16},{16,32},{32,48},{48,64},{64,80},{80,96},{96,112},{112,128},... | collective-permute-start | bytes 786440 | tf_op jit(solution)/shard_map/ppermute | solution.py:14
  16.8 2.4 %collective-permute-start.3 = (bf16[256,512]{1,0:T(8,128)(2,1)}, bf16[256,512]{1,0:T(8,128)(2,1)S(1)}, u32[]{:S(2)}, u32[]{:S(2)}) collective-permute-start(bf16[256,512]{1,0:T(8,128)(2,1)} %fusion.22), channel_id=1, source_target_pairs={{0,16},{16,32},{32,48},{48,64},{64,80},{80,96},{96,112},{112,128},... | collective-permute-start | bytes 786440 | tf_op jit(solution)/shard_map/ppermute | solution.py:14
  19.2 4.1 %collective-permute-done.2 = bf16[256,512]{1,0:T(8,128)(2,1)} collective-permute-done((bf16[256,512]{1,0:T(8,128)(2,1)S(1)}, bf16[256,512]{1,0:T(8,128)(2,1)}, u32[]{:S(2)}, u32[]{:S(2)}) %collective-permute-start.2) | collective-permute-done | bytes 262176 | tf_op jit(solution)/shard_map/ppermute | solution.py:14
  23.3 5.7 %collective-permute-done.3 = bf16[256,512]{1,0:T(8,128)(2,1)S(1)} collective-permute-done((bf16[256,512]{1,0:T(8,128)(2,1)}, bf16[256,512]{1,0:T(8,128)(2,1)S(1)}, u32[]{:S(2)}, u32[]{:S(2)}) %collective-permute-start.3) | collective-permute-done | bytes 262176 | tf_op jit(solution)/shard_map/ppermute | solution.py:14
  34.2 24.7 %all_to_all.10 = f32[8,32,512]{2,1,0:T(8,128)S(1)} all-to-all(f32[8,32,512]{2,1,0:T(8,128)S(1)} %bitcast.53), channel_id=1, replica_groups=mesh['ver'=16,'z'=8,'core'=2] {'z'}, dimensions={0} | all-to-all | bytes 1048576 | tf_op jit(solution)/shard_map/all_to_all | solution.py:36
  59.0 17.5 %all_to_all.11 = f32[8,32,512]{2,1,0:T(8,128)S(1)} all-to-all(f32[8,32,512]{2,1,0:T(8,128)S(1)} %broadcast_in_dim.2), channel_id=1, replica_groups=mesh['ver'=16,'z'=8,'core'=2] {'z'}, dimensions={0} | all-to-all | bytes 1048576 | tf_op jit(solution)/shard_map/all_to_all | solution.py:38
  76.6 3.3 %collective-permute-start.5 = (f32[256,512]{1,0:T(8,128)S(1)}, f32[256,512]{1,0:T(8,128)S(1)}, u32[]{:S(2)}, u32[]{:S(2)}) collective-permute-start(f32[256,512]{1,0:T(8,128)S(1)} %bitcast.50), channel_id=1, source_target_pairs={{0,1},{1,0},{2,3},{3,2},{4,5},{5,4},{6,7},{7,6},{8,9},{9,8},{10,11... | collective-permute-start | bytes 1572872 | tf_op jit(solution)/shard_map/ppermute | solution.py:19
  83.5 21.6 %while.10 = (s32[]{:T(128)}, f32[512,512]{0,1:T(8,128)S(1)}, s32[]{:T(128)}) while((s32[]{:T(128)}, f32[512,512]{0,1:T(8,128)S(1)}, s32[]{:T(128)}) %tuple.22), condition=%wide.region_3.4_spmd, body=%wide.region_2.3_spmd.sunk | while | flops 1611399168 | bytes 7340077 | solution.py:117
  105.5 1.9 fusion.70
  107.4 1.9 fusion.11
  109.3 1.9 fusion.71
  111.1 1.9 fusion.12
  113.1 4.0 %collective-permute-start.6 = (f32[512,256]{1,0:T(8,128)S(1)}, f32[512,256]{1,0:T(8,128)S(1)}, u32[]{:S(2)}, u32[]{:S(2)}) collective-permute-start(f32[512,256]{1,0:T(8,128)S(1)} %slice_select_fusion), channel_id=1, source_target_pairs={{0,16},{16,32},{32,48},{48,64},{64,80},{80,96},{96,112},{112,128},... | collective-permute-start | bytes 1572872 | tf_op jit(solution)/shard_map/ppermute | solution.py:14
  117.1 10.9 %collective-permute-done.6 = f32[512,256]{1,0:T(8,128)S(1)} collective-permute-done((f32[512,256]{1,0:T(8,128)S(1)}, f32[512,256]{1,0:T(8,128)S(1)}, u32[]{:S(2)}, u32[]{:S(2)}) %collective-permute-start.6) | collective-permute-done | bytes 524320 | tf_op jit(solution)/shard_map/ppermute | solution.py:14
  130.5 5.7 %collective-permute-start.8 = (f32[512,256]{1,0:T(8,128)S(1)}, f32[512,256]{1,0:T(8,128)S(1)}, u32[]{:S(2)}, u32[]{:S(2)}) collective-permute-start(f32[512,256]{1,0:T(8,128)S(1)} %convolution_select_fusion.3), channel_id=1, source_target_pairs={{0,32},{16,48},{32,64},{48,80},{64,96},{80,112},{96,128},{112,144}... | collective-permute-start | bytes 1572872 | tf_op jit(solution)/shard_map/ppermute | solution.py:14
  136.2 11.2 %collective-permute-done.8 = f32[512,256]{1,0:T(8,128)S(1)} collective-permute-done((f32[512,256]{1,0:T(8,128)S(1)}, f32[512,256]{1,0:T(8,128)S(1)}, u32[]{:S(2)}, u32[]{:S(2)}) %collective-permute-start.8) | collective-permute-done | bytes 524320 | tf_op jit(solution)/shard_map/ppermute | solution.py:14
  148.4 9.3 %collective-permute-start.10 = (f32[512,256]{1,0:T(8,128)S(1)}, f32[512,256]{1,0:T(8,128)S(1)}, u32[]{:S(2)}, u32[]{:S(2)}) collective-permute-start(f32[512,256]{1,0:T(8,128)S(1)} %convolution_select_fusion.2), channel_id=1, source_target_pairs={{0,64},{16,80},{32,96},{48,112},{64,128},{80,144},{96,160},{112,17... | collective-permute-start | bytes 1572872 | tf_op jit(solution)/shard_map/ppermute | solution.py:14
  159.0 9.1 %collective-permute-done.10 = f32[512,256]{1,0:T(8,128)S(1)} collective-permute-done((f32[512,256]{1,0:T(8,128)S(1)}, f32[512,256]{1,0:T(8,128)S(1)}, u32[]{:S(2)}, u32[]{:S(2)}) %collective-permute-start.10) | collective-permute-done | bytes 524320 | tf_op jit(solution)/shard_map/ppermute | solution.py:14
  170.9 5.7 %collective-permute-start.12 = (f32[512,256]{1,0:T(8,128)S(1)}, f32[512,256]{1,0:T(8,128)S(1)}, u32[]{:S(2)}, u32[]{:S(2)}) collective-permute-start(f32[512,256]{1,0:T(8,128)S(1)} %convolution_select_fusion.1), channel_id=1, source_target_pairs={{0,128},{16,144},{32,160},{48,176},{64,192},{80,208},{96,224},{112... | collective-permute-start | bytes 1572872 | tf_op jit(solution)/shard_map/ppermute | solution.py:14
  176.7 11.2 %collective-permute-done.12 = f32[512,256]{1,0:T(8,128)S(1)} collective-permute-done((f32[512,256]{1,0:T(8,128)S(1)}, f32[512,256]{1,0:T(8,128)S(1)}, u32[]{:S(2)}, u32[]{:S(2)}) %collective-permute-start.12) | collective-permute-done | bytes 524320 | tf_op jit(solution)/shard_map/ppermute | solution.py:14
  191.9 4.7 %shard_map.28 = bf16[1,2048,512]{2,1,0:T(8,128)(2,1)} custom-call(bf16[1,2048,512]{2,1,0:T(8,128)(2,1)} %rows_ref.1, bf16[512,512]{1,0:T(8,128)(2,1)} %maximum_select_fusion.7.prefix_ref), custom_call_target="tpu_custom_call" | custom-call | tf_op jit(solution)/shard_map/pallas_call | solution.py:84
  (65 shorter events, 45.3 us)
Async XLA Ops:
  0.0 7.2 %copy-start = (bf16[1,2048,512]{2,1,0:T(8,128)(2,1)S(1)}, bf16[1,2048,512]{2,1,0:T(8,128)(2,1)}, u32[]{:S(2)}) copy-start(bf16[1,2048,512]{2,1,0:T(8,128)(2,1)} %rows_ref.1) | copy-start | bytes 6291460
  3.2 16.0 %collective-permute-start = (bf16[256,512]{1,0:T(8,128)(2,1)S(1)}, bf16[256,512]{1,0:T(8,128)(2,1)S(1)}, u32[]{:S(2)}, u32[]{:S(2)}) collective-permute-start(bf16[256,512]{1,0:T(8,128)(2,1)S(1)} %fusion.13), channel_id=1, source_target_pairs={{0,16},{16,32},{32,48},{48,64},{64,80},{80,96},{96,112},{112,128},... | collective-permute-start | bytes 786440 | tf_op jit(solution)/shard_map/ppermute | solution.py:14
  7.9 11.3 %collective-permute-start.1 = (bf16[256,512]{1,0:T(8,128)(2,1)S(1)}, bf16[256,512]{1,0:T(8,128)(2,1)S(1)}, u32[]{:S(2)}, u32[]{:S(2)}) collective-permute-start(bf16[256,512]{1,0:T(8,128)(2,1)S(1)} %fusion.16), channel_id=1, source_target_pairs={{0,16},{16,32},{32,48},{48,64},{64,80},{80,96},{96,112},{112,128},... | collective-permute-start | bytes 786440 | tf_op jit(solution)/shard_map/ppermute | solution.py:14
  11.8 11.5 %collective-permute-start.2 = (bf16[256,512]{1,0:T(8,128)(2,1)S(1)}, bf16[256,512]{1,0:T(8,128)(2,1)}, u32[]{:S(2)}, u32[]{:S(2)}) collective-permute-start(bf16[256,512]{1,0:T(8,128)(2,1)S(1)} %fusion.19), channel_id=1, source_target_pairs={{0,16},{16,32},{32,48},{48,64},{64,80},{80,96},{96,112},{112,128},... | collective-permute-start | bytes 786440 | tf_op jit(solution)/shard_map/ppermute | solution.py:14
  16.8 12.3 %collective-permute-start.3 = (bf16[256,512]{1,0:T(8,128)(2,1)}, bf16[256,512]{1,0:T(8,128)(2,1)S(1)}, u32[]{:S(2)}, u32[]{:S(2)}) collective-permute-start(bf16[256,512]{1,0:T(8,128)(2,1)} %fusion.22), channel_id=1, source_target_pairs={{0,16},{16,32},{32,48},{48,64},{64,80},{80,96},{96,112},{112,128},... | collective-permute-start | bytes 786440 | tf_op jit(solution)/shard_map/ppermute | solution.py:14
  30.9 3.2 %collective-permute-start.4 = (f32[256,512]{1,0:T(8,128)S(1)}, f32[256,512]{1,0:T(8,128)S(1)}, u32[]{:S(2)}, u32[]{:S(2)}) collective-permute-start(f32[256,512]{1,0:T(8,128)S(1)} %slice_select_fusion.1), channel_id=1, source_target_pairs={{0,1},{1,0},{2,3},{3,2},{4,5},{5,4},{6,7},{7,6},{8,9},{9,8},{10,11... | collective-permute-start | bytes 1572872 | tf_op jit(solution)/shard_map/ppermute | solution.py:19
  76.6 4.9 %collective-permute-start.5 = (f32[256,512]{1,0:T(8,128)S(1)}, f32[256,512]{1,0:T(8,128)S(1)}, u32[]{:S(2)}, u32[]{:S(2)}) collective-permute-start(f32[256,512]{1,0:T(8,128)S(1)} %bitcast.50), channel_id=1, source_target_pairs={{0,1},{1,0},{2,3},{3,2},{4,5},{5,4},{6,7},{7,6},{8,9},{9,8},{10,11... | collective-permute-start | bytes 1572872 | tf_op jit(solution)/shard_map/ppermute | solution.py:19
  113.1 14.9 %collective-permute-start.6 = (f32[512,256]{1,0:T(8,128)S(1)}, f32[512,256]{1,0:T(8,128)S(1)}, u32[]{:S(2)}, u32[]{:S(2)}) collective-permute-start(f32[512,256]{1,0:T(8,128)S(1)} %slice_select_fusion), channel_id=1, source_target_pairs={{0,16},{16,32},{32,48},{48,64},{64,80},{80,96},{96,112},{112,128},... | collective-permute-start | bytes 1572872 | tf_op jit(solution)/shard_map/ppermute | solution.py:14
  129.0 7.2 %collective-permute-start.7 = (f32[512,256]{1,0:T(8,128)S(1)}, f32[512,256]{1,0:T(8,128)S(1)}, u32[]{:S(2)}, u32[]{:S(2)}) collective-permute-start(f32[512,256]{1,0:T(8,128)S(1)} %convolution_select_fusion.3), channel_id=1, source_target_pairs={{0,1},{1,0},{2,3},{3,2},{4,5},{5,4},{6,7},{7,6},{8,9},{9,8},{10,11... | collective-permute-start | bytes 1572872 | tf_op jit(solution)/shard_map/ppermute | solution.py:19
  130.5 16.9 %collective-permute-start.8 = (f32[512,256]{1,0:T(8,128)S(1)}, f32[512,256]{1,0:T(8,128)S(1)}, u32[]{:S(2)}, u32[]{:S(2)}) collective-permute-start(f32[512,256]{1,0:T(8,128)S(1)} %convolution_select_fusion.3), channel_id=1, source_target_pairs={{0,32},{16,48},{32,64},{48,80},{64,96},{80,112},{96,128},{112,144}... | collective-permute-start | bytes 1572872 | tf_op jit(solution)/shard_map/ppermute | solution.py:14
  148.4 19.7 %collective-permute-start.10 = (f32[512,256]{1,0:T(8,128)S(1)}, f32[512,256]{1,0:T(8,128)S(1)}, u32[]{:S(2)}, u32[]{:S(2)}) collective-permute-start(f32[512,256]{1,0:T(8,128)S(1)} %convolution_select_fusion.2), channel_id=1, source_target_pairs={{0,64},{16,80},{32,96},{48,112},{64,128},{80,144},{96,160},{112,17... | collective-permute-start | bytes 1572872 | tf_op jit(solution)/shard_map/ppermute | solution.py:14
  157.7 10.4 %collective-permute-start.9 = (f32[512,256]{1,0:T(8,128)S(1)}, f32[512,256]{1,0:T(8,128)S(1)}, u32[]{:S(2)}, u32[]{:S(2)}) collective-permute-start(f32[512,256]{1,0:T(8,128)S(1)} %convolution_select_fusion.2), channel_id=1, source_target_pairs={{0,1},{1,0},{2,3},{3,2},{4,5},{5,4},{6,7},{7,6},{8,9},{9,8},{10,11... | collective-permute-start | bytes 1572872 | tf_op jit(solution)/shard_map/ppermute | solution.py:19
  169.1 7.6 %collective-permute-start.11 = (f32[512,256]{1,0:T(8,128)S(1)}, f32[512,256]{1,0:T(8,128)S(1)}, u32[]{:S(2)}, u32[]{:S(2)}) collective-permute-start(f32[512,256]{1,0:T(8,128)S(1)} %convolution_select_fusion.1), channel_id=1, source_target_pairs={{0,1},{1,0},{2,3},{3,2},{4,5},{5,4},{6,7},{7,6},{8,9},{9,8},{10,11... | collective-permute-start | bytes 1572872 | tf_op jit(solution)/shard_map/ppermute | solution.py:19
  170.9 17.0 %collective-permute-start.12 = (f32[512,256]{1,0:T(8,128)S(1)}, f32[512,256]{1,0:T(8,128)S(1)}, u32[]{:S(2)}, u32[]{:S(2)}) collective-permute-start(f32[512,256]{1,0:T(8,128)S(1)} %convolution_select_fusion.1), channel_id=1, source_target_pairs={{0,128},{16,144},{32,160},{48,176},{64,192},{80,208},{96,224},{112... | collective-permute-start | bytes 1572872 | tf_op jit(solution)/shard_map/ppermute | solution.py:14
  188.9 2.1 %collective-permute-start.13 = (bf16[512,256]{1,0:T(8,128)(2,1)S(1)}, bf16[512,256]{1,0:T(8,128)(2,1)S(1)}, u32[]{:S(2)}, u32[]{:S(2)}) collective-permute-start(bf16[512,256]{1,0:T(8,128)(2,1)S(1)} %fusion.25), channel_id=1, source_target_pairs={{0,1},{1,0},{2,3},{3,2},{4,5},{5,4},{6,7},{7,6},{8,9},{9,8},{10,11... | collective-permute-start | bytes 786440 | tf_op jit(solution)/shard_map/ppermute | solution.py:19
